TPU v7x, 128 devices: a whole 4x4x4 slice. The times are simulated.
128 devices in a mesh: req: 4 (over y), exp: 32 (over x, z, core).
Axes of the slice: x: 4, y: 4, z: 4, core: 2. Of those that a mesh axis runs over, the one named last changes fastest.
Arguments:
- hidden_in: bfloat16 [16384, 1536], P(('req', 'exp')), may hold values from -6 to 6
- attn_gain: bfloat16 [1536], replicated, may hold values from 0.099609375 to 1.8984375
- w_query: bfloat16 [1536, 1536], replicated, may hold values from -0.625 to 0.625
- w_key: bfloat16 [1536, 512], replicated, may hold values from -0.625 to 0.625
- w_value: bfloat16 [1536, 512], replicated, may hold values from -0.15625 to 0.15625
- w_out: bfloat16 [1536, 1536], replicated, may hold values from -0.15625 to 0.15625
- cache_kv: bfloat16 [4, 1536, 1024], P('req', 'exp'), may hold values from -128 to 128
- cache_len: int32 [4], P('req'), may hold values from 48 to 1536, as said below
- moe_gain: bfloat16 [1536], replicated, may hold values from 0.099609375 to 1.8984375
- expert_ids: int32 [16384, 8], P(('req', 'exp')), may hold values from 0 to 39, all different within a row; in each aligned block of 128 rows (0 to 127, 128 to 255, ...) at most 26 rows name the same one
- expert_weights: bfloat16 [16384, 8], P(('req', 'exp')), may hold values from 0.019897461 to 0.5
- w_gate_up: bfloat16 [32, 5, 1536, 256], P('exp', None, 'req'), may hold values from -0.15625 to 0.15625
- w_down: bfloat16 [32, 5, 128, 1536], P('exp', None, None, 'req'), may hold values from -0.25 to 0.25
Outputs:
- attended: bfloat16 [16384, 1536], P(('req', 'exp'))
- layer_out: bfloat16 [16384, 1536], P(('req', 'exp'))
Inputs may be any that keep to these rules, and one draw needn't show every extreme that they name: `cache_len`: cached positions of each request; some request has exactly 1536, some exactly 48. `expert_ids`: each row names 8 different experts. Among the rows of one device no expert is named more than 26 times; in some devices' rows one expert is named exactly 26 times.
All inputs are finite; a program needn't handle non-finite values.
Results may differ from a plain program's by a relative error of at most 0.009.
Values may be sent and summed in bfloat16 or wider, within the bound.
No kernel may reach another device: no remote copies, remote signals or barrier semaphores. Data moves between devices by JAX's collectives and lax.ppermute only.
A program may use at most 256 MiB of HBM per device.

v0:
```python
import jax
import jax.numpy as jnp
from jax import lax
from jax.sharding import PartitionSpec as P

HEAD_DIM = 64
EXPERTS = 40
TOPK = 8
PIECES = 4
MOST = 26


rope_base = 10000.0
attn_scale = 0.015625
residual_scale = 1.0
norm_eps = 1e-06
neg_fill = -1e30
key_block = 512


def rms_scale(values, gain):
    widened = values.astype(jnp.float32)
    mean_sq = jnp.mean(widened * widened, axis=-1, keepdims=True)
    return (widened * lax.rsqrt(mean_sq + norm_eps) * gain.astype(jnp.float32)).astype(jnp.bfloat16)


def rotate(projected, positions, head_count, head_dim):
    row_count = projected.shape[0]
    shaped = projected.reshape(row_count, head_count, head_dim)
    half_dim = head_dim // 2
    inverse_freq = rope_base ** (-(jnp.arange(half_dim, dtype=jnp.float32) * 2.0 / head_dim))
    angles = positions.astype(jnp.float32)[:, None] * inverse_freq[None, :]
    cosine = jnp.cos(angles)[:, None, :]
    sinus = jnp.sin(angles)[:, None, :]
    lower_half = shaped[..., :half_dim]
    upper_half = shaped[..., half_dim:]
    turned = jnp.concatenate(
        [lower_half * cosine - upper_half * sinus, upper_half * cosine + lower_half * sinus],
        axis=-1,
    )
    return turned.reshape(row_count, head_count * head_dim).astype(jnp.bfloat16)


def attend_block(running, queries, block_rows, visible, kv_width):
    run_max, run_sum, run_acc = running
    kv_heads = run_max.shape[0]
    head_dim = run_acc.shape[-1]
    block_size = block_rows.shape[0]
    key_heads = block_rows[:, :kv_width].reshape(block_size, kv_heads, head_dim)
    value_heads = block_rows[:, kv_width:].reshape(block_size, kv_heads, head_dim)
    scores = (
        jnp.einsum("tkgd,rkd->kgtr", queries, key_heads, preferred_element_type=jnp.float32)
        * attn_scale
    )
    scores = jnp.where(visible[None, None], scores, neg_fill)
    new_max = jnp.maximum(run_max, jnp.max(scores, axis=-1))
    weights = jnp.where(visible[None, None], jnp.exp(scores - new_max[..., None]), 0.0)
    factor = jnp.exp(run_max - new_max)
    new_sum = run_sum * factor + jnp.sum(weights, axis=-1)
    new_acc = run_acc * factor[..., None] + jnp.einsum(
        "kgtr,rkd->kgtd",
        weights.astype(jnp.bfloat16),
        value_heads,
        preferred_element_type=jnp.float32,
    )
    return (new_max, new_sum, new_acc)


def shards(
    hidden_in,
    attn_gain,
    w_query,
    w_key,
    w_value,
    w_out,
    cache_kv,
    cache_len,
    moe_gain,
    expert_ids,
    expert_weights,
    w_gate_up,
    w_down,
):
    rows_here = hidden_in.shape[0]
    width = hidden_in.shape[1]
    kv_width = w_key.shape[1]
    kv_heads = kv_width // HEAD_DIM
    head_count = w_query.shape[1] // HEAD_DIM
    group_size = head_count // kv_heads
    position_exp = lax.axis_index("exp")
    length = cache_len[0]
    cache_rows = cache_kv[0]
    cache_count = cache_rows.shape[0]
    gate_up_full, down_full = (
        lax.all_gather(w_gate_up[0], "req", axis=1, tiled=True),
        lax.all_gather(w_down[0], "req", axis=2, tiled=True),
    )
    normed = rms_scale(hidden_in, attn_gain)
    query_pos = position_exp * rows_here + jnp.arange(rows_here, dtype=jnp.int32)
    positions = length + query_pos
    query = rotate(
        jnp.dot(normed, w_query, preferred_element_type=jnp.float32),
        positions,
        head_count,
        HEAD_DIM,
    )
    keys_new = rotate(
        jnp.dot(normed, w_key, preferred_element_type=jnp.float32), positions, kv_heads, HEAD_DIM
    )
    values_new = jnp.dot(normed, w_value, preferred_element_type=jnp.float32).astype(jnp.bfloat16)
    new_kv = jnp.concatenate([keys_new, values_new], axis=1)
    queries = query.reshape(rows_here, kv_heads, group_size, HEAD_DIM)
    initial = (
        jnp.full((kv_heads, group_size, rows_here), neg_fill, jnp.float32),
        jnp.zeros((kv_heads, group_size, rows_here), jnp.float32),
        jnp.zeros((kv_heads, group_size, rows_here, HEAD_DIM), jnp.float32),
    )
    shard_rows = cache_count + rows_here
    joined = jnp.concatenate([cache_rows, new_kv], axis=0)
    running = initial
    piece = lax.all_gather(joined, "exp", axis=0, tiled=True)
    first_row = jnp.int32(0)
    key_count = piece.shape[0]
    for offset in range(0, key_count, key_block):
        block_size = min(key_block, key_count - offset)
        key_index = first_row + offset + jnp.arange(block_size, dtype=jnp.int32)
        owner = key_index // shard_rows
        within = key_index - owner * shard_rows
        cached = within < cache_count
        cache_pos = owner * cache_count + within
        new_pos = owner * rows_here + within - cache_count
        running = attend_block(
            running,
            queries,
            piece[offset : offset + block_size],
            jnp.where(
                cached[None, :],
                (cache_pos < length)[None, :],
                new_pos[None, :] <= query_pos[:, None],
            ),
            kv_width,
        )
    run_max, run_sum, run_acc = running
    context = (
        (run_acc / run_sum[..., None])
        .transpose(2, 0, 1, 3)
        .reshape(rows_here, head_count * HEAD_DIM)
        .astype(jnp.bfloat16)
    )
    projected = jnp.dot(context, w_out, preferred_element_type=jnp.float32)
    attended = (hidden_in.astype(jnp.float32) + residual_scale * projected).astype(jnp.bfloat16)
    moe_in = rms_scale(attended, moe_gain)
    block_experts = gate_up_full.shape[0]
    slice_width = down_full.shape[1]
    flat_ids = expert_ids.reshape(-1)
    matches = (flat_ids[:, None] == jnp.arange(EXPERTS, dtype=jnp.int32)[None, :]).astype(jnp.int32)
    slot_rank = jnp.sum((jnp.cumsum(matches, axis=0) - matches) * matches, axis=1)
    slot_index = flat_ids * MOST + slot_rank
    token_of = jnp.arange(flat_ids.shape[0], dtype=jnp.int32) // TOPK
    sectioned = (
        jnp.zeros((EXPERTS * MOST, width), jnp.bfloat16).at[slot_index].set(moe_in[token_of])
    )
    blocks = EXPERTS // block_experts
    outgoing = jnp.broadcast_to(
        sectioned.reshape(blocks, 1, block_experts, MOST, width),
        (blocks, PIECES, block_experts, MOST, width),
    )
    outgoing = outgoing.reshape(blocks * PIECES, block_experts, MOST, width)
    gate_up = jnp.einsum(
        "sgmd,gdf->sgmf",
        lax.all_to_all(outgoing, "exp", split_axis=0, concat_axis=0, tiled=True),
        gate_up_full,
        preferred_element_type=jnp.float32,
    )
    activated = (jax.nn.silu(gate_up[..., :slice_width]) * gate_up[..., slice_width:]).astype(
        jnp.bfloat16
    )
    computed = jnp.einsum(
        "sgmf,gfd->sgmd", activated, down_full, preferred_element_type=jnp.float32
    ).astype(jnp.bfloat16)
    returned = lax.all_to_all(computed, "exp", split_axis=0, concat_axis=0, tiled=True)
    summed = jnp.sum(
        returned.reshape(blocks, PIECES, block_experts, MOST, width), axis=1, dtype=jnp.float32
    )
    summed = summed.reshape(EXPERTS * MOST, width)
    picked = summed[slot_index] * expert_weights.reshape(-1).astype(jnp.float32)[:, None]
    mixture = jnp.sum(picked.reshape(rows_here, TOPK, width), axis=1)
    layer_out = (attended.astype(jnp.float32) + residual_scale * mixture).astype(jnp.bfloat16)
    return (attended, layer_out)


def solution(mesh):
    in_specs = (
        P(("req", "exp"), None),
        P(),
        P(),
        P(),
        P(),
        P(),
        P("req", "exp", None),
        P("req"),
        P(),
        P(("req", "exp"), None),
        P(("req", "exp"), None),
        P("exp", None, "req", None),
        P("exp", None, None, "req"),
    )
    out_specs = (P(("req", "exp"), None), P(("req", "exp"), None))
    return jax.shard_map(shards, mesh=mesh, in_specs=in_specs, out_specs=out_specs, check_vma=False)
```

profile of v0, /device:TPU:36, one launch (start us, length us, event | category | flops | bytes accessed | tf_op | source)
XLA Modules:
  0.0 855.1 jit_solution(6877591872759413824)
XLA Ops:
  10.9 1.8 fusion.267
  12.9 2.0 convolution_convert_fusion
  17.5 11.3 %reduce-window.6 = s32[40,8,128]{2,1,0:T(8,128)S(1)} reduce-window(s32[40,8,128]{2,1,0:T(8,128)S(1)} %fusion.190, s32[]{:T(128)} %constant.109.clone.1), window={size=1x1x128 pad=0_0x0_0x127_0}, to_apply=%region_23.24 | reduce-window | flops 5201920 | bytes 327684 | tf_op jit(solution)/shard_map/reduce-window
  29.6 4.3 fusion.264
  35.5 2.2 compare_select_fusion.2
  37.7 2.4 compare_select_fusion.8
  40.1 37.3 %all-gather.6.cloned.1.call-done = bf16[5632,1024]{1,0:T(8,128)(2,1)} async-done(((bf16[176,1024]{1,0:T(8,128)(2,1)}), bf16[5632,1024]{1,0:T(8,128)(2,1)}) %all-gather.6.cloned.1.call-update) | async-done | bytes 11534352 | tf_op jit(solution)/shard_map/all_gather | solution.py:121
  77.4 7.1 fusion.272
  84.6 2.1 copy.111
  86.6 2.1 copy.105
  88.7 2.0 copy.117
  90.7 2.0 copy.114
  95.5 2.5 fusion.273
  99.4 2.1 copy.97
  101.5 2.1 copy.100
  103.5 2.0 copy.103
  105.6 2.0 copy.106
  107.6 2.1 copy.109
  109.7 2.0 copy.112
  111.7 2.1 copy.115
  113.8 2.1 copy.118
  115.8 2.1 copy.121
  117.9 2.0 copy.124
  120.0 2.1 copy.127
  122.0 2.2 fusion.8
  124.3 3.7 fusion.6
  130.2 3.7 fusion.7
  133.9 3.7 fusion.5
  140.0 3.6 fusion.11
  143.7 3.7 fusion.4
  147.4 3.8 fusion.3
  151.3 4.3 fusion.14
  155.5 4.3 fusion.16
  159.8 4.3 fusion.18
  164.1 4.3 fusion.20
  168.4 4.7 fusion.22
  177.6 4.3 fusion.30
  184.8 4.5 fusion.169
  189.5 4.7 fusion.163
  194.2 4.6 fusion.157
  199.0 1.7 fusion.151
  200.7 4.5 fusion.145
  205.3 1.7 fusion.139
  207.0 1.7 fusion.133
  208.8 1.7 fusion.127
  211.8 1.7 fusion.121
  213.6 1.9 fusion.115
  215.5 1.7 fusion.177
  218.4 18.6 %scatter_custom_fusion = bf16[1040,1536]{1,0:T(8,128)(2,1)} fusion(s32[1024]{0:T(1024)S(1)} %bitcast.678, bf16[128,1536]{1,0:T(8,128)(2,1)S(1)} %fusion.185, s32[1024]{0:T(1024)} %broadcast_clamp_fusion.1, bf16[]{:T(256)} %constant.132.clone.1), kind=kCustom, calls=%fused_computation.66 | custom fusion | bytes 3195392 | tf_op jit(solution)/shard_map/scatter | solution.py:161
  237.0 5.5 broadcast_in_dim.398
  242.5 7.1 broadcast_in_dim.399
  249.5 7.2 all-to-all-start
  257.9 48.1 %all-gather.8.cloned.1.call-done = bf16[1,5,1536,256]{3,2,1,0:T(8,128)(2,1)} async-done(((bf16[1,5,384,256]{3,2,1,0:T(8,128)(2,1)}), bf16[1,5,1536,256]{3,2,1,0:T(8,128)(2,1)}) %all-gather.8.cloned.1.call-update) | async-done | bytes 3932176 | tf_op jit(solution)/shard_map/all_gather | solution.py:95
  306.0 201.9 %all-to-all-done = bf16[32,5,26,1536]{3,2,1,0:T(8,128)(2,1)} async-done(((bf16[32,5,26,1536]{3,2,1,0:T(8,128)(2,1)}), bf16[32,5,26,1536]{3,2,1,0:T(8,128)(2,1)}, u32[]{:S(2)}, u32[]{:S(2)}) %all-to-all-start) | async-done | bytes 12779552 | tf_op jit(solution)/shard_map/all_to_all | solution.py:171
  507.9 13.1 %fusion = f32[5,32,26,256]{3,2,1,0:T(8,128)} fusion(bf16[32,5,26,1536]{3,2,1,0:T(8,128)(2,1)} %all-to-all-done, bf16[1,5,1536,256]{3,2,1,0:T(8,128)(2,1)} %all-gather.8.cloned.1.call-done), kind=kOutput, calls=%fused_computation.4 | convolution fusion | flops 3271557120 | bytes 20971520 | tf_op jit(solution)/shard_map/sgmd,gdf->sgmf/dot_general | solution.py:169
  521.0 6.9 copy.185
  527.9 10.9 %convert_bitcast_fusion = bf16[32,5,26,1536]{3,0,2,1:T(8,128)(2,1)} fusion(bf16[1,5,128,1536]{3,2,1,0:T(8,128)(2,1)} %all-gather.10.cloned.1.call-done, f32[32,5,26,256]{3,0,2,1:T(8,128)} %bitcast.646), kind=kOutput, calls=%fused_computation.6 | convolution fusion | flops 1645363200 | bytes 19005440 | tf_op jit(solution)/shard_map/sgmf,gfd->sgmd/dot_general | solution.py:178
  538.8 14.6 %copy.135 = bf16[32,5,26,1536]{3,2,1,0:T(8,128)(2,1)} copy(bf16[32,5,26,1536]{3,0,2,1:T(8,128)(2,1)} %convert_bitcast_fusion) | data formatting | bytes 25559040 | tf_op jit(solution)/shard_map/convert_element_type | solution.py:180
  553.5 6.4 all-to-all-start.1
  560.0 250.8 %all-to-all-done.1 = bf16[32,5,26,1536]{3,2,1,0:T(8,128)(2,1)} async-done(((bf16[32,5,26,1536]{3,2,1,0:T(8,128)(2,1)}), bf16[32,5,26,1536]{3,2,1,0:T(8,128)(2,1)}, u32[]{:S(2)}, u32[]{:S(2)}) %all-to-all-start.1) | async-done | bytes 12779552 | tf_op jit(solution)/shard_map/all_to_all | solution.py:181
  810.8 12.2 %convert_reduce_fusion = f32[8,5,26,1536]{3,2,1,0:T(8,128)} fusion(bf16[32,5,26,1536]{3,2,1,0:T(8,128)(2,1)} %all-to-all-done.1), kind=kLoop, calls=%fused_computation.3 | loop fusion | flops 11182080 | bytes 19169280 | tf_op jit(solution)/shard_map/reduce_sum | solution.py:182
  823.0 7.8 reshape.1557
  830.8 10.7 %gather_fusion = f32[1024,1536]{1,0:T(8,128)} fusion(f32[1040,1536]{1,0:T(8,128)} %reshape.1557, s32[1024]{0:T(1024)S(1)} %broadcast_clamp_fusion), kind=kCustom, calls=%fused_computation.1 | custom fusion | bytes 12587008 | tf_op jit(solution)/shard_map/gather | solution.py:186
  841.5 5.1 fusion.2
  (162 shorter events, 28.1 us)
Async XLA Ops:
  8.0 2.9 copy-start
  8.0 21.6 %copy-start.2 = (bf16[128,1536]{1,0:T(8,128)(2,1)S(1)}, bf16[128,1536]{1,0:T(8,128)(2,1)}, u32[]{:S(2)}) copy-start(bf16[128,1536]{1,0:T(8,128)(2,1)} %param.13) | copy-start | bytes 1179652
  8.0 8.5 copy-start.30
  8.0 8.8 %copy-start.32 = (bf16[1536]{0:T(1024)(128)(2,1)S(1)}, bf16[1536]{0:T(1024)(128)(2,1)}, u32[]{:S(2)}) copy-start(bf16[1536]{0:T(1024)(128)(2,1)} %param.21) | copy-start | bytes 9220
  8.0 69.4 %all-gather.6.cloned.1.call-start = ((), (), s32[]{:S(2)}) async-start(), calls=%async_computation.2 | async-start | bytes 11894784 | tf_op jit(solution)/shard_map/all_gather | solution.py:121
  122.0 2.2 copy-start.8
  122.0 2.2 copy-start.11
  122.0 6.0 copy-start.7
  124.3 4.8 copy-start.6
  128.0 2.2 copy-start.5
  128.0 2.2 copy-start.10
  129.1 4.8 copy-start.4
  129.1 4.8 copy-start.12
  130.2 7.4 copy-start.13
  133.9 5.0 copy-start.14
  137.6 2.4 copy-start.15
  138.9 4.8 copy-start.16
  140.0 7.4 copy-start.17
  164.1 9.0 %copy-start.9 = (pred[128,512]{0,1:T(8,128)(4,1)S(1)}, pred[128,512]{0,1:T(8,128)(4,1)}, u32[]{:S(2)}) copy-start(pred[128,512]{0,1:T(8,128)(4,1)} %get-tuple-element.59) | copy-start | bytes 196612
  181.9 3.0 copy-start.28
  184.8 4.6 copy-start.27
  189.3 4.8 copy-start.26
  194.1 4.6 slice-start.2
  194.1 4.6 copy-start.25
  194.2 4.8 slice-start.3
  198.8 2.0 copy-start.24
  200.7 4.5 copy-start.23
  205.3 1.8 copy-start.22
  207.0 1.8 copy-start.21
  208.8 2.2 slice-start
  208.8 2.3 copy-start.20
  208.8 3.0 slice-start.1
  210.5 3.0 copy-start.19
  213.5 2.0 copy-start.18
  213.5 3.7 slice-start.4
  215.5 1.8 slice-start.5
  215.5 2.7 copy-start.29
  217.3 1.2 copy-start.31
  218.2 628.4 %copy-start.3 = (bf16[128,1536]{1,0:T(8,128)(2,1)}, bf16[128,1536]{1,0:T(8,128)(2,1)S(1)}, u32[]{:S(2)}) copy-start(bf16[128,1536]{1,0:T(8,128)(2,1)S(1)} %get-tuple-element.90) | copy-start | bytes 1179652
  249.5 258.4 %all-to-all-start = ((bf16[32,5,26,1536]{3,2,1,0:T(8,128)(2,1)}), bf16[32,5,26,1536]{3,2,1,0:T(8,128)(2,1)}, u32[]{:S(2)}, u32[]{:S(2)}) async-start(bf16[32,5,26,1536]{3,2,1,0:T(8,128)(2,1)} %bitcast.630), calls=%async_computation | async-start | bytes 31457280 | tf_op jit(solution)/shard_map/all_to_all | solution.py:171
  256.8 49.3 %all-gather.8.cloned.1.call-start = ((), (), s32[]{:S(2)}) async-start(), calls=%async_computation.3 | async-start | bytes 4915200 | tf_op jit(solution)/shard_map/all_gather | solution.py:95
  257.3 270.6 %all-gather.10.cloned.1.call-start = ((), (), s32[]{:S(2)}) async-start(), calls=%async_computation.4 | async-start | bytes 2457600 | tf_op jit(solution)/shard_map/all_gather | solution.py:96
  553.5 6.4 copy-start.33
  553.5 257.4 %all-to-all-start.1 = ((bf16[32,5,26,1536]{3,2,1,0:T(8,128)(2,1)}), bf16[32,5,26,1536]{3,2,1,0:T(8,128)(2,1)}, u32[]{:S(2)}, u32[]{:S(2)}) async-start(bf16[32,5,26,1536]{3,2,1,0:T(8,128)(2,1)} %copy.135), calls=%async_computation.1 | async-start | bytes 31457280 | tf_op jit(solution)/shard_map/all_to_all | solution.py:181
  830.8 16.6 %copy-start.1 = (bf16[1536,512]{1,0:T(8,128)(2,1)S(1)}, bf16[1536,512]{1,0:T(8,128)(2,1)}, u32[]{:S(2)}) copy-start(bf16[1536,512]{1,0:T(8,128)(2,1)} %param.16) | copy-start | bytes 4718596
Sparse Core Ops, SparseCore 0:
  16.7 60.7 all-gather.5
Sparse Core Ops, SparseCore 1:
  258.9 47.1 all-gather.7
  307.6 29.8 all-gather.9
where the time goes:
time: 862 us; the launch traced here: 855 us
  waiting for transfers between devices  539 us (63%)
  local copies, waits for them, and re-layouts  118 us (14%)
  matrix products  92.5 us (11%)
  other arithmetic  74 us (9%)
  between operations  17.3 us (2%)
  starting transfers between devices  13.7 us (2%)
    all_to_all x1, waiting for transfers between devices, shards(): lax.all_to_all(computed, 'exp', split_axis=0, concat_axis=0, tiled=True)  251 us
    all_to_all x1, waiting for transfers between devices, shards(): lax.all_to_all(outgoing, 'exp', split_axis=0, concat_axis=0, tiled=True)  202 us
    all_gather x1, waiting for transfers between devices, shards(): lax.all_gather(w_gate_up[0], 'req', axis=1, tiled=True)  48.1 us
    all_gather x1, waiting for transfers between devices, shards(): piece = lax.all_gather(joined, 'exp', axis=0, tiled=True)  37.3 us
    reduce_sum x11, other arithmetic, attend_block(): new_sum = run_sum * factor + jnp.sum(weights, axis=-1)  33.5 us
    dot_general x11, matrix products, attend_block(): jnp.einsum('kgtr,rkd->kgtd', weights.astype(jnp.bfloat16), value_heads, p...  30.6 us
    slice x12, local copies, waits for them, and re-layouts, attend_block(): block_rows[:, kv_width:].reshape(block_size, kv_heads, head_dim)  29.8 us
    dot_general x11, matrix products, attend_block(): jnp.einsum('tkgd,rkd->kgtr', queries, key_heads, preferred_element_type=j...  29 us
  transfers between devices with their start and end apart: 5, of which 4 were waited for; matrix products, arithmetic and copies ran while one was open for 5% of the time, Pallas kernels for 0%

commit v1 on v0

--- a/solution.py
+++ b/solution.py
@@ -1,7 +1,7 @@
 import jax
 import jax.numpy as jnp
 from jax import lax
-from jax.sharding import PartitionSpec as P
+from jax.sharding import Mesh, PartitionSpec as P
 
 HEAD_DIM = 64
 EXPERTS = 40
@@ -87,13 +87,13 @@
     kv_heads = kv_width // HEAD_DIM
     head_count = w_query.shape[1] // HEAD_DIM
     group_size = head_count // kv_heads
-    position_exp = lax.axis_index("exp")
+    position_exp = lax.axis_index("xz") * lax.axis_size("core") + lax.axis_index("core")
     length = cache_len[0]
     cache_rows = cache_kv[0]
     cache_count = cache_rows.shape[0]
     gate_up_full, down_full = (
-        lax.all_gather(w_gate_up[0], "req", axis=1, tiled=True),
-        lax.all_gather(w_down[0], "req", axis=2, tiled=True),
+        lax.all_gather(lax.all_gather(w_gate_up[0], "req", axis=1, tiled=True), "core", axis=0),
+        lax.all_gather(lax.all_gather(w_down[0], "req", axis=2, tiled=True), "core", axis=0),
     )
     normed = rms_scale(hidden_in, attn_gain)
     query_pos = position_exp * rows_here + jnp.arange(rows_here, dtype=jnp.int32)
@@ -118,7 +118,7 @@
     shard_rows = cache_count + rows_here
     joined = jnp.concatenate([cache_rows, new_kv], axis=0)
     running = initial
-    piece = lax.all_gather(joined, "exp", axis=0, tiled=True)
+    piece = lax.all_gather(joined, ("xz", "core"), axis=0, tiled=True)
     first_row = jnp.int32(0)
     key_count = piece.shape[0]
     for offset in range(0, key_count, key_block):
@@ -150,8 +150,9 @@
     projected = jnp.dot(context, w_out, preferred_element_type=jnp.float32)
     attended = (hidden_in.astype(jnp.float32) + residual_scale * projected).astype(jnp.bfloat16)
     moe_in = rms_scale(attended, moe_gain)
-    block_experts = gate_up_full.shape[0]
-    slice_width = down_full.shape[1]
+    block_experts = gate_up_full.shape[1]
+    slice_width = down_full.shape[2]
+    pairs = lax.axis_size("xz") // (EXPERTS // block_experts)
     flat_ids = expert_ids.reshape(-1)
     matches = (flat_ids[:, None] == jnp.arange(EXPERTS, dtype=jnp.int32)[None, :]).astype(jnp.int32)
     slot_rank = jnp.sum((jnp.cumsum(matches, axis=0) - matches) * matches, axis=1)
@@ -163,12 +164,12 @@
     blocks = EXPERTS // block_experts
     outgoing = jnp.broadcast_to(
         sectioned.reshape(blocks, 1, block_experts, MOST, width),
-        (blocks, PIECES, block_experts, MOST, width),
-    )
-    outgoing = outgoing.reshape(blocks * PIECES, block_experts, MOST, width)
+        (blocks, pairs, block_experts, MOST, width),
+    )
+    outgoing = outgoing.reshape(blocks * pairs, block_experts, MOST, width)
     gate_up = jnp.einsum(
-        "sgmd,gdf->sgmf",
-        lax.all_to_all(outgoing, "exp", split_axis=0, concat_axis=0, tiled=True),
+        "skmd,ckdf->sckmf",
+        lax.all_to_all(outgoing, "xz", split_axis=0, concat_axis=0, tiled=True),
         gate_up_full,
         preferred_element_type=jnp.float32,
     )
@@ -176,11 +177,12 @@
         jnp.bfloat16
     )
     computed = jnp.einsum(
-        "sgmf,gfd->sgmd", activated, down_full, preferred_element_type=jnp.float32
+        "sckmf,ckfd->sckmd", activated, down_full, preferred_element_type=jnp.float32
     ).astype(jnp.bfloat16)
-    returned = lax.all_to_all(computed, "exp", split_axis=0, concat_axis=0, tiled=True)
+    computed = jnp.sum(computed, axis=1, dtype=jnp.float32).astype(jnp.bfloat16)
+    returned = lax.all_to_all(computed, "xz", split_axis=0, concat_axis=0, tiled=True)
     summed = jnp.sum(
-        returned.reshape(blocks, PIECES, block_experts, MOST, width), axis=1, dtype=jnp.float32
+        returned.reshape(blocks, pairs, block_experts, MOST, width), axis=1, dtype=jnp.float32
     )
     summed = summed.reshape(EXPERTS * MOST, width)
     picked = summed[slot_index] * expert_weights.reshape(-1).astype(jnp.float32)[:, None]
@@ -190,20 +192,24 @@
 
 
 def solution(mesh):
+    req_size, exp_size = mesh.shape["req"], mesh.shape["exp"]
+    mesh = Mesh(mesh.devices.reshape(req_size, exp_size // 2, 2), ("req", "xz", "core"))
+    rows = ("req", "xz", "core")
+    cols = ("xz", "core")
     in_specs = (
-        P(("req", "exp"), None),
-        P(),
-        P(),
-        P(),
-        P(),
-        P(),
-        P("req", "exp", None),
+        P(rows, None),
+        P(),
+        P(),
+        P(),
+        P(),
+        P(),
+        P("req", cols, None),
         P("req"),
         P(),
-        P(("req", "exp"), None),
-        P(("req", "exp"), None),
-        P("exp", None, "req", None),
-        P("exp", None, None, "req"),
-    )
-    out_specs = (P(("req", "exp"), None), P(("req", "exp"), None))
+        P(rows, None),
+        P(rows, None),
+        P(cols, None, "req", None),
+        P(cols, None, None, "req"),
+    )
+    out_specs = (P(rows, None), P(rows, None))
     return jax.shard_map(shards, mesh=mesh, in_specs=in_specs, out_specs=out_specs, check_vma=False)

time: 862 us -> 655 us (0.76)
  the two profiles are of different devices: /device:TPU:36 before, /device:TPU:0 now
where the time goes in v1:
time: 655 us; the launch traced here: 644 us
  waiting for transfers between devices  345 us (53%)
  local copies, waits for them, and re-layouts  108 us (16%)
  matrix products  87.5 us (13%)
  other arithmetic  70.4 us (11%)
  starting transfers between devices  16.9 us (3%)
  between operations  15.8 us (2%)
    all_to_all x1, waiting for transfers between devices, shards(): lax.all_to_all(outgoing, 'xz', split_axis=0, concat_axis=0, tiled=True)  138 us
    all_to_all x1, waiting for transfers between devices, shards(): lax.all_to_all(computed, 'xz', split_axis=0, concat_axis=0, tiled=True)  124 us
    all_gather x1, waiting for transfers between devices, shards(): piece = lax.all_gather(joined, ('xz', 'core'), axis=0, tiled=True)  63.4 us
    reduce_sum x11, other arithmetic, attend_block(): new_sum = run_sum * factor + jnp.sum(weights, axis=-1)  33.7 us
    dot_general x11, matrix products, attend_block(): jnp.einsum('tkgd,rkd->kgtr', queries, key_heads, preferred_element_type=j...  30.5 us
    slice x12, local copies, waits for them, and re-layouts, attend_block(): key_heads = block_rows[:, :kv_width].reshape(block_size, kv_heads, head_dim)  25.3 us
    dot_general x11, matrix products, attend_block(): jnp.einsum('kgtr,rkd->kgtd', weights.astype(jnp.bfloat16), value_heads, p...  23.5 us
    slice x12, local copies, waits for them, and re-layouts, attend_block(): block_rows[:, kv_width:].reshape(block_size, kv_heads, head_dim)  21.6 us
  transfers between devices with their start and end apart: 7, of which 4 were waited for; matrix products, arithmetic and copies ran while one was open for 32% of the time, Pallas kernels for 0%

profile of v1, /device:TPU:0, one launch (start us, length us, event | category | flops | bytes accessed | tf_op | source)
XLA Modules:
  0.0 644.1 jit_solution(1080598783245781933)
XLA Ops:
  10.7 1.8 fusion.270
  12.6 2.0 convolution_convert_fusion
  17.3 11.2 %reduce-window.6 = s32[40,8,128]{2,1,0:T(8,128)S(1)} reduce-window(s32[40,8,128]{2,1,0:T(8,128)S(1)} %fusion.194, s32[]{:T(128)} %constant.114.clone.1), window={size=1x1x128 pad=0_0x0_0x127_0}, to_apply=%region_23.24 | reduce-window | flops 5201920 | bytes 327684 | tf_op jit(solution)/shard_map/reduce-window
  29.3 4.4 fusion.267
  35.2 2.2 compare_select_fusion.2
  37.4 2.4 compare_select_fusion.8
  39.8 18.5 %all-gather.12.cloned.1.call-done = bf16[1,5,1536,256]{3,2,0,1:T(8,128)(2,1)} async-done(((bf16[1,5,384,256]{3,2,0,1:T(8,128)(2,1)}), bf16[1,5,1536,256]{3,2,0,1:T(8,128)(2,1)}) %all-gather.12.cloned.1.call-update) | async-done | bytes 3932176 | tf_op jit(solution)/shard_map/all_gather | solution.py:95
  58.3 63.4 %all-gather.10.cloned.1.call-done = bf16[5632,1024]{1,0:T(8,128)(2,1)} async-done(((bf16[176,1024]{1,0:T(8,128)(2,1)}), bf16[5632,1024]{1,0:T(8,128)(2,1)}) %all-gather.10.cloned.1.call-update) | async-done | bytes 11534352 | tf_op jit(solution)/shard_map/all_gather | solution.py:121
  121.7 7.1 %fusion.275 = (bf16[512,512]{1,0:T(8,128)(2,1)S(1)}, bf16[512,512]{1,0:T(8,128)(2,1)}, bf16[512,512]{1,0:T(8,128)(2,1)S(1)}, bf16[512,512]{1,0:T(8,128)(2,1)}, b...) fusion(bf16[5632,1024]{1,0:T(8,128)(2,1)} %all-gather.10.cloned, ...), kind=kLoop, calls=%fused_computation.370 | loop fusion | bytes 19922944 | tf_op jit(solution)/shard_map/slice | solution.py:50
  128.8 2.1 copy.160
  130.8 2.1 copy.154
  132.9 2.1 copy.166
  135.0 2.0 copy.163
  137.0 2.1 copy.157
  139.1 2.1 copy.151
  141.2 2.1 copy.175
  143.3 2.0 copy.172
  145.3 2.0 copy.169
  147.3 2.6 fusion.276
  149.9 2.1 copy.148
  152.0 2.1 copy.144
  154.0 2.0 copy.146
  156.1 2.0 copy.149
  158.1 2.1 copy.152
  160.2 2.1 copy.155
  162.3 2.2 copy.158
  164.5 2.1 copy.161
  166.6 2.3 fusion.9
  169.0 4.2 fusion.7
  175.4 4.1 fusion.8
  179.6 3.8 fusion.6
  185.9 4.2 fusion.12
  190.1 3.7 fusion.5
  193.8 3.7 fusion.4
  197.7 4.3 fusion.15
  202.0 4.3 fusion.17
  206.2 4.3 fusion.19
  210.5 4.3 fusion.21
  214.8 4.3 fusion.23
  219.0 1.9 fusion.25
  224.0 4.4 fusion.31
  234.1 1.7 fusion.169
  236.5 1.9 fusion.163
  238.9 1.7 fusion.157
  243.2 2.6 fusion.145
  247.8 4.9 fusion.139
  252.8 1.7 fusion.133
  255.5 1.7 fusion.127
  257.5 1.9 fusion.121
  260.2 1.8 fusion.181
  263.5 18.6 %scatter_custom_fusion = bf16[1040,1536]{1,0:T(8,128)(2,1)} fusion(s32[1024]{0:T(1024)S(1)} %bitcast.696, bf16[128,1536]{1,0:T(8,128)(2,1)S(1)} %fusion.189, s32[1024]{0:T(1024)} %broadcast_clamp_fusion.1, bf16[]{:T(256)} %constant.139.clone.1), kind=kCustom, calls=%fused_computation.66 | custom fusion | bytes 3195392 | tf_op jit(solution)/shard_map/scatter | solution.py:162
  282.1 5.5 broadcast_in_dim.398
  287.5 6.3 broadcast_in_dim.399
  293.8 5.2 all-to-all-start
  299.6 137.7 %all-to-all-done = bf16[16,5,26,1536]{3,2,1,0:T(8,128)(2,1)} async-done(((bf16[16,5,26,1536]{3,2,1,0:T(8,128)(2,1)}), bf16[16,5,26,1536]{3,2,1,0:T(8,128)(2,1)}, u32[]{:S(2)}, u32[]{:S(2)}) %all-to-all-start) | async-done | bytes 6389792 | tf_op jit(solution)/shard_map/all_to_all | solution.py:172
  437.3 12.0 %fusion.74 = f32[16,2,5,26,256]{4,3,1,0,2:T(8,128)} fusion(bf16[2,5,1536,256]{3,2,0,1:T(8,128)(2,1)} %all-gather.14.cloned.1.call-done, bf16[16,5,26,1536]{3,2,1,0:T(8,128)(2,1)} %all-to-all-done), kind=kOutput, calls=%fused_computation.93 | convolution fusion | flops 3271557120 | bytes 18513920 | tf_op jit(solution)/shard_map/skmd,ckdf->sckmf/dot_general | solution.py:170
  449.3 12.3 %convert_reduce_fusion.1 = bf16[5,16,26,1536]{3,2,1,0:T(8,128)(2,1)} fusion(bf16[2,5,128,1536]{3,2,1,0:T(8,128)(2,1)} %all-gather.18.cloned.1.call-done, f32[16,2,5,26,256]{4,3,1,0,2:T(8,128)} %fusion.74), kind=kOutput, calls=%fused_computation.4 | convolution fusion | flops 1648558080 | bytes 14581760 | tf_op jit(solution)/shard_map/sckmf,ckfd->sckmd/dot_general | solution.py:179
  461.7 7.3 %copy.186 = bf16[16,5,26,1536]{3,2,1,0:T(8,128)(2,1)} copy(bf16[16,5,26,1536]{3,2,0,1:T(8,128)(2,1)} %bitcast.663) | data formatting | bytes 12779520 | tf_op jit(solution)/shard_map/reduce_sum | solution.py:182
  468.9 11.5 %all-to-all-start.1 = ((bf16[16,5,26,1536]{3,2,1,0:T(8,128)(2,1)}), bf16[16,5,26,1536]{3,2,1,0:T(8,128)(2,1)}, u32[]{:S(2)}, u32[]{:S(2)}) async-start(bf16[16,5,26,1536]{3,2,1,0:T(8,128)(2,1)} %copy.186), calls=%async_computation.1 | async-start | bytes 15728640 | tf_op jit(solution)/shard_map/all_to_all | solution.py:183
  480.5 123.6 %all-to-all-done.1 = bf16[16,5,26,1536]{3,2,1,0:T(8,128)(2,1)} async-done(((bf16[16,5,26,1536]{3,2,1,0:T(8,128)(2,1)}), bf16[16,5,26,1536]{3,2,1,0:T(8,128)(2,1)}, u32[]{:S(2)}, u32[]{:S(2)}) %all-to-all-start.1) | async-done | bytes 6389792 | tf_op jit(solution)/shard_map/all_to_all | solution.py:183
  604.2 8.8 %convert_reduce_fusion = f32[8,5,26,1536]{3,2,1,0:T(8,128)} fusion(bf16[16,5,26,1536]{3,2,1,0:T(8,128)(2,1)} %all-to-all-done.1), kind=kLoop, calls=%fused_computation.3 | loop fusion | flops 4792320 | bytes 12779520 | tf_op jit(solution)/shard_map/reduce_sum | solution.py:184
  613.0 7.8 %reshape.1557 = f32[1040,1536]{1,0:T(8,128)} reshape(f32[8,5,26,1536]{3,2,1,0:T(8,128)} %convert_reduce_fusion) | data formatting | bytes 12779520 | tf_op jit(solution)/shard_map/reshape | solution.py:187
  620.8 10.7 %gather_fusion = f32[1024,1536]{1,0:T(8,128)} fusion(f32[1040,1536]{1,0:T(8,128)} %reshape.1557, s32[1024]{0:T(1024)S(1)} %broadcast_clamp_fusion), kind=kCustom, calls=%fused_computation.1 | custom fusion | bytes 12587008 | tf_op jit(solution)/shard_map/gather | solution.py:188
  631.5 5.1 fusion.3
  (250 shorter events, 31.5 us)
Async XLA Ops:
  7.2 3.5 copy-start
  7.2 22.1 %copy-start.6 = (bf16[128,1536]{1,0:T(8,128)(2,1)S(1)}, bf16[128,1536]{1,0:T(8,128)(2,1)}, u32[]{:S(2)}) copy-start(bf16[128,1536]{1,0:T(8,128)(2,1)} %param.13) | copy-start | bytes 1179652
  7.2 7.4 %copy-start.46 = (bf16[1,48,1024]{2,1,0:T(8,128)(2,1)S(1)}, bf16[1,48,1024]{2,1,0:T(8,128)(2,1)}, u32[]{:S(2)}) copy-start(bf16[1,48,1024]{2,1,0:T(8,128)(2,1)} %param.19) | copy-start | bytes 294916
  7.2 9.1 %copy-start.54 = (s32[128,8]{0,1:T(8,128)S(1)}, s32[128,8]{0,1:T(8,128)}, u32[]{:S(2)}) copy-start(s32[128,8]{0,1:T(8,128)} %param.22) | copy-start | bytes 12292
  7.2 9.5 %copy-start.56 = (bf16[1536]{0:T(1024)(128)(2,1)S(1)}, bf16[1536]{0:T(1024)(128)(2,1)}, u32[]{:S(2)}) copy-start(bf16[1536]{0:T(1024)(128)(2,1)} %param.21) | copy-start | bytes 9220
  7.2 51.1 %all-gather.12.cloned.1.call-start = ((), (), s32[]{:S(2)}) async-start(), calls=%async_computation.3 | async-start | bytes 4915200 | tf_op jit(solution)/shard_map/all_gather | solution.py:95
  8.0 113.7 %all-gather.10.cloned.1.call-start = ((), (), s32[]{:S(2)}) async-start(), calls=%async_computation.2 | async-start | bytes 11894784 | tf_op jit(solution)/shard_map/all_gather | solution.py:121
  15.4 283.6 %all-gather.16.cloned.1.call-start = ((), (), s32[]{:S(2)}) async-start(), calls=%async_computation.5 | async-start | bytes 2457600 | tf_op jit(solution)/shard_map/all_gather | solution.py:96
  16.2 283.4 %all-gather.14.cloned.1.call-start = ((), (), s32[]{:S(2)}) async-start(), calls=%async_computation.4 | async-start | bytes 11796480 | tf_op jit(solution)/shard_map/all_gather | solution.py:95
  166.6 6.5 %copy-start.16 = (bf16[512,512]{0,1:T(8,128)(2,1)S(1)}, bf16[512,512]{0,1:T(8,128)(2,1)}, u32[]{:S(2)}) copy-start(bf16[512,512]{0,1:T(8,128)(2,1)} %copy.166) | copy-start | bytes 1572868
  169.0 5.3 copy-start.15
  174.2 23.3 %copy-start.38 = (f32[8,3,128]{2,1,0:T(4,128)}, f32[8,3,128]{2,1,0:T(4,128)S(1)}, u32[]{:S(2)}) copy-start(f32[8,3,128]{2,1,0:T(4,128)S(1)} %get-tuple-element.73) | copy-start | bytes 36868
  174.2 48.2 %copy-start.3 = (f32[8,512,128,3]{2,1,3,0:T(8,128)}, f32[8,512,128,3]{2,1,3,0:T(8,128)S(1)}, u32[]{:S(2)}) copy-start(f32[8,512,128,3]{2,1,3,0:T(8,128)S(1)} %get-tuple-element.74) | copy-start | bytes 18874372
  174.3 5.3 copy-start.13
  174.3 5.3 copy-start.21
  175.4 45.6 %copy-start.5 = (f32[8,512,128,3]{2,1,3,0:T(8,128)}, f32[8,512,128,3]{2,1,3,0:T(8,128)S(1)}, u32[]{:S(2)}) copy-start(f32[8,512,128,3]{2,1,3,0:T(8,128)S(1)} %get-tuple-element.76) | copy-start | bytes 18874372
  175.4 8.0 %copy-start.12 = (bf16[512,512]{0,1:T(8,128)(2,1)S(1)}, bf16[512,512]{0,1:T(8,128)(2,1)}, u32[]{:S(2)}) copy-start(bf16[512,512]{0,1:T(8,128)(2,1)} %copy.175) | copy-start | bytes 1572868
  175.4 7.9 %copy-start.22 = (pred[128,512]{0,1:T(8,128)(4,1)S(1)}, pred[128,512]{0,1:T(8,128)(4,1)}, u32[]{:S(2)}) copy-start(pred[128,512]{0,1:T(8,128)(4,1)} %get-tuple-element.64) | copy-start | bytes 196612
  179.6 4.9 copy-start.10
  179.6 4.9 copy-start.24
  183.3 2.5 copy-start.9
  183.3 2.5 copy-start.26
  184.4 13.1 %copy-start.40 = (f32[8,3,128]{2,1,0:T(4,128)}, f32[8,3,128]{2,1,0:T(4,128)S(1)}, u32[]{:S(2)}) copy-start(f32[8,3,128]{2,1,0:T(4,128)S(1)} %get-tuple-element.67) | copy-start | bytes 36868
  184.5 45.5 %copy-start.2 = (f32[8,512,128,3]{2,1,3,0:T(8,128)}, f32[8,512,128,3]{2,1,3,0:T(8,128)S(1)}, u32[]{:S(2)}) copy-start(f32[8,512,128,3]{2,1,3,0:T(8,128)S(1)} %get-tuple-element.68) | copy-start | bytes 18874372
  184.5 5.6 copy-start.11
  184.5 5.6 copy-start.28
  185.8 11.8 %copy-start.42 = (f32[8,3,128]{2,1,0:T(4,128)}, f32[8,3,128]{2,1,0:T(4,128)S(1)}, u32[]{:S(2)}) copy-start(f32[8,3,128]{2,1,0:T(4,128)S(1)} %get-tuple-element.69) | copy-start | bytes 36868
  185.8 42.6 %copy-start.4 = (f32[8,512,128,3]{2,1,3,0:T(8,128)}, f32[8,512,128,3]{2,1,3,0:T(8,128)S(1)}, u32[]{:S(2)}) copy-start(f32[8,512,128,3]{2,1,3,0:T(8,128)S(1)} %get-tuple-element.70) | copy-start | bytes 18874372
  185.9 7.9 %copy-start.8 = (bf16[512,512]{0,1:T(8,128)(2,1)S(1)}, bf16[512,512]{0,1:T(8,128)(2,1)}, u32[]{:S(2)}) copy-start(bf16[512,512]{0,1:T(8,128)(2,1)} %copy.144) | copy-start | bytes 1572868
  185.9 7.9 %copy-start.30 = (pred[128,512]{0,1:T(8,128)(4,1)S(1)}, pred[128,512]{0,1:T(8,128)(4,1)}, u32[]{:S(2)}) copy-start(pred[128,512]{0,1:T(8,128)(4,1)} %get-tuple-element.66) | copy-start | bytes 196612
  190.1 7.5 %copy-start.44 = (f32[8,3,128]{2,1,0:T(4,128)}, f32[8,3,128]{2,1,0:T(4,128)S(1)}, u32[]{:S(2)}) copy-start(f32[8,3,128]{2,1,0:T(4,128)S(1)} %get-tuple-element.71) | copy-start | bytes 36868
  190.1 7.5 %copy-start.31 = (pred[128,512]{0,1:T(8,128)(4,1)S(1)}, pred[128,512]{0,1:T(8,128)(4,1)}, u32[]{:S(2)}) copy-start(pred[128,512]{0,1:T(8,128)(4,1)} %get-tuple-element.66) | copy-start | bytes 196612
  193.8 8.2 %copy-start.29 = (pred[128,512]{0,1:T(8,128)(4,1)S(1)}, pred[128,512]{0,1:T(8,128)(4,1)}, u32[]{:S(2)}) copy-start(pred[128,512]{0,1:T(8,128)(4,1)} %get-tuple-element.65) | copy-start | bytes 196612
  197.6 32.3 %copy-start.47 = (f32[8,3,128]{2,1,0:T(4,128)}, f32[8,3,128]{2,1,0:T(4,128)S(1)}, u32[]{:S(2)}) copy-start(f32[8,3,128]{2,1,0:T(4,128)S(1)} %get-tuple-element.12) | copy-start | bytes 36868
  210.5 8.6 %copy-start.18 = (pred[128,512]{0,1:T(8,128)(4,1)S(1)}, pred[128,512]{0,1:T(8,128)(4,1)}, u32[]{:S(2)}) copy-start(pred[128,512]{0,1:T(8,128)(4,1)} %get-tuple-element.59) | copy-start | bytes 196612
  221.0 3.0 copy-start.27
  222.5 5.9 copy-start.25
  224.0 7.5 %slice-start.16 = ((s8[6291456]{0:T(1024)(128)(4,1)}), s8[4194304]{0:T(1024)(128)(4,1)S(1)}, s32[]{:S(2)}) async-start(s8[6291456]{0:T(1024)(128)(4,1)} %bitcast.661), calls=%async_computation.23 | async-start | bytes 8388608
  228.4 3.1 slice-start.17
  228.4 3.1 copy-start.37
  230.0 4.1 slice-start.14
  231.6 2.5 slice-start.15
  231.6 2.5 copy-start.36
  233.3 2.5 slice-start.12
  233.3 2.5 copy-start.35
  235.9 2.5 slice-start.8
  235.9 2.5 copy-start.34
  238.9 2.5 slice-start.11
  240.7 2.5 copy-start.32
  243.2 4.6 copy-start.53
  247.7 5.0 slice-start.2
  247.7 5.0 copy-start.52
  247.8 5.0 slice-start.3
  252.8 2.7 slice-start.7
  254.6 2.8 slice-start.4
  257.5 2.6 slice-start.1
  257.5 4.4 slice-start.18
  260.2 3.1 copy-start.49
  263.3 373.3 %copy-start.7 = (bf16[128,1536]{1,0:T(8,128)(2,1)}, bf16[128,1536]{1,0:T(8,128)(2,1)S(1)}, u32[]{:S(2)}) copy-start(bf16[128,1536]{1,0:T(8,128)(2,1)S(1)} %get-tuple-element.90) | copy-start | bytes 1179652
  293.8 143.5 %all-to-all-start = ((bf16[16,5,26,1536]{3,2,1,0:T(8,128)(2,1)}), bf16[16,5,26,1536]{3,2,1,0:T(8,128)(2,1)}, u32[]{:S(2)}, u32[]{:S(2)}) async-start(bf16[16,5,26,1536]{3,2,1,0:T(8,128)(2,1)} %bitcast.644), calls=%async_computation | async-start | bytes 15728640 | tf_op jit(solution)/shard_map/all_to_all | solution.py:172
  299.0 150.3 %all-gather.18.cloned.1.call-start = ((), (), s32[]{:S(2)}) async-start(), calls=%async_computation.6 | async-start | bytes 5898240 | tf_op jit(solution)/shard_map/all_gather | solution.py:96
  468.9 11.5 %copy-start.57 = (bf16[128,8]{0,1:T(8,128)(2,1)S(1)}, bf16[128,8]{0,1:T(8,128)(2,1)}, u32[]{:S(2)}) copy-start(bf16[128,8]{0,1:T(8,128)(2,1)} %param.23) | copy-start | bytes 6148
  468.9 135.2 %all-to-all-start.1 = ((bf16[16,5,26,1536]{3,2,1,0:T(8,128)(2,1)}), bf16[16,5,26,1536]{3,2,1,0:T(8,128)(2,1)}, u32[]{:S(2)}, u32[]{:S(2)}) async-start(bf16[16,5,26,1536]{3,2,1,0:T(8,128)(2,1)} %copy.186), calls=%async_computation.1 | async-start | bytes 15728640 | tf_op jit(solution)/shard_map/all_to_all | solution.py:183
  620.8 16.6 %copy-start.1 = (bf16[1536,512]{1,0:T(8,128)(2,1)S(1)}, bf16[1536,512]{1,0:T(8,128)(2,1)}, u32[]{:S(2)}) copy-start(bf16[1536,512]{1,0:T(8,128)(2,1)} %param.16) | copy-start | bytes 4718596
  (21 other events, 45.1 us)
Sparse Core Ops, SparseCore 0:
  9.7 48.5 all-gather.11
  61.1 60.5 all-gather.9
  123.4 29.1 all-gather.15
  154.1 21.7 all-gather.13
  301.2 17.4 all-gather.17

commit v2 on v1

--- a/solution.py
+++ b/solution.py
@@ -91,10 +91,7 @@
     length = cache_len[0]
     cache_rows = cache_kv[0]
     cache_count = cache_rows.shape[0]
-    gate_up_full, down_full = (
-        lax.all_gather(lax.all_gather(w_gate_up[0], "req", axis=1, tiled=True), "core", axis=0),
-        lax.all_gather(lax.all_gather(w_down[0], "req", axis=2, tiled=True), "core", axis=0),
-    )
+    cache_all = lax.all_gather(cache_rows, ("xz", "core"), axis=0, tiled=True)
     normed = rms_scale(hidden_in, attn_gain)
     query_pos = position_exp * rows_here + jnp.arange(rows_here, dtype=jnp.int32)
     positions = length + query_pos
@@ -115,29 +112,31 @@
         jnp.zeros((kv_heads, group_size, rows_here), jnp.float32),
         jnp.zeros((kv_heads, group_size, rows_here, HEAD_DIM), jnp.float32),
     )
-    shard_rows = cache_count + rows_here
-    joined = jnp.concatenate([cache_rows, new_kv], axis=0)
     running = initial
-    piece = lax.all_gather(joined, ("xz", "core"), axis=0, tiled=True)
-    first_row = jnp.int32(0)
-    key_count = piece.shape[0]
-    for offset in range(0, key_count, key_block):
-        block_size = min(key_block, key_count - offset)
-        key_index = first_row + offset + jnp.arange(block_size, dtype=jnp.int32)
-        owner = key_index // shard_rows
-        within = key_index - owner * shard_rows
-        cached = within < cache_count
-        cache_pos = owner * cache_count + within
-        new_pos = owner * rows_here + within - cache_count
+    for offset in range(0, cache_all.shape[0], key_block):
+        block_size = min(key_block, cache_all.shape[0] - offset)
+        cache_pos = offset + jnp.arange(block_size, dtype=jnp.int32)
         running = attend_block(
             running,
             queries,
-            piece[offset : offset + block_size],
-            jnp.where(
-                cached[None, :],
-                (cache_pos < length)[None, :],
-                new_pos[None, :] <= query_pos[:, None],
-            ),
+            cache_all[offset : offset + block_size],
+            jnp.broadcast_to((cache_pos < length)[None, :], (rows_here, block_size)),
+            kv_width,
+        )
+    new_all = lax.all_gather(new_kv, ("xz", "core"), axis=0, tiled=True)
+    gate_up_local, down_local, new_all = lax.optimization_barrier((w_gate_up[0], w_down[0], new_all))
+    gate_up_full, down_full = (
+        lax.all_gather(lax.all_gather(gate_up_local, "req", axis=1, tiled=True), "core", axis=0),
+        lax.all_gather(lax.all_gather(down_local, "req", axis=2, tiled=True), "core", axis=0),
+    )
+    for offset in range(0, new_all.shape[0], key_block):
+        block_size = min(key_block, new_all.shape[0] - offset)
+        new_pos = offset + jnp.arange(block_size, dtype=jnp.int32)
+        running = attend_block(
+            running,
+            queries,
+            new_all[offset : offset + block_size],
+            new_pos[None, :] <= query_pos[:, None],
             kv_width,
         )
     run_max, run_sum, run_acc = running
@@ -155,18 +154,20 @@
     pairs = lax.axis_size("xz") // (EXPERTS // block_experts)
     flat_ids = expert_ids.reshape(-1)
     matches = (flat_ids[:, None] == jnp.arange(EXPERTS, dtype=jnp.int32)[None, :]).astype(jnp.int32)
-    slot_rank = jnp.sum((jnp.cumsum(matches, axis=0) - matches) * matches, axis=1)
+    pair_count = flat_ids.shape[0]
+    earlier = (
+        jnp.arange(pair_count, dtype=jnp.int32)[None, :] < jnp.arange(pair_count, dtype=jnp.int32)[:, None]
+    ).astype(jnp.bfloat16)
+    before = jnp.dot(earlier, matches.astype(jnp.bfloat16), preferred_element_type=jnp.float32)
+    slot_rank = jnp.sum(before.astype(jnp.int32) * matches, axis=1)
     slot_index = flat_ids * MOST + slot_rank
     token_of = jnp.arange(flat_ids.shape[0], dtype=jnp.int32) // TOPK
-    sectioned = (
-        jnp.zeros((EXPERTS * MOST, width), jnp.bfloat16).at[slot_index].set(moe_in[token_of])
-    )
+    slot_token = jnp.zeros((EXPERTS * MOST,), jnp.int32).at[slot_index].set(token_of)
     blocks = EXPERTS // block_experts
-    outgoing = jnp.broadcast_to(
-        sectioned.reshape(blocks, 1, block_experts, MOST, width),
-        (blocks, pairs, block_experts, MOST, width),
-    )
-    outgoing = outgoing.reshape(blocks * pairs, block_experts, MOST, width)
+    slot_token = jnp.broadcast_to(
+        slot_token.reshape(blocks, 1, block_experts, MOST), (blocks, pairs, block_experts, MOST)
+    ).reshape(blocks * pairs, block_experts, MOST)
+    outgoing = moe_in[slot_token]
     gate_up = jnp.einsum(
         "skmd,ckdf->sckmf",
         lax.all_to_all(outgoing, "xz", split_axis=0, concat_axis=0, tiled=True),

time: 655 us -> 610 us (0.931)
  other arithmetic: 70.4 us -> 50.2 us
  waiting for transfers between devices: 345 us -> 327 us
  local copies, waits for them, and re-layouts: 108 us -> 92.7 us
  matrix products: 87.5 us -> 100 us
    all_gather x5 -> x6, waiting for transfers between devices: 81.9 us -> 61.6 us  [the longest x1 32.4 us: shards(): new_all = lax.all_gather(new_kv, ('xz', 'core'), axis=0, tiled=True)]
    gather x0 -> x2, local copies, waits for them, and re-layouts: none -> 18.6 us  [shards(): outgoing = moe_in[slot_token]]
    slice x12 -> x11, local copies, waits for them, and re-layouts: 25.3 us -> 8.9 us  [attend_block(): key_heads = block_rows[:, :kv_width].reshape(block_size, kv_heads, head_dim)]
    scatter x1, local copies, waits for them, and re-layouts: 18.6 us -> 4.61 us  [shards(): jnp.zeros((EXPERTS * MOST,), jnp.int32).at[slot_index].set(token_of)]
    broadcast_in_dim x2 -> x1, local copies, waits for them, and re-layouts: 11.8 us -> 0.1 us  [shards(): jnp.broadcast_to(slot_token.reshape(blocks, 1, block_experts, MOST), (blo...]
    another operation x5 -> x2, other arithmetic: 11.5 us -> 0.15 us
    dot_general x11, matrix products: 23.5 us -> 33 us  [attend_block(): jnp.einsum('kgtr,rkd->kgtd', weights.astype(jnp.bfloat16), value_heads, p...]
    slice x12 -> x13, local copies, waits for them, and re-layouts: 21.6 us -> 29.5 us  [attend_block(): block_rows[:, kv_width:].reshape(block_size, kv_heads, head_dim)]
  transfers between devices with their start and end apart: 7 -> 8, of which waited for: 4 -> 4; matrix products, arithmetic and copies ran while one was open for 32% -> 26% of each run, Pallas kernels for 0% -> 0%
where the time goes in v2:
time: 610 us; the launch traced here: 603 us
  waiting for transfers between devices  327 us (54%)
  matrix products  100 us (16%)
  local copies, waits for them, and re-layouts  92.7 us (15%)
  other arithmetic  50.2 us (8%)
  starting transfers between devices  16.6 us (3%)
  between operations  16.2 us (3%)
    all_to_all x1, waiting for transfers between devices, shards(): lax.all_to_all(outgoing, 'xz', split_axis=0, concat_axis=0, tiled=True)  139 us
    all_to_all x1, waiting for transfers between devices, shards(): lax.all_to_all(computed, 'xz', split_axis=0, concat_axis=0, tiled=True)  125 us
    dot_general x11, matrix products, attend_block(): jnp.einsum('tkgd,rkd->kgtr', queries, key_heads, preferred_element_type=j...  33.6 us
    dot_general x11, matrix products, attend_block(): jnp.einsum('kgtr,rkd->kgtd', weights.astype(jnp.bfloat16), value_heads, p...  33 us
    all_gather x1, waiting for transfers between devices, shards(): new_all = lax.all_gather(new_kv, ('xz', 'core'), axis=0, tiled=True)  32.4 us
    slice x13, local copies, waits for them, and re-layouts, attend_block(): block_rows[:, kv_width:].reshape(block_size, kv_heads, head_dim)  29.5 us
    reduce_sum x11, other arithmetic, attend_block(): new_sum = run_sum * factor + jnp.sum(weights, axis=-1)  29.5 us
    all_gather x1, waiting for transfers between devices, shards(): cache_all = lax.all_gather(cache_rows, ('xz', 'core'), axis=0, tiled=True)  29.2 us
  transfers between devices with their start and end apart: 8, of which 4 were waited for; matrix products, arithmetic and copies ran while one was open for 26% of the time, Pallas kernels for 0%

profile of v2, /device:TPU:0, one launch (start us, length us, event | category | flops | bytes accessed | tf_op | source)
XLA Modules:
  0.0 602.7 jit_solution(8716280990917006149)
XLA Ops:
  10.7 1.8 fusion.252
  12.6 2.0 convolution_convert_fusion
  17.0 4.6 scatter_custom_fusion
  23.0 4.3 fusion.254
  28.6 29.2 %all-gather.16.cloned.1.call-done = bf16[1,1536,1024]{2,1,0:T(8,128)(2,1)} async-done(((bf16[1,48,1024]{2,1,0:T(8,128)(2,1)}), bf16[1,1536,1024]{2,1,0:T(8,128)(2,1)}) %all-gather.16.cloned.1.call-update) | async-done | bytes 3145744 | tf_op jit(solution)/shard_map/all_gather | solution.py:94
  57.8 3.2 fusion.260
  62.6 2.0 copy.89
  66.7 4.9 bitcast_reduce_fusion.2
  71.6 4.4 bitcast_reduce_fusion
  76.0 4.4 bitcast_reduce_fusion.1
  80.4 32.4 %all-gather.10.cloned.1.call-done = bf16[4096,1024]{1,0:T(8,128)(2,1)} async-done(((bf16[128,1024]{1,0:T(8,128)(2,1)}), bf16[4096,1024]{1,0:T(8,128)(2,1)}) %all-gather.10.cloned.1.call-update) | async-done | bytes 8388624 | tf_op jit(solution)/shard_map/all_gather | solution.py:126
  112.8 5.8 fusion.259
  118.5 2.1 copy.102
  120.6 2.0 copy.96
  125.8 2.0 copy.98
  127.8 2.1 copy.101
  129.9 2.0 copy.104
  131.9 2.0 copy.107
  133.9 2.1 copy.110
  136.1 2.0 copy.113
  138.1 2.0 copy.116
  140.1 2.1 copy.119
  142.9 2.4 fusion.12
  145.3 3.8 fusion.10
  149.1 1.3 fusion.16
  151.7 1.3 fusion.14
  153.0 4.3 fusion.13
  157.4 4.4 fusion.11
  163.1 2.2 slice-done.3
  165.3 1.9 fusion.34
  167.3 4.1 fusion.18
  171.4 3.9 fusion.20
  175.3 1.8 fusion.36
  177.1 2.0 fusion.22
  179.1 3.9 fusion.24
  183.0 2.0 fusion.26
  185.0 2.0 fusion.28
  187.1 2.0 fusion.30
  189.1 2.0 fusion.32
  191.2 1.8 fusion.94
  193.4 2.9 fusion.97
  196.4 2.7 fusion.100
  199.2 3.9 fusion.38
  203.1 5.5 fusion.103
  208.7 2.8 fusion.106
  211.5 2.8 fusion.109
  214.3 2.8 fusion.112
  217.3 4.0 fusion.115
  221.4 3.9 fusion.136
  225.5 1.6 fusion.130
  228.6 2.2 fusion.187
  232.0 8.6 %gather_fusion = bf16[2080,1536]{1,0:T(8,128)(2,1)} fusion(bf16[128,1536]{1,0:T(8,128)(2,1)S(1)} %fusion.195, s32[3072]{0:T(1024)S(1)} %pad_clamp_fusion), kind=kCustom, calls=%fused_computation | custom fusion | bytes 12787840 | tf_op jit(solution)/shard_map/gather | solution.py:170
  240.6 10.0 %reshape.871 = bf16[16,5,26,1536]{3,2,1,0:T(8,128)(2,1)} reshape(bf16[2080,1536]{1,0:T(8,128)(2,1)} %gather_fusion) | data formatting | bytes 12779520 | tf_op jit(solution)/shard_map/gather | solution.py:170
  250.6 5.4 all-to-all-start
  256.5 138.8 %all-to-all-done = bf16[16,5,26,1536]{3,2,1,0:T(8,128)(2,1)} async-done(((bf16[16,5,26,1536]{3,2,1,0:T(8,128)(2,1)}), bf16[16,5,26,1536]{3,2,1,0:T(8,128)(2,1)}, u32[]{:S(2)}, u32[]{:S(2)}) %all-to-all-start) | async-done | bytes 6389792 | tf_op jit(solution)/shard_map/all_to_all | solution.py:173
  395.4 12.0 %fusion.78 = f32[16,2,5,26,256]{4,3,0,1,2:T(8,128)} fusion(bf16[2,5,1536,256,1]{3,2,1,0,4:T(8,128)(2,1)} %bitcast.681, bf16[16,5,26,1536]{3,2,1,0:T(8,128)(2,1)} %all-to-all-done), kind=kOutput, calls=%fused_computation.101 | convolution fusion | flops 3271557120 | bytes 18513920 | tf_op jit(solution)/shard_map/skmd,ckdf->sckmf/dot_general | solution.py:171
  407.4 12.3 %convert_reduce_fusion.1 = bf16[5,1536,16,26]{1,3,2,0:T(8,128)(2,1)} fusion(bf16[2,5,128,1536,1]{3,2,4,1,0:T(8,128)(2,1)} %bitcast.682, f32[16,2,5,26,256]{4,3,0,1,2:T(8,128)} %fusion.78), kind=kOutput, calls=%fused_computation.4 | convolution fusion | flops 1648558080 | bytes 14581760 | tf_op jit(solution)/shard_map/sckmf,ckfd->sckmd/dot_general | solution.py:180
  419.7 7.3 %copy.125 = bf16[16,5,26,1536]{3,2,1,0:T(8,128)(2,1)} copy(bf16[16,5,26,1536]{3,2,0,1:T(8,128)(2,1)} %bitcast.646) | data formatting | bytes 12779520 | tf_op jit(solution)/shard_map/reduce_sum | solution.py:183
  426.9 10.1 %all-to-all-start.1 = ((bf16[16,5,26,1536]{3,2,1,0:T(8,128)(2,1)}), bf16[16,5,26,1536]{3,2,1,0:T(8,128)(2,1)}, u32[]{:S(2)}, u32[]{:S(2)}) async-start(bf16[16,5,26,1536]{3,2,1,0:T(8,128)(2,1)} %copy.125), calls=%async_computation.1 | async-start | bytes 15728640 | tf_op jit(solution)/shard_map/all_to_all | solution.py:184
  437.2 125.3 %all-to-all-done.1 = bf16[16,5,26,1536]{3,2,1,0:T(8,128)(2,1)} async-done(((bf16[16,5,26,1536]{3,2,1,0:T(8,128)(2,1)}), bf16[16,5,26,1536]{3,2,1,0:T(8,128)(2,1)}, u32[]{:S(2)}, u32[]{:S(2)}) %all-to-all-start.1) | async-done | bytes 6389792 | tf_op jit(solution)/shard_map/all_to_all | solution.py:184
  562.4 8.8 %convert_reduce_fusion = f32[8,5,26,1536]{3,2,1,0:T(8,128)} fusion(bf16[16,5,26,1536]{3,2,1,0:T(8,128)(2,1)} %all-to-all-done.1), kind=kLoop, calls=%fused_computation.3 | loop fusion | flops 4792320 | bytes 12779520 | tf_op jit(solution)/shard_map/reduce_sum | solution.py:185
  571.2 7.8 %reshape.868 = f32[1040,1536]{1,0:T(8,128)} reshape(f32[8,5,26,1536]{3,2,1,0:T(8,128)} %convert_reduce_fusion) | data formatting | bytes 12779520 | tf_op jit(solution)/shard_map/reshape | solution.py:188
  579.0 10.7 %gather_fusion.1 = f32[1024,1536]{1,0:T(8,128)} fusion(f32[1040,1536]{1,0:T(8,128)} %reshape.868, s32[1024]{0:T(1024)S(1)} %broadcast_clamp_fusion), kind=kCustom, calls=%fused_computation.1 | custom fusion | bytes 12587008 | tf_op jit(solution)/shard_map/gather | solution.py:189
  589.8 5.1 fusion.3
  (233 shorter events, 22.9 us)
Async XLA Ops:
  7.2 3.5 copy-start
  7.2 15.8 %copy-start.6 = (bf16[128,1536]{1,0:T(8,128)(2,1)S(1)}, bf16[128,1536]{1,0:T(8,128)(2,1)}, u32[]{:S(2)}) copy-start(bf16[128,1536]{1,0:T(8,128)(2,1)} %param.13) | copy-start | bytes 1179652
  7.2 8.2 %copy-start.49 = (bf16[1536]{0:T(1024)(128)(2,1)S(1)}, bf16[1536]{0:T(1024)(128)(2,1)}, u32[]{:S(2)}) copy-start(bf16[1536]{0:T(1024)(128)(2,1)} %param.21) | copy-start | bytes 9220
  7.2 8.8 %copy-start.43 = (s32[128,8]{0,1:T(8,128)S(1)}, s32[128,8]{0,1:T(8,128)}, u32[]{:S(2)}) copy-start(s32[128,8]{0,1:T(8,128)} %param.22) | copy-start | bytes 12292
  7.2 50.6 %all-gather.16.cloned.1.call-start = ((), (), s32[]{:S(2)}) async-start(), calls=%async_computation.5 | async-start | bytes 3244032 | tf_op jit(solution)/shard_map/all_gather | solution.py:94
  7.9 104.8 %all-gather.10.cloned.1.call-start = ((), (), s32[]{:S(2)}) async-start(), calls=%async_computation.2 | async-start | bytes 8650752 | tf_op jit(solution)/shard_map/all_gather | solution.py:126
  15.4 201.7 %all-gather.14.cloned.1.call-start = ((), (), s32[]{:S(2)}) async-start(), calls=%async_computation.4 | async-start | bytes 4915200 | tf_op jit(solution)/shard_map/all_gather | solution.py:129
  17.0 4.6 copy-start.44
  66.7 9.3 %copy-start.46 = (pred[512]{0:T(512)(128)(4,1)S(1)}, pred[512]{0:T(512)(128)(4,1)}, u32[]{:S(2)}) copy-start(pred[512]{0:T(512)(128)(4,1)} %broadcast_compare_fusion.8) | copy-start | bytes 1540
  142.3 114.2 %all-gather.12.cloned.1.call-start = ((), (), s32[]{:S(2)}) async-start(), calls=%async_computation.3 | async-start | bytes 2457600 | tf_op jit(solution)/shard_map/all_gather | solution.py:130
  142.9 6.2 %copy-start.8 = (bf16[512,512]{0,1:T(8,128)(2,1)S(1)}, bf16[512,512]{0,1:T(8,128)(2,1)}, u32[]{:S(2)}) copy-start(bf16[512,512]{0,1:T(8,128)(2,1)} %copy.114) | copy-start | bytes 1572868
  145.3 17.7 %copy-start.33 = (f32[8,3,128]{2,1,0:T(4,128)}, f32[8,3,128]{2,1,0:T(4,128)S(1)}, u32[]{:S(2)}) copy-start(f32[8,3,128]{2,1,0:T(4,128)S(1)} %get-tuple-element.80) | copy-start | bytes 36868
  145.3 5.1 copy-start.10
  149.1 13.9 %copy-start.35 = (f32[8,3,128]{2,1,0:T(4,128)}, f32[8,3,128]{2,1,0:T(4,128)S(1)}, u32[]{:S(2)}) copy-start(f32[8,3,128]{2,1,0:T(4,128)S(1)} %get-tuple-element.84) | copy-start | bytes 36868
  150.4 12.6 %copy-start.38 = (f32[8,3,128]{2,1,0:T(4,128)}, f32[8,3,128]{2,1,0:T(4,128)S(1)}, u32[]{:S(2)}) copy-start(f32[8,3,128]{2,1,0:T(4,128)S(1)} %get-tuple-element.72) | copy-start | bytes 36868
  150.4 36.6 %copy-start.3 = (f32[8,512,128,3]{1,2,3,0:T(8,128)}, f32[8,512,128,3]{1,2,3,0:T(8,128)S(1)}, u32[]{:S(2)}) copy-start(f32[8,512,128,3]{1,2,3,0:T(8,128)S(1)} %get-tuple-element.73) | copy-start | bytes 18874372
  151.7 11.4 %copy-start.40 = (f32[8,3,128]{2,1,0:T(4,128)}, f32[8,3,128]{2,1,0:T(4,128)S(1)}, u32[]{:S(2)}) copy-start(f32[8,3,128]{2,1,0:T(4,128)S(1)} %get-tuple-element.74) | copy-start | bytes 36868
  151.7 33.3 %copy-start.4 = (f32[8,512,128,3]{1,2,3,0:T(8,128)}, f32[8,512,128,3]{1,2,3,0:T(8,128)S(1)}, u32[]{:S(2)}) copy-start(f32[8,512,128,3]{1,2,3,0:T(8,128)S(1)} %get-tuple-element.75) | copy-start | bytes 18874372
  151.7 5.6 copy-start.17
  153.0 30.0 %copy-start.5 = (f32[8,512,128,3]{1,2,3,0:T(8,128)}, f32[8,512,128,3]{1,2,3,0:T(8,128)S(1)}, u32[]{:S(2)}) copy-start(f32[8,512,128,3]{1,2,3,0:T(8,128)S(1)} %get-tuple-element.77) | copy-start | bytes 18874372
  157.3 5.7 copy-start.31
  157.3 5.7 copy-start.32
  157.3 5.7 copy-start.37
  157.3 5.8 slice-start.2
  157.4 5.8 copy-start.48
  161.7 3.6 slice-start.3
  163.0 26.1 %copy-start.2 = (f32[8,512,128,3]{1,2,3,0:T(8,128)}, f32[8,512,128,3]{1,2,3,0:T(8,128)S(1)}, u32[]{:S(2)}) copy-start(f32[8,512,128,3]{1,2,3,0:T(8,128)S(1)} %get-tuple-element.71) | copy-start | bytes 18874372
  165.3 10.0 %slice-start.4 = ((s8[6291456]{0:T(1024)(128)(4,1)}), s8[2097152]{0:T(1024)(128)(4,1)S(1)}, s32[]{:S(2)}) async-start(s8[6291456]{0:T(1024)(128)(4,1)} %bitcast.632), calls=%async_computation.12 | async-start | bytes 4194304
  167.3 8.0 %slice-start.5 = ((s8[6291456]{0:T(1024)(128)(4,1)}), s8[4194304]{0:T(1024)(128)(4,1)S(1)}, s32[]{:S(2)}) async-start(s8[6291456]{0:T(1024)(128)(4,1)} %bitcast.632), calls=%async_computation.13 | async-start | bytes 8388608
  167.3 8.0 %copy-start.47 = (pred[512]{0:T(512)(128)(4,1)S(1)}, pred[512]{0:T(512)(128)(4,1)}, u32[]{:S(2)}) copy-start(pred[512]{0:T(512)(128)(4,1)} %broadcast_compare_fusion.8) | copy-start | bytes 1540
  171.4 5.8 copy-start.16
  185.0 6.1 %slice-start.14 = ((s8[6291456]{0:T(1024)(128)(4,1)}), s8[2097152]{0:T(1024)(128)(4,1)S(1)}, s32[]{:S(2)}) async-start(s8[6291456]{0:T(1024)(128)(4,1)} %bitcast.642), calls=%async_computation.22 | async-start | bytes 4194304
  187.0 4.1 slice-start.15
  187.0 4.1 copy-start.19
  187.1 4.1 copy-start.30
  189.1 3.9 slice-start.16
  193.4 2.9 copy-start.28
  199.1 4.0 copy-start.15
  199.1 4.0 copy-start.27
  199.1 196.3 %all-gather.20.cloned.1.call-start = ((), (), s32[]{:S(2)}) async-start(), calls=%async_computation.7 | async-start | bytes 11796480 | tf_op jit(solution)/shard_map/all_gather | solution.py:129
  199.2 9.5 %slice-start.12 = ((s8[6291456]{0:T(1024)(128)(4,1)}), s8[4194304]{0:T(1024)(128)(4,1)S(1)}, s32[]{:S(2)}) async-start(s8[6291456]{0:T(1024)(128)(4,1)} %bitcast.640), calls=%async_computation.20 | async-start | bytes 8388608
  203.1 5.6 slice-start.13
  203.1 5.5 copy-start.13
  203.1 5.5 copy-start.26
  203.1 8.4 %slice-start.10 = ((s8[6291456]{0:T(1024)(128)(4,1)}), s8[4194304]{0:T(1024)(128)(4,1)S(1)}, s32[]{:S(2)}) async-start(s8[6291456]{0:T(1024)(128)(4,1)} %bitcast.638), calls=%async_computation.18 | async-start | bytes 8388608
  208.7 5.6 slice-start.8
  214.3 2.9 copy-start.39
  214.3 3.0 copy-start.23
  217.3 4.0 copy-start.22
  217.3 8.0 %slice-start.6 = ((s8[6291456]{0:T(1024)(128)(4,1)}), s8[4194304]{0:T(1024)(128)(4,1)S(1)}, s32[]{:S(2)}) async-start(s8[6291456]{0:T(1024)(128)(4,1)} %bitcast.634), calls=%async_computation.14 | async-start | bytes 8388608
  221.4 4.0 slice-start.7
  221.4 4.0 copy-start.21
  221.4 5.7 slice-start
  225.4 2.9 copy-start.55
  225.5 3.2 copy-start.56
  225.5 5.4 slice-start.18
  228.6 3.2 copy-start.42
  231.8 363.1 %copy-start.7 = (bf16[128,1536]{1,0:T(8,128)(2,1)}, bf16[128,1536]{1,0:T(8,128)(2,1)S(1)}, u32[]{:S(2)}) copy-start(bf16[128,1536]{1,0:T(8,128)(2,1)S(1)} %get-tuple-element.93) | copy-start | bytes 1179652
  250.6 144.8 %all-to-all-start = ((bf16[16,5,26,1536]{3,2,1,0:T(8,128)(2,1)}), bf16[16,5,26,1536]{3,2,1,0:T(8,128)(2,1)}, u32[]{:S(2)}, u32[]{:S(2)}) async-start(bf16[16,5,26,1536]{3,2,1,0:T(8,128)(2,1)} %reshape.871), calls=%async_computation | async-start | bytes 15728640 | tf_op jit(solution)/shard_map/all_to_all | solution.py:173
  256.0 151.4 %all-gather.18.cloned.1.call-start = ((), (), s32[]{:S(2)}) async-start(), calls=%async_computation.6 | async-start | bytes 5898240 | tf_op jit(solution)/shard_map/all_gather | solution.py:130
  426.9 10.1 %copy-start.50 = (bf16[128,8]{0,1:T(8,128)(2,1)S(1)}, bf16[128,8]{0,1:T(8,128)(2,1)}, u32[]{:S(2)}) copy-start(bf16[128,8]{0,1:T(8,128)(2,1)} %param.23) | copy-start | bytes 6148
  426.9 10.2 %copy-start.45 = (s32[1024,1]{0,1:T(1,128)S(1)}, s32[1024,1]{0,1:T(1,128)}, u32[]{:S(2)}) copy-start(s32[1024,1]{0,1:T(1,128)} %copy-done.44) | copy-start | bytes 12292
  426.9 135.5 %all-to-all-start.1 = ((bf16[16,5,26,1536]{3,2,1,0:T(8,128)(2,1)}), bf16[16,5,26,1536]{3,2,1,0:T(8,128)(2,1)}, u32[]{:S(2)}, u32[]{:S(2)}) async-start(bf16[16,5,26,1536]{3,2,1,0:T(8,128)(2,1)} %copy.125), calls=%async_computation.1 | async-start | bytes 15728640 | tf_op jit(solution)/shard_map/all_to_all | solution.py:184
  579.0 16.6 %copy-start.1 = (bf16[1536,512]{1,0:T(8,128)(2,1)S(1)}, bf16[1536,512]{1,0:T(8,128)(2,1)}, u32[]{:S(2)}) copy-start(bf16[1536,512]{1,0:T(8,128)(2,1)} %param.16) | copy-start | bytes 4718596
  (21 other events, 52.6 us)
Sparse Core Ops, SparseCore 0:
  10.3 47.4 all-gather.15
  60.6 52.1 all-gather.9
  142.4 45.5 all-gather.13
  199.3 29.2 all-gather.11
  230.0 21.7 all-gather.19
  258.1 17.4 all-gather.17

commit v3 on v2

--- a/solution.py
+++ b/solution.py
@@ -16,6 +16,7 @@
 norm_eps = 1e-06
 neg_fill = -1e30
 key_block = 512
+EXP_AXES = ("x", "zhi", "zlo", "core")
 
 
 def rms_scale(values, gain):
@@ -87,11 +88,15 @@
     kv_heads = kv_width // HEAD_DIM
     head_count = w_query.shape[1] // HEAD_DIM
     group_size = head_count // kv_heads
-    position_exp = lax.axis_index("xz") * lax.axis_size("core") + lax.axis_index("core")
+    core = lax.axis_index("core")
+    position_exp = (
+        (lax.axis_index("x") * lax.axis_size("zhi") + lax.axis_index("zhi")) * lax.axis_size("zlo")
+        + lax.axis_index("zlo")
+    ) * lax.axis_size("core") + core
     length = cache_len[0]
     cache_rows = cache_kv[0]
     cache_count = cache_rows.shape[0]
-    cache_all = lax.all_gather(cache_rows, ("xz", "core"), axis=0, tiled=True)
+    cache_all = lax.all_gather(cache_rows, EXP_AXES, axis=0, tiled=True)
     normed = rms_scale(hidden_in, attn_gain)
     query_pos = position_exp * rows_here + jnp.arange(rows_here, dtype=jnp.int32)
     positions = length + query_pos
@@ -123,11 +128,11 @@
             jnp.broadcast_to((cache_pos < length)[None, :], (rows_here, block_size)),
             kv_width,
         )
-    new_all = lax.all_gather(new_kv, ("xz", "core"), axis=0, tiled=True)
+    new_all = lax.all_gather(new_kv, EXP_AXES, axis=0, tiled=True)
     gate_up_local, down_local, new_all = lax.optimization_barrier((w_gate_up[0], w_down[0], new_all))
     gate_up_full, down_full = (
-        lax.all_gather(lax.all_gather(gate_up_local, "req", axis=1, tiled=True), "core", axis=0),
-        lax.all_gather(lax.all_gather(down_local, "req", axis=2, tiled=True), "core", axis=0),
+        lax.all_gather(lax.all_gather(gate_up_local, "zlo", axis=0), "req", axis=2, tiled=True),
+        lax.all_gather(lax.all_gather(down_local, "zlo", axis=0), "req", axis=3, tiled=True),
     )
     for offset in range(0, new_all.shape[0], key_block):
         block_size = min(key_block, new_all.shape[0] - offset)
@@ -151,7 +156,6 @@
     moe_in = rms_scale(attended, moe_gain)
     block_experts = gate_up_full.shape[1]
     slice_width = down_full.shape[2]
-    pairs = lax.axis_size("xz") // (EXPERTS // block_experts)
     flat_ids = expert_ids.reshape(-1)
     matches = (flat_ids[:, None] == jnp.arange(EXPERTS, dtype=jnp.int32)[None, :]).astype(jnp.int32)
     pair_count = flat_ids.shape[0]
@@ -164,28 +168,25 @@
     token_of = jnp.arange(flat_ids.shape[0], dtype=jnp.int32) // TOPK
     slot_token = jnp.zeros((EXPERTS * MOST,), jnp.int32).at[slot_index].set(token_of)
     blocks = EXPERTS // block_experts
-    slot_token = jnp.broadcast_to(
-        slot_token.reshape(blocks, 1, block_experts, MOST), (blocks, pairs, block_experts, MOST)
-    ).reshape(blocks * pairs, block_experts, MOST)
-    outgoing = moe_in[slot_token]
+    outgoing = moe_in[slot_token.reshape(blocks, block_experts, MOST)]
+    arrived = lax.all_to_all(outgoing, ("x", "zhi"), split_axis=0, concat_axis=0, tiled=True)
+    arrived = lax.all_gather(arrived, "core", axis=0)
     gate_up = jnp.einsum(
-        "skmd,ckdf->sckmf",
-        lax.all_to_all(outgoing, "xz", split_axis=0, concat_axis=0, tiled=True),
-        gate_up_full,
-        preferred_element_type=jnp.float32,
+        "askmd,pkdf->aspkmf", arrived, gate_up_full, preferred_element_type=jnp.float32
     )
     activated = (jax.nn.silu(gate_up[..., :slice_width]) * gate_up[..., slice_width:]).astype(
         jnp.bfloat16
     )
     computed = jnp.einsum(
-        "sckmf,ckfd->sckmd", activated, down_full, preferred_element_type=jnp.float32
+        "aspkmf,pkfd->aspkmd", activated, down_full, preferred_element_type=jnp.float32
     ).astype(jnp.bfloat16)
-    computed = jnp.sum(computed, axis=1, dtype=jnp.float32).astype(jnp.bfloat16)
-    returned = lax.all_to_all(computed, "xz", split_axis=0, concat_axis=0, tiled=True)
-    summed = jnp.sum(
-        returned.reshape(blocks, pairs, block_experts, MOST, width), axis=1, dtype=jnp.float32
-    )
-    summed = summed.reshape(EXPERTS * MOST, width)
+    computed = jnp.sum(computed, axis=2, dtype=jnp.float32)
+    mine = lax.dynamic_index_in_dim(computed, core, axis=0, keepdims=False)
+    theirs = lax.dynamic_index_in_dim(computed, 1 - core, axis=0, keepdims=False)
+    theirs = lax.ppermute(theirs, "core", [(0, 1), (1, 0)])
+    computed = (mine + theirs).astype(jnp.bfloat16)
+    returned = lax.all_to_all(computed, ("x", "zhi"), split_axis=0, concat_axis=0, tiled=True)
+    summed = returned.astype(jnp.float32).reshape(EXPERTS * MOST, width)
     picked = summed[slot_index] * expert_weights.reshape(-1).astype(jnp.float32)[:, None]
     mixture = jnp.sum(picked.reshape(rows_here, TOPK, width), axis=1)
     layer_out = (attended.astype(jnp.float32) + residual_scale * mixture).astype(jnp.bfloat16)
@@ -194,9 +195,9 @@
 
 def solution(mesh):
     req_size, exp_size = mesh.shape["req"], mesh.shape["exp"]
-    mesh = Mesh(mesh.devices.reshape(req_size, exp_size // 2, 2), ("req", "xz", "core"))
-    rows = ("req", "xz", "core")
-    cols = ("xz", "core")
+    mesh = Mesh(mesh.devices.reshape(req_size, exp_size // 8, 2, 2, 2), ("req",) + EXP_AXES)
+    rows = ("req",) + EXP_AXES
+    cols = EXP_AXES
     in_specs = (
         P(rows, None),
         P(),

time: 610 us -> 657 us (1.077)
  local copies, waits for them, and re-layouts: 92.7 us -> 118 us
  waiting for transfers between devices: 327 us -> 302 us
  matrix products: 100 us -> 122 us
  blocking collectives: 0 us -> 14.3 us
  other arithmetic: 50.2 us -> 61.1 us
    all_to_all x2, waiting for transfers between devices: 264 us -> 112 us  [the longest x1 56.3 us: shards(): lax.all_to_all(computed, ('x', 'zhi'), split_axis=0, concat_axis=0, tiled...]
    all_gather x6, waiting for transfers between devices: 61.6 us -> 178 us  [the longest x1 71.9 us: shards(): lax.all_gather(lax.all_gather(gate_up_local, 'zlo', axis=0), 'req', axis=...]
    all_gather x0 -> x1, blocking collectives: none -> 14.3 us  [shards(): lax.all_gather(down_local, 'zlo', axis=0)]
    another operation x0 -> x1, local copies, waits for them, and re-layouts: none -> 13.9 us
    all_gather x0 -> x2, local copies, waits for them, and re-layouts: none -> 12.7 us  [the longest x1 9.75 us: shards(): arrived = lax.all_gather(arrived, 'core', axis=0)]
    reduce_sum x11, other arithmetic: 29.5 us -> 40.8 us  [attend_block(): new_sum = run_sum * factor + jnp.sum(weights, axis=-1)]
    dot_general x11, matrix products: 33 us -> 44.4 us  [attend_block(): jnp.einsum('kgtr,rkd->kgtd', weights.astype(jnp.bfloat16), value_heads, p...]
    ppermute x0 -> x1, waiting for transfers between devices: none -> 10.3 us  [shards(): theirs = lax.ppermute(theirs, 'core', [(0, 1), (1, 0)])]
  transfers between devices with their start and end apart: 8 -> 9, of which waited for: 4 -> 9; matrix products, arithmetic and copies ran while one was open for 26% -> 11% of each run, Pallas kernels for 0% -> 0%
where the time goes in v3:
time: 657 us; the launch traced here: 647 us
  waiting for transfers between devices  302 us (46%)
  matrix products  122 us (19%)
  local copies, waits for them, and re-layouts  118 us (18%)
  other arithmetic  61.1 us (9%)
  between operations  16.2 us (2%)
  blocking collectives  14.3 us (2%)
  starting transfers between devices  12.4 us (2%)
    all_gather x1, waiting for transfers between devices, shards(): lax.all_gather(lax.all_gather(gate_up_local, 'zlo', axis=0), 'req', axis=...  71.9 us
    all_to_all x1, waiting for transfers between devices, shards(): lax.all_to_all(computed, ('x', 'zhi'), split_axis=0, concat_axis=0, tiled...  56.3 us
    all_to_all x1, waiting for transfers between devices, shards(): lax.all_to_all(outgoing, ('x', 'zhi'), split_axis=0, concat_axis=0, tiled...  55.8 us
    dot_general x11, matrix products, attend_block(): jnp.einsum('kgtr,rkd->kgtd', weights.astype(jnp.bfloat16), value_heads, p...  44.4 us
    dot_general x11, matrix products, attend_block(): jnp.einsum('tkgd,rkd->kgtr', queries, key_heads, preferred_element_type=j...  42.5 us
    reduce_sum x11, other arithmetic, attend_block(): new_sum = run_sum * factor + jnp.sum(weights, axis=-1)  40.8 us
    all_gather x1, waiting for transfers between devices, shards(): lax.all_gather(lax.all_gather(down_local, 'zlo', axis=0), 'req', axis=3,...  36.5 us
    all_gather x1, waiting for transfers between devices, shards(): new_all = lax.all_gather(new_kv, EXP_AXES, axis=0, tiled=True)  32.4 us
  transfers between devices with their start and end apart: 9, of which 9 were waited for; matrix products, arithmetic and copies ran while one was open for 11% of the time, Pallas kernels for 0%

profile of v3, /device:TPU:0, one launch (start us, length us, event | category | flops | bytes accessed | tf_op | source)
XLA Modules:
  0.0 647.0 jit_solution(6857993776049868719)
XLA Ops:
  17.0 4.3 scatter_custom_fusion
  23.3 4.3 fusion.254
  28.8 29.0 %all-gather.17.cloned.1.call-done = bf16[1,1536,1024]{2,1,0:T(8,128)(2,1)} async-done(((bf16[1,48,1024]{2,1,0:T(8,128)(2,1)}), bf16[1,1536,1024]{2,1,0:T(8,128)(2,1)}) %all-gather.17.cloned.1.call-update) | async-done | bytes 3145744 | tf_op jit(solution)/shard_map/all_gather | solution.py:99
  57.7 3.2 fusion.260
  62.6 2.1 copy.176
  66.7 4.3 bitcast_reduce_fusion.2
  71.0 5.0 bitcast_reduce_fusion
  76.0 4.3 bitcast_reduce_fusion.1
  80.3 32.4 %all-gather.11.cloned.1.call-done = bf16[4096,1024]{1,0:T(8,128)(2,1)} async-done(((bf16[128,1024]{1,0:T(8,128)(2,1)}), bf16[4096,1024]{1,0:T(8,128)(2,1)}) %all-gather.11.cloned.1.call-update) | async-done | bytes 8388624 | tf_op jit(solution)/shard_map/all_gather | solution.py:131
  112.7 6.0 fusion.259
  118.7 2.1 copy.189
  122.8 2.1 copy.201
  126.9 2.1 copy.195
  135.1 2.1 copy.185
  137.1 4.9 fusion.13
  143.4 3.8 fusion.17
  147.2 3.8 fusion.16
  151.0 3.8 fusion.15
  154.8 3.8 fusion.14
  158.6 3.8 fusion.12
  162.4 3.8 fusion.18
  167.6 3.0 fusion.19
  170.6 2.8 fusion.94
  175.3 4.5 fusion.21
  179.9 5.4 fusion.97
  187.3 4.5 fusion.23
  191.8 5.4 fusion.100
  198.3 4.5 fusion.25
  202.8 5.4 fusion.103
  208.4 4.6 fusion.27
  213.0 5.4 fusion.106
  218.6 3.9 fusion.29
  222.5 5.3 fusion.109
  228.0 3.9 fusion.31
  231.9 5.4 fusion.112
  237.5 4.0 fusion.33
  241.5 3.9 fusion.115
  245.5 4.2 fusion.35
  258.5 2.2 fusion.187
  261.9 5.2 gather_fusion
  267.1 5.5 reshape.871
  272.6 5.1 all-to-all-start
  278.4 55.8 %all-to-all-done = bf16[8,5,26,1536]{3,2,1,0:T(8,128)(2,1)} async-done(((bf16[8,5,26,1536]{3,2,1,0:T(8,128)(2,1)}), bf16[8,5,26,1536]{3,2,1,0:T(8,128)(2,1)}, u32[]{:S(2)}, u32[]{:S(2)}) %all-to-all-start) | async-done | bytes 3194912 | tf_op jit(solution)/shard_map/all_to_all | solution.py:172
  334.2 5.6 copy.210
  339.9 3.1 all-gather.19.cloned.1.call-done
  343.0 3.0 copy.207
  346.0 14.3 %all-gather.1 = bf16[10,128,384]{2,1,0:T(8,128)(2,1)} all-gather(bf16[5,128,384]{2,1,0:T(8,128)(2,1)S(1)} %bitcast.676), channel_id=3, replica_groups=mesh['req'=4,'x'=4,'zhi'=2,'zlo'=2,'core'=2] {'zlo'}, dimensions={0}, use_global_device_ids=true | all-gather | bytes 1474560 | tf_op jit(solution)/shard_map/all_gather | solution.py:135
  360.4 5.6 all-gather.21.cloned.1.call-done
  366.0 9.8 %copy.211 = bf16[16,5,26,1536]{3,2,0,1:T(8,128)(2,1)} copy(bf16[16,5,26,1536]{3,0,2,1:T(8,128)(2,1)} %all-gather.21.cloned.1.call-done) | data formatting | bytes 12779520 | tf_op jit(solution)/shard_map/all_gather | solution.py:173
  375.7 71.9 %all-gather.15.cloned.1.call-done = bf16[2,5,1536,256]{3,2,0,1:T(8,128)(2,1)} async-done(((bf16[2,5,384,256]{3,2,0,1:T(8,128)(2,1)}), bf16[2,5,1536,256]{3,2,0,1:T(8,128)(2,1)}) %all-gather.15.cloned.1.call-update) | async-done | bytes 7864336 | tf_op jit(solution)/shard_map/all_gather | solution.py:134
  447.6 12.0 %fusion.80 = f32[2,8,2,5,26,256]{5,4,1,0,2,3:T(8,128)} fusion(bf16[2,8,5,26,1536,1]{4,3,1,0,5,2:T(8,128)(2,1)} %bitcast.644, bf16[2,5,1536,256]{3,2,0,1:T(8,128)(2,1)} %all-gather.15.cloned.1.call-done), kind=kOutput, calls=%fused_computation.104 | convolution fusion | flops 3271557120 | bytes 18513920 | tf_op jit(solution)/shard_map/askmd,pkdf->aspkmf/dot_general | solution.py:174
  459.6 36.5 %all-gather.13.cloned.1.call-done = bf16[2,5,128,1536]{3,2,1,0:T(8,128)(2,1)} async-done(((bf16[2,5,128,384]{3,2,1,0:T(8,128)(2,1)}), bf16[2,5,128,1536]{3,2,1,0:T(8,128)(2,1)}) %all-gather.13.cloned.1.call-update) | async-done | bytes 3932176 | tf_op jit(solution)/shard_map/all_gather | solution.py:135
  496.1 14.1 %convert_reduce_fusion = f32[5,1536,2,8,26]{1,4,3,2,0:T(8,128)} fusion(bf16[2,5,128,1536]{3,2,1,0:T(8,128)(2,1)} %all-gather.13.cloned.1.call-done, f32[2,8,2,5,26,256]{5,4,1,0,2,3:T(8,128)} %fusion.80), kind=kOutput, calls=%fused_computation.3 | convolution fusion | flops 1654947840 | bytes 20971520 | tf_op jit(solution)/shard_map/aspkmf,pkfd->aspkmd/dot_general | solution.py:180
  510.1 13.9 %constant_dynamic-slice_fusion = (f32[5,1536,1,8,26]{1,4,3,2,0:T(8,128)}, f32[8,5,26,1536]{3,2,0,1:T(8,128)}) fusion(f32[5,1536,2,8,26]{1,4,3,2,0:T(8,128)} %convert_reduce_fusion, s32[]{:T(128)S(6)} %select_n.137, s32[]{:T(128)S(6)} %select_n.138), kind=kLoop, calls=%fused_computation.247 | loop fusion | bytes 25559048 | tf_op jit(solution)/shard_map/dynamic-slice
  524.1 7.0 %copy.214 = f32[8,5,26,1536]{3,0,2,1:T(8,128)S(1)} copy(f32[8,5,26,1536]{3,2,0,1:T(8,128)} %get-tuple-element.32) | data formatting | bytes 12779520 | tf_op jit(solution)/shard_map/jit(dynamic_index_in_dim)/squeeze | solution.py:185
  531.4 10.3 %collective-permute-done = f32[8,5,26,1536]{3,0,2,1:T(8,128)S(1)} collective-permute-done((f32[8,5,26,1536]{3,0,2,1:T(8,128)S(1)}, f32[8,5,26,1536]{3,0,2,1:T(8,128)S(1)}, u32[]{:S(2)}, u32[]{:S(2)}) %collective-permute-start) | collective-permute-done | bytes 6389792 | tf_op jit(solution)/shard_map/ppermute | solution.py:186
  541.7 2.7 copy-done.3
  544.4 6.5 %fusion.3 = bf16[8,5,26,1536]{3,0,2,1:T(8,128)(2,1)S(1)} fusion(f32[8,5,26,1536]{3,0,2,1:T(8,128)} %copy-done.3, f32[5,1536,1,8,26]{1,4,3,2,0:T(8,128)S(1)} %copy-done.2), kind=kLoop, calls=%fused_computation.9 | loop fusion | flops 3194880 | bytes 15974400 | tf_op jit(solution)/shard_map/convert_element_type | solution.py:187
  550.9 3.1 copy.215
  554.0 6.8 %all-to-all-start.1 = ((bf16[8,5,26,1536]{3,2,1,0:T(8,128)(2,1)}), bf16[8,5,26,1536]{3,2,1,0:T(8,128)(2,1)}, u32[]{:S(2)}, u32[]{:S(2)}) async-start(bf16[8,5,26,1536]{3,2,1,0:T(8,128)(2,1)} %copy.215), calls=%async_computation.1 | async-start | bytes 7864320 | tf_op jit(solution)/shard_map/all_to_all | solution.py:188
  561.0 56.3 %all-to-all-done.1 = bf16[8,5,26,1536]{3,2,1,0:T(8,128)(2,1)} async-done(((bf16[8,5,26,1536]{3,2,1,0:T(8,128)(2,1)}), bf16[8,5,26,1536]{3,2,1,0:T(8,128)(2,1)}, u32[]{:S(2)}, u32[]{:S(2)}) %all-to-all-start.1) | async-done | bytes 3194912 | tf_op jit(solution)/shard_map/all_to_all | solution.py:188
  617.2 6.1 reshape.869
  623.4 10.7 %gather_fusion.1 = f32[1024,1536]{1,0:T(8,128)} fusion(f32[1040,1536]{1,0:T(8,128)} %reshape.869, s32[1024]{0:T(1024)S(1)} %broadcast_clamp_fusion), kind=kCustom, calls=%fused_computation.1 | custom fusion | bytes 12587008 | tf_op jit(solution)/shard_map/gather | solution.py:190
  634.1 5.1 fusion.4
  (253 shorter events, 46.1 us)
Async XLA Ops:
  7.2 16.1 %copy-start.4 = (bf16[128,1536]{1,0:T(8,128)(2,1)S(1)}, bf16[128,1536]{1,0:T(8,128)(2,1)}, u32[]{:S(2)}) copy-start(bf16[128,1536]{1,0:T(8,128)(2,1)} %param.13) | copy-start | bytes 1179652
  7.2 8.2 %copy-start.69 = (bf16[1536]{0:T(1024)(128)(2,1)S(1)}, bf16[1536]{0:T(1024)(128)(2,1)}, u32[]{:S(2)}) copy-start(bf16[1536]{0:T(1024)(128)(2,1)} %param.21) | copy-start | bytes 9220
  7.2 8.8 %copy-start.62 = (s32[128,8]{0,1:T(8,128)S(1)}, s32[128,8]{0,1:T(8,128)}, u32[]{:S(2)}) copy-start(s32[128,8]{0,1:T(8,128)} %param.22) | copy-start | bytes 12292
  7.2 50.5 %all-gather.17.cloned.1.call-start = ((), (), s32[]{:S(2)}) async-start(), calls=%async_computation.5 | async-start | bytes 3244032 | tf_op jit(solution)/shard_map/all_gather | solution.py:99
  7.9 104.8 %all-gather.11.cloned.1.call-start = ((), (), s32[]{:S(2)}) async-start(), calls=%async_computation.2 | async-start | bytes 8650752 | tf_op jit(solution)/shard_map/all_gather | solution.py:131
  17.0 4.3 copy-start.63
  66.7 9.3 %copy-start.66 = (pred[512]{0:T(512)(128)(4,1)S(1)}, pred[512]{0:T(512)(128)(4,1)}, u32[]{:S(2)}) copy-start(pred[512]{0:T(512)(128)(4,1)} %broadcast_compare_fusion.8) | copy-start | bytes 1540
  137.1 4.9 copy-start.12
  137.1 4.9 copy-start.22
  137.1 6.2 copy-start.11
  142.1 24.8 %copy-start.33 = (f32[8,3,128]{2,1,0:T(4,128)}, f32[8,3,128]{2,1,0:T(4,128)S(1)}, u32[]{:S(2)}) copy-start(f32[8,3,128]{2,1,0:T(4,128)S(1)} %get-tuple-element.82) | copy-start | bytes 36868
  142.1 5.1 copy-start.10
  142.1 5.1 copy-start.13
  143.4 23.5 %copy-start.35 = (f32[8,3,128]{2,1,0:T(4,128)}, f32[8,3,128]{2,1,0:T(4,128)S(1)}, u32[]{:S(2)}) copy-start(f32[8,3,128]{2,1,0:T(4,128)S(1)} %get-tuple-element.86) | copy-start | bytes 36868
  143.4 7.6 %copy-start.9 = (bf16[512,512]{0,1:T(8,128)(2,1)S(1)}, bf16[512,512]{0,1:T(8,128)(2,1)}, u32[]{:S(2)}) copy-start(bf16[512,512]{0,1:T(8,128)(2,1)} %copy.195) | copy-start | bytes 1572868
  143.4 7.6 %copy-start.15 = (pred[128,512]{1,0:T(8,128)(4,1)S(1)}, pred[128,512]{1,0:T(8,128)(4,1)}, u32[]{:S(2)}) copy-start(pred[128,512]{1,0:T(8,128)(4,1)} %get-tuple-element.67) | copy-start | bytes 196612
  147.2 19.7 %copy-start.38 = (f32[8,3,128]{2,1,0:T(4,128)}, f32[8,3,128]{2,1,0:T(4,128)S(1)}, u32[]{:S(2)}) copy-start(f32[8,3,128]{2,1,0:T(4,128)S(1)} %get-tuple-element.74) | copy-start | bytes 36868
  147.2 7.6 %copy-start.8 = (bf16[512,512]{0,1:T(8,128)(2,1)S(1)}, bf16[512,512]{0,1:T(8,128)(2,1)}, u32[]{:S(2)}) copy-start(bf16[512,512]{0,1:T(8,128)(2,1)} %copy.192) | copy-start | bytes 1572868
  147.2 7.6 %copy-start.17 = (pred[128,512]{1,0:T(8,128)(4,1)S(1)}, pred[128,512]{1,0:T(8,128)(4,1)}, u32[]{:S(2)}) copy-start(pred[128,512]{1,0:T(8,128)(4,1)} %get-tuple-element.66) | copy-start | bytes 196612
  151.0 15.9 %copy-start.40 = (f32[8,3,128]{2,1,0:T(4,128)}, f32[8,3,128]{2,1,0:T(4,128)S(1)}, u32[]{:S(2)}) copy-start(f32[8,3,128]{2,1,0:T(4,128)S(1)} %get-tuple-element.76) | copy-start | bytes 36868
  151.0 7.6 %copy-start.7 = (bf16[512,512]{0,1:T(8,128)(2,1)S(1)}, bf16[512,512]{0,1:T(8,128)(2,1)}, u32[]{:S(2)}) copy-start(bf16[512,512]{0,1:T(8,128)(2,1)} %copy.186) | copy-start | bytes 1572868
  151.0 7.6 %copy-start.20 = (pred[128,512]{1,0:T(8,128)(4,1)S(1)}, pred[128,512]{1,0:T(8,128)(4,1)}, u32[]{:S(2)}) copy-start(pred[128,512]{1,0:T(8,128)(4,1)} %get-tuple-element.71) | copy-start | bytes 196612
  154.8 12.1 %copy-start.42 = (f32[8,3,128]{2,1,0:T(4,128)}, f32[8,3,128]{2,1,0:T(4,128)S(1)}, u32[]{:S(2)}) copy-start(f32[8,3,128]{2,1,0:T(4,128)S(1)} %get-tuple-element.78) | copy-start | bytes 36868
  154.8 7.6 %copy-start.6 = (bf16[512,512]{0,1:T(8,128)(2,1)S(1)}, bf16[512,512]{0,1:T(8,128)(2,1)}, u32[]{:S(2)}) copy-start(bf16[512,512]{0,1:T(8,128)(2,1)} %copy.204) | copy-start | bytes 1572868
  158.6 7.6 %copy-start.31 = (f32[8,3,128]{2,1,0:T(4,128)S(1)}, f32[8,3,128]{2,1,0:T(4,128)}, u32[]{:S(2)}) copy-start(f32[8,3,128]{2,1,0:T(4,128)} %get-tuple-element.90) | copy-start | bytes 36868
  158.6 7.6 %copy-start.46 = (f32[8,3,128]{2,1,0:T(4,128)S(1)}, f32[8,3,128]{2,1,0:T(4,128)}, u32[]{:S(2)}) copy-start(f32[8,3,128]{2,1,0:T(4,128)} %get-tuple-element.88) | copy-start | bytes 36868
  162.4 8.1 %copy-start.26 = (bf16[512,512]{0,1:T(8,128)(2,1)S(1)}, bf16[512,512]{0,1:T(8,128)(2,1)}, u32[]{:S(2)}) copy-start(bf16[512,512]{0,1:T(8,128)(2,1)} %copy.185) | copy-start | bytes 1572868
  166.2 4.3 copy-start.44
  167.6 77.9 %copy-start.52 = (f32[8,3,128]{2,1,0:T(4,128)}, f32[8,3,128]{2,1,0:T(4,128)S(1)}, u32[]{:S(2)}) copy-start(f32[8,3,128]{2,1,0:T(4,128)S(1)} %get-tuple-element.61) | copy-start | bytes 36868
  170.6 4.8 copy-start.21
  175.3 4.5 copy-start.27
  179.9 7.5 %copy-start.19 = (pred[128,512]{1,0:T(8,128)(4,1)S(1)}, pred[128,512]{1,0:T(8,128)(4,1)}, u32[]{:S(2)}) copy-start(pred[128,512]{1,0:T(8,128)(4,1)} %get-tuple-element.65) | copy-start | bytes 196612
  187.3 4.5 copy-start.28
  191.8 6.4 copy-start.18
  198.3 4.5 copy-start.29
  202.8 5.6 copy-start.16
  213.0 5.6 copy-start.14
  237.5 14.2 %slice-start = ((s8[6291456]{0:T(1024)(128)(4,1)}), s8[4194304]{0:T(1024)(128)(4,1)S(1)}, s32[]{:S(2)}) async-start(s8[6291456]{0:T(1024)(128)(4,1)} %bitcast.638), calls=%async_computation.8 | async-start | bytes 8388608
  241.5 8.3 %slice-start.2 = ((s8[6291456]{0:T(1024)(128)(4,1)}), s8[4194304]{0:T(1024)(128)(4,1)S(1)}, s32[]{:S(2)}) async-start(s8[6291456]{0:T(1024)(128)(4,1)} %bitcast.640), calls=%async_computation.10 | async-start | bytes 8388608
  241.5 4.0 copy-start.68
  241.5 8.3 %slice-start.3 = ((s8[6291456]{0:T(1024)(128)(4,1)}), s8[2097152]{0:T(1024)(128)(4,1)S(1)}, s32[]{:S(2)}) async-start(s8[6291456]{0:T(1024)(128)(4,1)} %bitcast.640), calls=%async_computation.11 | async-start | bytes 4194304
  241.5 10.2 %slice-start.1 = ((s8[6291456]{0:T(1024)(128)(4,1)}), s8[2097152]{0:T(1024)(128)(4,1)S(1)}, s32[]{:S(2)}) async-start(s8[6291456]{0:T(1024)(128)(4,1)} %bitcast.638), calls=%async_computation.9 | async-start | bytes 4194304
  245.5 4.3 copy-start.48
  245.5 4.3 copy-start.67
  245.5 6.2 copy-start.47
  245.5 6.2 copy-start.65
  245.5 8.2 %slice-start.4 = ((s8[6291456]{0:T(1024)(128)(4,1)}), s8[4194304]{0:T(1024)(128)(4,1)S(1)}, s32[]{:S(2)}) async-start(s8[6291456]{0:T(1024)(128)(4,1)} %bitcast.642), calls=%async_computation.12 | async-start | bytes 8388608
  249.8 3.9 slice-start.5
  249.8 3.9 copy-start.25
  249.9 3.9 copy-start.53
  255.9 4.9 slice-start.6
  261.7 377.4 %copy-start.5 = (bf16[128,1536]{1,0:T(8,128)(2,1)}, bf16[128,1536]{1,0:T(8,128)(2,1)S(1)}, u32[]{:S(2)}) copy-start(bf16[128,1536]{1,0:T(8,128)(2,1)S(1)} %get-tuple-element.95) | copy-start | bytes 1179652
  272.6 61.6 %all-to-all-start = ((bf16[8,5,26,1536]{3,2,1,0:T(8,128)(2,1)}), bf16[8,5,26,1536]{3,2,1,0:T(8,128)(2,1)}, u32[]{:S(2)}, u32[]{:S(2)}) async-start(bf16[8,5,26,1536]{3,2,1,0:T(8,128)(2,1)} %reshape.871), calls=%async_computation | async-start | bytes 7864320 | tf_op jit(solution)/shard_map/all_to_all | solution.py:172
  277.7 65.3 %all-gather.19.cloned.1.call-start = ((), (), s32[]{:S(2)}) async-start(), calls=%async_computation.6 | async-start | bytes 2949120 | tf_op jit(solution)/shard_map/all_gather | solution.py:134
  278.4 87.6 %all-gather.21.cloned.1.call-start = ((), (), s32[]{:S(2)}) async-start(), calls=%async_computation.7 | async-start | bytes 9584640 | tf_op jit(solution)/shard_map/all_gather | solution.py:173
  339.8 6.2 copy-start.30
  339.9 107.7 %all-gather.15.cloned.1.call-start = ((), (), s32[]{:S(2)}) async-start(), calls=%async_computation.4 | async-start | bytes 9830400 | tf_op jit(solution)/shard_map/all_gather | solution.py:134
  346.0 150.1 %all-gather.13.cloned.1.call-start = ((), (), s32[]{:S(2)}) async-start(), calls=%async_computation.3 | async-start | bytes 4915200 | tf_op jit(solution)/shard_map/all_gather | solution.py:135
  524.1 20.3 %copy-start.2 = (f32[5,1536,1,8,26]{1,4,3,2,0:T(8,128)S(1)}, f32[5,1536,1,8,26]{1,4,3,2,0:T(8,128)}, u32[]{:S(2)}) copy-start(f32[5,1536,1,8,26]{1,4,3,2,0:T(8,128)} %get-tuple-element.31) | copy-start | bytes 19169284
  531.1 10.6 %collective-permute-start = (f32[8,5,26,1536]{3,0,2,1:T(8,128)S(1)}, f32[8,5,26,1536]{3,0,2,1:T(8,128)S(1)}, u32[]{:S(2)}, u32[]{:S(2)}) collective-permute-start(f32[8,5,26,1536]{3,0,2,1:T(8,128)S(1)} %copy.214), channel_id=1, source_target_pairs={{0,1},{1,0},{2,3},{3,2},{4,5},{5,4},{6,7},{7,6},{8,9},{9,8},{10,11... | collective-permute-start | bytes 19169288 | tf_op jit(solution)/shard_map/ppermute | solution.py:186
  550.9 10.0 %copy-start.70 = (bf16[128,8]{0,1:T(8,128)(2,1)S(1)}, bf16[128,8]{0,1:T(8,128)(2,1)}, u32[]{:S(2)}) copy-start(bf16[128,8]{0,1:T(8,128)(2,1)} %param.23) | copy-start | bytes 6148
  550.9 10.1 %copy-start.64 = (s32[1024,1]{0,1:T(1,128)S(1)}, s32[1024,1]{0,1:T(1,128)}, u32[]{:S(2)}) copy-start(s32[1024,1]{0,1:T(1,128)} %copy-done.63) | copy-start | bytes 12292
  554.0 63.2 %all-to-all-start.1 = ((bf16[8,5,26,1536]{3,2,1,0:T(8,128)(2,1)}), bf16[8,5,26,1536]{3,2,1,0:T(8,128)(2,1)}, u32[]{:S(2)}, u32[]{:S(2)}) async-start(bf16[8,5,26,1536]{3,2,1,0:T(8,128)(2,1)} %copy.215), calls=%async_computation.1 | async-start | bytes 7864320 | tf_op jit(solution)/shard_map/all_to_all | solution.py:188
  623.4 16.6 %copy-start.1 = (bf16[1536,512]{1,0:T(8,128)(2,1)S(1)}, bf16[1536,512]{1,0:T(8,128)(2,1)}, u32[]{:S(2)}) copy-start(bf16[1536,512]{1,0:T(8,128)(2,1)} %param.16) | copy-start | bytes 4718596
  (31 other events, 64.1 us)
Sparse Core Ops, SparseCore 0:
  10.3 47.4 all-gather.16
  60.6 52.1 all-gather.10
  280.1 62.8 all-gather.18
  344.5 21.4 all-gather.20
  367.5 80.0 all-gather.14
  449.1 46.8 all-gather.12

commit v4 on v3

--- a/solution.py
+++ b/solution.py
@@ -3,10 +3,10 @@
 from jax import lax
 from jax.sharding import Mesh, PartitionSpec as P
 
+
 HEAD_DIM = 64
 EXPERTS = 40
 TOPK = 8
-PIECES = 4
 MOST = 26
 
 
@@ -65,6 +65,32 @@
         preferred_element_type=jnp.float32,
     )
     return (new_max, new_sum, new_acc)
+
+
+def spread_pieces(local, width_axis):
+    req_count = lax.axis_size("req")
+    pair = lax.axis_size("zlo")
+    stacked = []
+    for dz in range(pair):
+        chunks = []
+        for dr in range(req_count):
+            if dr == 0 and dz == 0:
+                chunks.append(local)
+                continue
+            perm = [
+                (a * pair + z, ((a + dr) % req_count) * pair + (z + dz) % pair)
+                for a in range(req_count)
+                for z in range(pair)
+            ]
+            chunks.append(lax.ppermute(local, ("req", "zlo"), perm))
+        stacked.append(jnp.concatenate(chunks, axis=width_axis))
+    return jnp.stack(stacked, axis=0)
+
+
+def in_chunk_order(rows, chunk_order):
+    count = chunk_order.shape[0]
+    shaped = rows.reshape(rows.shape[0], count, rows.shape[1] // count)
+    return jnp.take(shaped, chunk_order, axis=1).reshape(rows.shape)
 
 
 def shards(
@@ -95,8 +121,11 @@
     ) * lax.axis_size("core") + core
     length = cache_len[0]
     cache_rows = cache_kv[0]
-    cache_count = cache_rows.shape[0]
     cache_all = lax.all_gather(cache_rows, EXP_AXES, axis=0, tiled=True)
+    gate_up_full = spread_pieces(w_gate_up[0], 1)
+    down_full = spread_pieces(w_down[0], 2)
+    req_index = lax.axis_index("req")
+    chunk_order = (req_index - jnp.arange(lax.axis_size("req"), dtype=jnp.int32)) % lax.axis_size("req")
     normed = rms_scale(hidden_in, attn_gain)
     query_pos = position_exp * rows_here + jnp.arange(rows_here, dtype=jnp.int32)
     positions = length + query_pos
@@ -119,21 +148,16 @@
     )
     running = initial
     for offset in range(0, cache_all.shape[0], key_block):
-        block_size = min(key_block, cache_all.shape[0] - offset)
-        cache_pos = offset + jnp.arange(block_size, dtype=jnp.int32)
-        running = attend_block(
-            running,
-            queries,
-            cache_all[offset : offset + block_size],
-            jnp.broadcast_to((cache_pos < length)[None, :], (rows_here, block_size)),
-            kv_width,
-        )
+      block_size = min(key_block, cache_all.shape[0] - offset)
+      cache_pos = offset + jnp.arange(block_size, dtype=jnp.int32)
+      running = attend_block(
+          running,
+          queries,
+          cache_all[offset : offset + block_size],
+          jnp.broadcast_to((cache_pos < length)[None, :], (rows_here, block_size)),
+          kv_width,
+      )
     new_all = lax.all_gather(new_kv, EXP_AXES, axis=0, tiled=True)
-    gate_up_local, down_local, new_all = lax.optimization_barrier((w_gate_up[0], w_down[0], new_all))
-    gate_up_full, down_full = (
-        lax.all_gather(lax.all_gather(gate_up_local, "zlo", axis=0), "req", axis=2, tiled=True),
-        lax.all_gather(lax.all_gather(down_local, "zlo", axis=0), "req", axis=3, tiled=True),
-    )
     for offset in range(0, new_all.shape[0], key_block):
         block_size = min(key_block, new_all.shape[0] - offset)
         new_pos = offset + jnp.arange(block_size, dtype=jnp.int32)
@@ -144,7 +168,7 @@
             new_pos[None, :] <= query_pos[:, None],
             kv_width,
         )
-    run_max, run_sum, run_acc = running
+    _, run_sum, run_acc = running
     context = (
         (run_acc / run_sum[..., None])
         .transpose(2, 0, 1, 3)
@@ -154,6 +178,7 @@
     projected = jnp.dot(context, w_out, preferred_element_type=jnp.float32)
     attended = (hidden_in.astype(jnp.float32) + residual_scale * projected).astype(jnp.bfloat16)
     moe_in = rms_scale(attended, moe_gain)
+    moe_in = in_chunk_order(moe_in, chunk_order)
     block_experts = gate_up_full.shape[1]
     slice_width = down_full.shape[2]
     flat_ids = expert_ids.reshape(-1)
@@ -188,7 +213,7 @@
     returned = lax.all_to_all(computed, ("x", "zhi"), split_axis=0, concat_axis=0, tiled=True)
     summed = returned.astype(jnp.float32).reshape(EXPERTS * MOST, width)
     picked = summed[slot_index] * expert_weights.reshape(-1).astype(jnp.float32)[:, None]
-    mixture = jnp.sum(picked.reshape(rows_here, TOPK, width), axis=1)
+    mixture = in_chunk_order(jnp.sum(picked.reshape(rows_here, TOPK, width), axis=1), chunk_order)
     layer_out = (attended.astype(jnp.float32) + residual_scale * mixture).astype(jnp.bfloat16)
     return (attended, layer_out)
 
@@ -214,4 +239,5 @@
         P(cols, None, None, "req"),
     )
     out_specs = (P(rows, None), P(rows, None))
+
     return jax.shard_map(shards, mesh=mesh, in_specs=in_specs, out_specs=out_specs, check_vma=False)

time: 657 us -> 709 us (1.079)
  blocking collectives: 14.3 us -> 53.2 us
  waiting for transfers between devices: 302 us -> 277 us
  starting transfers between devices: 12.4 us -> 32.4 us
  other arithmetic: 61.1 us -> 74.4 us
    ppermute x0 -> x14, waiting for transfers between devices: none -> 150 us  [spread_pieces(): chunks.append(lax.ppermute(local, ('req', 'zlo'), perm))]
    all_gather x3 -> x0, waiting for transfers between devices: 111 us -> none  [the longest x1 71.9 us: shards(): lax.all_gather(lax.all_gather(gate_up_local, 'zlo', axis=0), 'req', axis=...]
    all_to_all x1 -> x0, waiting for transfers between devices: 55.8 us -> none  [shards(): lax.all_to_all(outgoing, ('x', 'zhi'), split_axis=0, concat_axis=0, tiled...]
    all_to_all x0 -> x1, blocking collectives: none -> 53.2 us  [shards(): lax.all_to_all(outgoing, ('x', 'zhi'), split_axis=0, concat_axis=0, tiled...]
    ppermute x0 -> x14, starting transfers between devices: none -> 24.6 us  [spread_pieces(): chunks.append(lax.ppermute(local, ('req', 'zlo'), perm))]
    all_gather x1 -> x0, blocking collectives: 14.3 us -> none  [shards(): lax.all_gather(down_local, 'zlo', axis=0)]
    another operation x2 -> x6, other arithmetic: 0.15 us -> 12.7 us  [the longest x4 12.6 us: spread_pieces(): return jnp.stack(stacked, axis=0)]
  transfers between devices with their start and end apart: 9 -> 19, of which waited for: 9 -> 10; matrix products, arithmetic and copies ran while one was open for 11% -> 8% of each run, Pallas kernels for 0% -> 0%
where the time goes in v4:
time: 709 us; the launch traced here: 698 us
  waiting for transfers between devices  277 us (39%)
  matrix products  123 us (17%)
  local copies, waits for them, and re-layouts  121 us (17%)
  other arithmetic  74.4 us (10%)
  blocking collectives  53.2 us (8%)
  starting transfers between devices  32.4 us (5%)
  between operations  15.9 us (2%)
    ppermute x14, waiting for transfers between devices, spread_pieces(): chunks.append(lax.ppermute(local, ('req', 'zlo'), perm))  150 us
    all_to_all x1, waiting for transfers between devices, shards(): lax.all_to_all(computed, ('x', 'zhi'), split_axis=0, concat_axis=0, tiled...  56.3 us
    all_to_all x1, blocking collectives, shards(): lax.all_to_all(outgoing, ('x', 'zhi'), split_axis=0, concat_axis=0, tiled...  53.2 us
    dot_general x11, matrix products, attend_block(): jnp.einsum('kgtr,rkd->kgtd', weights.astype(jnp.bfloat16), value_heads, p...  44.4 us
    dot_general x11, matrix products, attend_block(): jnp.einsum('tkgd,rkd->kgtr', queries, key_heads, preferred_element_type=j...  42.4 us
    reduce_sum x11, other arithmetic, attend_block(): new_sum = run_sum * factor + jnp.sum(weights, axis=-1)  40.9 us
    all_gather x1, waiting for transfers between devices, shards(): new_all = lax.all_gather(new_kv, EXP_AXES, axis=0, tiled=True)  32.4 us
    all_gather x1, waiting for transfers between devices, shards(): cache_all = lax.all_gather(cache_rows, EXP_AXES, axis=0, tiled=True)  27.6 us
  transfers between devices with their start and end apart: 19, of which 10 were waited for; matrix products, arithmetic and copies ran while one was open for 8% of the time, Pallas kernels for 0%

profile of v4, /device:TPU:0, one launch (start us, length us, event | category | flops | bytes accessed | tf_op | source)
XLA Modules:
  0.0 697.8 jit_solution(1682775176977182396)
XLA Ops:
  17.7 4.3 scatter_custom_fusion
  24.6 4.3 fusion.259
  30.1 27.6 %all-gather.8.cloned.1.call-done = bf16[1,1536,1024]{2,1,0:T(8,128)(2,1)} async-done(((bf16[1,48,1024]{2,1,0:T(8,128)(2,1)}), bf16[1,1536,1024]{2,1,0:T(8,128)(2,1)}) %all-gather.8.cloned.1.call-update) | async-done | bytes 3145744 | tf_op jit(solution)/shard_map/all_gather | solution.py:124
  57.7 3.2 fusion.265
  66.7 4.4 bitcast_reduce_fusion.2
  71.1 5.0 bitcast_reduce_fusion
  76.0 4.3 bitcast_reduce_fusion.1
  80.3 32.4 %all-gather.6.cloned.1.call-done = bf16[4096,1024]{1,0:T(8,128)(2,1)} async-done(((bf16[128,1024]{1,0:T(8,128)(2,1)}), bf16[4096,1024]{1,0:T(8,128)(2,1)}) %all-gather.6.cloned.1.call-update) | async-done | bytes 8388624 | tf_op jit(solution)/shard_map/all_gather | solution.py:160
  112.7 6.0 fusion.264
  137.2 4.9 fusion.14
  143.5 3.8 fusion.18
  147.3 3.8 fusion.17
  151.1 3.8 fusion.16
  154.8 3.8 fusion.15
  158.6 3.8 fusion.13
  162.4 3.7 fusion.19
  167.5 2.8 fusion.20
  170.3 2.8 fusion.94
  175.1 4.5 fusion.22
  179.6 5.5 fusion.97
  187.2 4.5 fusion.24
  191.7 5.4 fusion.100
  198.1 4.5 fusion.26
  202.6 5.4 fusion.103
  208.3 4.8 fusion.28
  213.1 5.4 fusion.106
  218.7 3.9 fusion.30
  222.6 5.3 fusion.109
  228.1 3.9 fusion.32
  232.0 5.3 fusion.112
  237.5 4.0 fusion.34
  241.6 3.9 fusion.115
  245.6 4.3 fusion.36
  262.9 5.2 gather_fusion.1
  268.1 5.5 reshape.947
  273.6 53.2 %all_to_all.10 = bf16[8,5,26,1536]{3,2,1,0:T(8,128)(2,1)S(1)} all-to-all(bf16[8,5,26,1536]{3,2,1,0:T(8,128)(2,1)} %reshape.947), channel_id=1, replica_groups=mesh['req'=4,'x'=4,'zhi'=2,'zlo'=2,'core'=2] {'x','zhi'}, dimensions={0} | all-to-all | bytes 6389760 | tf_op jit(solution)/shard_map/all_to_all | solution.py:197
  326.8 3.5 copy.269
  333.4 2.6 collective-permute-start.5
  336.0 2.5 collective-permute-start.6
  339.1 34.5 %collective-permute-done.3 = bf16[5,128,384]{2,1,0:T(8,128)(2,1)S(1)} collective-permute-done((bf16[5,128,384]{2,1,0:T(8,128)(2,1)S(1)}, bf16[5,128,384]{2,1,0:T(8,128)(2,1)S(1)}, u32[]{:S(2)}, u32[]{:S(2)}) %collective-permute-start.3) | collective-permute-done | bytes 491552 | tf_op jit(solution)/shard_map/ppermute | solution.py:85
  373.6 3.6 collective-permute-start
  380.2 42.9 %collective-permute-done = bf16[5,128,384]{2,1,0:T(8,128)(2,1)S(1)} collective-permute-done((bf16[5,128,384]{2,1,0:T(8,128)(2,1)S(1)}, bf16[5,128,384]{2,1,0:T(8,128)(2,1)S(1)}, u32[]{:S(2)}, u32[]{:S(2)}) %collective-permute-start) | collective-permute-done | bytes 491552 | tf_op jit(solution)/shard_map/ppermute | solution.py:85
  424.1 8.7 %collective-permute-done.1 = bf16[5,128,384]{2,1,0:T(8,128)(2,1)} collective-permute-done((bf16[5,128,384]{2,1,0:T(8,128)(2,1)S(1)}, bf16[5,128,384]{2,1,0:T(8,128)(2,1)}, u32[]{:S(2)}, u32[]{:S(2)}) %collective-permute-start.1) | collective-permute-done | bytes 491552 | tf_op jit(solution)/shard_map/ppermute | solution.py:85
  432.9 5.6 collective-permute-start.12
  438.5 3.4 collective-permute-start.13
  442.0 2.8 maximum_bitcast_fusion.8
  444.8 3.0 maximum_bitcast_fusion.9
  447.7 29.2 %collective-permute-done.9 = bf16[5,384,256]{2,1,0:T(8,128)(2,1)} collective-permute-done((bf16[5,384,256]{2,1,0:T(8,128)(2,1)S(1)}, bf16[5,384,256]{2,1,0:T(8,128)(2,1)}, u32[]{:S(2)}, u32[]{:S(2)}) %collective-permute-start.9) | collective-permute-done | bytes 983072 | tf_op jit(solution)/shard_map/ppermute | solution.py:85
  476.9 4.5 maximum_bitcast_fusion.4
  481.4 33.7 %collective-permute-done.10 = bf16[5,384,256]{2,1,0:T(8,128)(2,1)S(1)} collective-permute-done((bf16[5,384,256]{2,1,0:T(8,128)(2,1)S(1)}, bf16[5,384,256]{2,1,0:T(8,128)(2,1)S(1)}, u32[]{:S(2)}, u32[]{:S(2)}) %collective-permute-start.10) | collective-permute-done | bytes 983072 | tf_op jit(solution)/shard_map/ppermute | solution.py:85
  518.4 9.8 %copy.270 = bf16[16,5,26,1536]{3,2,0,1:T(8,128)(2,1)} copy(bf16[16,5,26,1536]{3,0,2,1:T(8,128)(2,1)} %all-gather.10.cloned.1.call-done) | data formatting | bytes 12779520 | tf_op jit(solution)/shard_map/all_gather | solution.py:198
  528.1 12.1 %fusion.82 = f32[2,8,2,5,26,256]{5,4,1,0,2,3:T(8,128)} fusion(bf16[2,8,5,26,1536,1]{4,3,1,0,5,2:T(8,128)(2,1)} %bitcast.665, bf16[1,5,1536,256]{3,2,0,1:T(8,128)(2,1)} %maximum_bitcast_fusion.5, bf16[1,5,1536,256]{3,2,0,1:T(8,128)(2,1)} %maximum_bitcast_fusion.4), kind=kOutput, calls=%fused_computation.112 | convolution fusion | flops 3287285760 | bytes 18513920 | tf_op jit(solution)/shard_map/askmd,pkdf->aspkmf/dot_general | solution.py:199
  540.2 14.8 %convert_reduce_fusion = f32[5,1536,2,8,26]{1,4,3,2,0:T(8,128)} fusion(bf16[1,5,128,1536]{3,2,1,0:T(8,128)(2,1)} %maximum_bitcast_fusion.9, bf16[1,5,128,1536]{3,2,1,0:T(8,128)(2,1)} %maximum_bitcast_fusion.8, f32[2,8,2,5,26,256]{5,4,1,0,2,3:T(8,128)} %fusion.82), kind=kOutput, calls=%fused_computation.5 | convolution fusion | flops 1662812160 | bytes 20971520 | tf_op jit(solution)/shard_map/aspkmf,pkfd->aspkmd/dot_general | solution.py:205
  555.1 14.1 %constant_dynamic-slice_fusion = (f32[5,1536,1,8,26]{1,4,3,2,0:T(8,128)}, f32[8,5,26,1536]{3,2,0,1:T(8,128)}) fusion(f32[5,1536,2,8,26]{1,4,3,2,0:T(8,128)} %convert_reduce_fusion, s32[]{:T(128)S(6)} %select_n.188, s32[]{:T(128)S(6)} %select_n.189), kind=kLoop, calls=%fused_computation.273 | loop fusion | bytes 25559048 | tf_op jit(solution)/shard_map/dynamic-slice
  569.2 7.0 %copy.273 = f32[8,5,26,1536]{3,0,2,1:T(8,128)S(1)} copy(f32[8,5,26,1536]{3,2,0,1:T(8,128)} %get-tuple-element.26) | data formatting | bytes 12779520 | tf_op jit(solution)/shard_map/jit(dynamic_index_in_dim)/squeeze | solution.py:210
  576.5 10.3 %collective-permute-done.14 = f32[8,5,26,1536]{3,0,2,1:T(8,128)S(1)} collective-permute-done((f32[8,5,26,1536]{3,0,2,1:T(8,128)S(1)}, f32[8,5,26,1536]{3,0,2,1:T(8,128)S(1)}, u32[]{:S(2)}, u32[]{:S(2)}) %collective-permute-start.14) | collective-permute-done | bytes 6389792 | tf_op jit(solution)/shard_map/ppermute | solution.py:211
  586.7 2.7 copy-done.3
  589.5 6.5 fusion.4
  596.0 3.1 copy.274
  599.1 7.4 %all-to-all-start.1 = ((bf16[8,5,26,1536]{3,2,1,0:T(8,128)(2,1)}), bf16[8,5,26,1536]{3,2,1,0:T(8,128)(2,1)}, u32[]{:S(2)}, u32[]{:S(2)}) async-start(bf16[8,5,26,1536]{3,2,1,0:T(8,128)(2,1)} %copy.274), calls=%async_computation.1 | async-start | bytes 7864320 | tf_op jit(solution)/shard_map/all_to_all | solution.py:213
  606.6 56.3 %all-to-all-done.1 = bf16[8,5,26,1536]{3,2,1,0:T(8,128)(2,1)} async-done(((bf16[8,5,26,1536]{3,2,1,0:T(8,128)(2,1)}), bf16[8,5,26,1536]{3,2,1,0:T(8,128)(2,1)}, u32[]{:S(2)}, u32[]{:S(2)}) %all-to-all-start.1) | async-done | bytes 3194912 | tf_op jit(solution)/shard_map/all_to_all | solution.py:213
  662.9 6.2 reshape.937
  669.1 10.7 %gather_fusion.2 = f32[1024,1536]{1,0:T(8,128)} fusion(f32[1040,1536]{1,0:T(8,128)} %reshape.937, s32[1024]{0:T(1024)S(1)} %broadcast_clamp_fusion), kind=kCustom, calls=%fused_computation.2 | custom fusion | bytes 12587008 | tf_op jit(solution)/shard_map/gather | solution.py:215
  679.7 5.0 fusion.5
  (300 shorter events, 76.5 us)
Async XLA Ops:
  7.2 17.4 %copy-start.4 = (bf16[128,1536]{1,0:T(8,128)(2,1)S(1)}, bf16[128,1536]{1,0:T(8,128)(2,1)}, u32[]{:S(2)}) copy-start(bf16[128,1536]{1,0:T(8,128)(2,1)} %param.13) | copy-start | bytes 1179652
  7.2 8.2 %copy-start.76 = (bf16[1536]{0:T(1024)(128)(2,1)S(1)}, bf16[1536]{0:T(1024)(128)(2,1)}, u32[]{:S(2)}) copy-start(bf16[1536]{0:T(1024)(128)(2,1)} %param.21) | copy-start | bytes 9220
  7.2 9.5 %copy-start.69 = (s32[128,8]{0,1:T(8,128)S(1)}, s32[128,8]{0,1:T(8,128)}, u32[]{:S(2)}) copy-start(s32[128,8]{0,1:T(8,128)} %param.22) | copy-start | bytes 12292
  7.2 50.5 %all-gather.8.cloned.1.call-start = ((), (), s32[]{:S(2)}) async-start(), calls=%async_computation.3 | async-start | bytes 3244032 | tf_op jit(solution)/shard_map/all_gather | solution.py:124
  7.9 104.8 %all-gather.6.cloned.1.call-start = ((), (), s32[]{:S(2)}) async-start(), calls=%async_computation.2 | async-start | bytes 8650752 | tf_op jit(solution)/shard_map/all_gather | solution.py:160
  15.4 503.0 %all-gather.10.cloned.1.call-start = ((), (), s32[]{:S(2)}) async-start(), calls=%async_computation.4 | async-start | bytes 9584640 | tf_op jit(solution)/shard_map/all_gather | solution.py:198
  66.7 9.4 %copy-start.73 = (pred[512]{0:T(512)(128)(4,1)S(1)}, pred[512]{0:T(512)(128)(4,1)}, u32[]{:S(2)}) copy-start(pred[512]{0:T(512)(128)(4,1)} %broadcast_compare_fusion.8) | copy-start | bytes 1540
  137.2 5.0 copy-start.23
  137.2 6.2 copy-start.11
  142.1 24.7 %copy-start.39 = (f32[8,3,128]{2,1,0:T(4,128)}, f32[8,3,128]{2,1,0:T(4,128)S(1)}, u32[]{:S(2)}) copy-start(f32[8,3,128]{2,1,0:T(4,128)S(1)} %get-tuple-element.76) | copy-start | bytes 36868
  142.2 5.1 copy-start.10
  142.2 5.1 copy-start.14
  143.4 23.4 %copy-start.41 = (f32[8,3,128]{2,1,0:T(4,128)}, f32[8,3,128]{2,1,0:T(4,128)S(1)}, u32[]{:S(2)}) copy-start(f32[8,3,128]{2,1,0:T(4,128)S(1)} %get-tuple-element.80) | copy-start | bytes 36868
  143.4 7.6 %copy-start.9 = (bf16[512,512]{0,1:T(8,128)(2,1)S(1)}, bf16[512,512]{0,1:T(8,128)(2,1)}, u32[]{:S(2)}) copy-start(bf16[512,512]{0,1:T(8,128)(2,1)} %copy.252) | copy-start | bytes 1572868
  143.5 7.6 %copy-start.16 = (pred[128,512]{1,0:T(8,128)(4,1)S(1)}, pred[128,512]{1,0:T(8,128)(4,1)}, u32[]{:S(2)}) copy-start(pred[128,512]{1,0:T(8,128)(4,1)} %get-tuple-element.61) | copy-start | bytes 196612
  147.2 19.6 %copy-start.44 = (f32[8,3,128]{2,1,0:T(4,128)}, f32[8,3,128]{2,1,0:T(4,128)S(1)}, u32[]{:S(2)}) copy-start(f32[8,3,128]{2,1,0:T(4,128)S(1)} %get-tuple-element.68) | copy-start | bytes 36868
  147.3 7.6 %copy-start.8 = (bf16[512,512]{0,1:T(8,128)(2,1)S(1)}, bf16[512,512]{0,1:T(8,128)(2,1)}, u32[]{:S(2)}) copy-start(bf16[512,512]{0,1:T(8,128)(2,1)} %copy.249) | copy-start | bytes 1572868
  147.3 7.6 %copy-start.18 = (pred[128,512]{1,0:T(8,128)(4,1)S(1)}, pred[128,512]{1,0:T(8,128)(4,1)}, u32[]{:S(2)}) copy-start(pred[128,512]{1,0:T(8,128)(4,1)} %get-tuple-element.60) | copy-start | bytes 196612
  151.0 15.8 %copy-start.46 = (f32[8,3,128]{2,1,0:T(4,128)}, f32[8,3,128]{2,1,0:T(4,128)S(1)}, u32[]{:S(2)}) copy-start(f32[8,3,128]{2,1,0:T(4,128)S(1)} %get-tuple-element.70) | copy-start | bytes 36868
  151.0 7.6 %copy-start.7 = (bf16[512,512]{0,1:T(8,128)(2,1)S(1)}, bf16[512,512]{0,1:T(8,128)(2,1)}, u32[]{:S(2)}) copy-start(bf16[512,512]{0,1:T(8,128)(2,1)} %copy.243) | copy-start | bytes 1572868
  151.1 7.6 %copy-start.21 = (pred[128,512]{1,0:T(8,128)(4,1)S(1)}, pred[128,512]{1,0:T(8,128)(4,1)}, u32[]{:S(2)}) copy-start(pred[128,512]{1,0:T(8,128)(4,1)} %get-tuple-element.65) | copy-start | bytes 196612
  154.8 12.0 %copy-start.48 = (f32[8,3,128]{2,1,0:T(4,128)}, f32[8,3,128]{2,1,0:T(4,128)S(1)}, u32[]{:S(2)}) copy-start(f32[8,3,128]{2,1,0:T(4,128)S(1)} %get-tuple-element.72) | copy-start | bytes 36868
  154.8 7.6 %copy-start.6 = (bf16[512,512]{0,1:T(8,128)(2,1)S(1)}, bf16[512,512]{0,1:T(8,128)(2,1)}, u32[]{:S(2)}) copy-start(bf16[512,512]{0,1:T(8,128)(2,1)} %copy.261) | copy-start | bytes 1572868
  158.6 7.5 %copy-start.37 = (f32[8,3,128]{2,1,0:T(4,128)S(1)}, f32[8,3,128]{2,1,0:T(4,128)}, u32[]{:S(2)}) copy-start(f32[8,3,128]{2,1,0:T(4,128)} %get-tuple-element.84) | copy-start | bytes 36868
  158.6 7.5 %copy-start.52 = (f32[8,3,128]{2,1,0:T(4,128)S(1)}, f32[8,3,128]{2,1,0:T(4,128)}, u32[]{:S(2)}) copy-start(f32[8,3,128]{2,1,0:T(4,128)} %get-tuple-element.82) | copy-start | bytes 36868
  162.4 7.9 %copy-start.27 = (bf16[512,512]{0,1:T(8,128)(2,1)S(1)}, bf16[512,512]{0,1:T(8,128)(2,1)}, u32[]{:S(2)}) copy-start(bf16[512,512]{0,1:T(8,128)(2,1)} %copy.242) | copy-start | bytes 1572868
  167.5 78.1 %copy-start.58 = (f32[8,3,128]{2,1,0:T(4,128)}, f32[8,3,128]{2,1,0:T(4,128)S(1)}, u32[]{:S(2)}) copy-start(f32[8,3,128]{2,1,0:T(4,128)S(1)} %get-tuple-element.55) | copy-start | bytes 36868
  179.6 7.5 %copy-start.20 = (pred[128,512]{1,0:T(8,128)(4,1)S(1)}, pred[128,512]{1,0:T(8,128)(4,1)}, u32[]{:S(2)}) copy-start(pred[128,512]{1,0:T(8,128)(4,1)} %get-tuple-element.59) | copy-start | bytes 196612
  191.7 6.5 copy-start.19
  202.6 5.6 copy-start.17
  213.1 5.6 copy-start.15
  237.5 14.3 %slice-start = ((s8[6291456]{0:T(1024)(128)(4,1)}), s8[4194304]{0:T(1024)(128)(4,1)S(1)}, s32[]{:S(2)}) async-start(s8[6291456]{0:T(1024)(128)(4,1)} %bitcast.659), calls=%async_computation.5 | async-start | bytes 8388608
  241.5 8.4 %slice-start.2 = ((s8[6291456]{0:T(1024)(128)(4,1)}), s8[4194304]{0:T(1024)(128)(4,1)S(1)}, s32[]{:S(2)}) async-start(s8[6291456]{0:T(1024)(128)(4,1)} %bitcast.661), calls=%async_computation.7 | async-start | bytes 8388608
  241.6 8.4 %slice-start.3 = ((s8[6291456]{0:T(1024)(128)(4,1)}), s8[2097152]{0:T(1024)(128)(4,1)S(1)}, s32[]{:S(2)}) async-start(s8[6291456]{0:T(1024)(128)(4,1)} %bitcast.661), calls=%async_computation.8 | async-start | bytes 4194304
  241.6 10.3 %slice-start.1 = ((s8[6291456]{0:T(1024)(128)(4,1)}), s8[2097152]{0:T(1024)(128)(4,1)S(1)}, s32[]{:S(2)}) async-start(s8[6291456]{0:T(1024)(128)(4,1)} %bitcast.659), calls=%async_computation.6 | async-start | bytes 4194304
  245.6 6.3 copy-start.53
  245.6 6.3 copy-start.72
  245.6 8.2 %slice-start.4 = ((s8[6291456]{0:T(1024)(128)(4,1)}), s8[4194304]{0:T(1024)(128)(4,1)S(1)}, s32[]{:S(2)}) async-start(s8[6291456]{0:T(1024)(128)(4,1)} %bitcast.663), calls=%async_computation.9 | async-start | bytes 8388608
  261.8 428.5 %copy-start.5 = (bf16[128,1536]{1,0:T(8,128)(2,1)}, bf16[128,1536]{1,0:T(8,128)(2,1)S(1)}, u32[]{:S(2)}) copy-start(bf16[128,1536]{1,0:T(8,128)(2,1)S(1)} %get-tuple-element.89) | copy-start | bytes 1179652
  326.8 11.7 %copy-start.13 = (bf16[1,5,384,256]{3,2,1,0:T(8,128)(2,1)S(1)}, bf16[1,5,384,256]{3,2,1,0:T(8,128)(2,1)}, u32[]{:S(2)}) copy-start(bf16[1,5,384,256]{3,2,1,0:T(8,128)(2,1)} %param.24) | copy-start | bytes 2949124
  330.4 43.2 %collective-permute-start.3 = (bf16[5,128,384]{2,1,0:T(8,128)(2,1)S(1)}, bf16[5,128,384]{2,1,0:T(8,128)(2,1)S(1)}, u32[]{:S(2)}, u32[]{:S(2)}) collective-permute-start(bf16[5,128,384]{2,1,0:T(8,128)(2,1)S(1)} %bitcast.709), channel_id=1, source_target_pairs={{0,2},{2,0},{32,34},{34,32},{64,66},{66,64},{96,98},{98,96},{1,3},... | collective-permute-start | bytes 1474568 | tf_op jit(solution)/shard_map/ppermute | solution.py:85
  330.9 42.7 %collective-permute-start.4 = (bf16[5,128,384]{2,1,0:T(8,128)(2,1)S(1)}, bf16[5,128,384]{2,1,0:T(8,128)(2,1)S(1)}, u32[]{:S(2)}, u32[]{:S(2)}) collective-permute-start(bf16[5,128,384]{2,1,0:T(8,128)(2,1)S(1)} %bitcast.710), channel_id=1, source_target_pairs={{0,34},{2,32},{32,66},{34,64},{64,98},{66,96},{96,2},{98,0},{1,35}... | collective-permute-start | bytes 1474568 | tf_op jit(solution)/shard_map/ppermute | solution.py:85
  333.4 43.8 %collective-permute-start.5 = (bf16[5,128,384]{2,1,0:T(8,128)(2,1)S(1)}, bf16[5,128,384]{2,1,0:T(8,128)(2,1)S(1)}, u32[]{:S(2)}, u32[]{:S(2)}) collective-permute-start(bf16[5,128,384]{2,1,0:T(8,128)(2,1)S(1)} %bitcast.711), channel_id=1, source_target_pairs={{0,66},{2,64},{32,98},{34,96},{64,2},{66,0},{96,34},{98,32},{1,67}... | collective-permute-start | bytes 1474568 | tf_op jit(solution)/shard_map/ppermute | solution.py:85
  336.0 43.2 %collective-permute-start.6 = (bf16[5,128,384]{2,1,0:T(8,128)(2,1)S(1)}, bf16[5,128,384]{2,1,0:T(8,128)(2,1)S(1)}, u32[]{:S(2)}, u32[]{:S(2)}) collective-permute-start(bf16[5,128,384]{2,1,0:T(8,128)(2,1)S(1)} %bitcast.712), channel_id=1, source_target_pairs={{0,98},{2,96},{32,2},{34,0},{64,34},{66,32},{96,66},{98,64},{1,99}... | collective-permute-start | bytes 1474568 | tf_op jit(solution)/shard_map/ppermute | solution.py:85
  338.5 94.4 %collective-permute-start.7 = (bf16[5,384,256]{2,1,0:T(8,128)(2,1)S(1)}, bf16[5,384,256]{2,1,0:T(8,128)(2,1)S(1)}, u32[]{:S(2)}, u32[]{:S(2)}) collective-permute-start(bf16[5,384,256]{2,1,0:T(8,128)(2,1)S(1)} %bitcast.689), channel_id=1, source_target_pairs={{0,32},{2,34},{32,64},{34,66},{64,96},{66,98},{96,0},{98,2},{1,33}... | collective-permute-start | bytes 2949128 | tf_op jit(solution)/shard_map/ppermute | solution.py:85
  373.6 49.5 %copy-start.32 = (bf16[5,128,384]{2,1,0:T(8,128)(2,1)}, bf16[5,128,384]{2,1,0:T(8,128)(2,1)S(1)}, u32[]{:S(2)}) copy-start(bf16[5,128,384]{2,1,0:T(8,128)(2,1)S(1)} %collective-permute-done.3) | copy-start | bytes 1474564
  373.6 64.9 %collective-permute-start.8 = (bf16[5,384,256]{2,1,0:T(8,128)(2,1)S(1)}, bf16[5,384,256]{2,1,0:T(8,128)(2,1)}, u32[]{:S(2)}, u32[]{:S(2)}) collective-permute-start(bf16[5,384,256]{2,1,0:T(8,128)(2,1)S(1)} %bitcast.690), channel_id=1, source_target_pairs={{0,64},{2,66},{32,96},{34,98},{64,0},{66,2},{96,32},{98,34},{1,65}... | collective-permute-start | bytes 2949128 | tf_op jit(solution)/shard_map/ppermute | solution.py:85
  373.6 49.5 %copy-start.33 = (bf16[5,128,384]{2,1,0:T(8,128)(2,1)}, bf16[5,128,384]{2,1,0:T(8,128)(2,1)S(1)}, u32[]{:S(2)}) copy-start(bf16[5,128,384]{2,1,0:T(8,128)(2,1)S(1)} %collective-permute-done.4) | copy-start | bytes 1474564
  373.6 49.5 %collective-permute-start = (bf16[5,128,384]{2,1,0:T(8,128)(2,1)S(1)}, bf16[5,128,384]{2,1,0:T(8,128)(2,1)S(1)}, u32[]{:S(2)}, u32[]{:S(2)}) collective-permute-start(bf16[5,128,384]{2,1,0:T(8,128)(2,1)S(1)} %bitcast.713), channel_id=1, source_target_pairs={{0,32},{2,34},{32,64},{34,66},{64,96},{66,98},{96,0},{98,2},{1,33}... | collective-permute-start | bytes 1474568 | tf_op jit(solution)/shard_map/ppermute | solution.py:85
  377.2 45.9 %copy-start.34 = (bf16[5,128,384]{2,1,0:T(8,128)(2,1)}, bf16[5,128,384]{2,1,0:T(8,128)(2,1)S(1)}, u32[]{:S(2)}) copy-start(bf16[5,128,384]{2,1,0:T(8,128)(2,1)S(1)} %collective-permute-done.5) | copy-start | bytes 1474564
  377.2 55.7 %collective-permute-start.1 = (bf16[5,128,384]{2,1,0:T(8,128)(2,1)S(1)}, bf16[5,128,384]{2,1,0:T(8,128)(2,1)}, u32[]{:S(2)}, u32[]{:S(2)}) collective-permute-start(bf16[5,128,384]{2,1,0:T(8,128)(2,1)S(1)} %bitcast.714), channel_id=1, source_target_pairs={{0,64},{2,66},{32,96},{34,98},{64,0},{66,2},{96,32},{98,34},{1,65}... | collective-permute-start | bytes 1474568 | tf_op jit(solution)/shard_map/ppermute | solution.py:85
  379.2 43.9 %copy-start.35 = (bf16[5,128,384]{2,1,0:T(8,128)(2,1)}, bf16[5,128,384]{2,1,0:T(8,128)(2,1)S(1)}, u32[]{:S(2)}) copy-start(bf16[5,128,384]{2,1,0:T(8,128)(2,1)S(1)} %collective-permute-done.6) | copy-start | bytes 1474564
  379.2 53.7 %collective-permute-start.2 = (bf16[5,128,384]{2,1,0:T(8,128)(2,1)S(1)}, bf16[5,128,384]{2,1,0:T(8,128)(2,1)}, u32[]{:S(2)}, u32[]{:S(2)}) collective-permute-start(bf16[5,128,384]{2,1,0:T(8,128)(2,1)S(1)} %bitcast.715), channel_id=1, source_target_pairs={{0,96},{2,98},{32,0},{34,2},{64,32},{66,34},{96,64},{98,66},{1,97}... | collective-permute-start | bytes 1474568 | tf_op jit(solution)/shard_map/ppermute | solution.py:85
  423.8 53.1 %collective-permute-start.9 = (bf16[5,384,256]{2,1,0:T(8,128)(2,1)S(1)}, bf16[5,384,256]{2,1,0:T(8,128)(2,1)}, u32[]{:S(2)}, u32[]{:S(2)}) collective-permute-start(bf16[5,384,256]{2,1,0:T(8,128)(2,1)S(1)} %bitcast.691), channel_id=1, source_target_pairs={{0,96},{2,98},{32,0},{34,2},{64,32},{66,34},{96,64},{98,66},{1,97}... | collective-permute-start | bytes 2949128 | tf_op jit(solution)/shard_map/ppermute | solution.py:85
  432.9 82.2 %collective-permute-start.10 = (bf16[5,384,256]{2,1,0:T(8,128)(2,1)S(1)}, bf16[5,384,256]{2,1,0:T(8,128)(2,1)S(1)}, u32[]{:S(2)}, u32[]{:S(2)}) collective-permute-start(bf16[5,384,256]{2,1,0:T(8,128)(2,1)S(1)} %bitcast.692), channel_id=1, source_target_pairs={{0,2},{2,0},{32,34},{34,32},{64,66},{66,64},{96,98},{98,96},{1,3},... | collective-permute-start | bytes 2949128 | tf_op jit(solution)/shard_map/ppermute | solution.py:85
  432.9 82.2 %collective-permute-start.11 = (bf16[5,384,256]{2,1,0:T(8,128)(2,1)S(1)}, bf16[5,384,256]{2,1,0:T(8,128)(2,1)S(1)}, u32[]{:S(2)}, u32[]{:S(2)}) collective-permute-start(bf16[5,384,256]{2,1,0:T(8,128)(2,1)S(1)} %bitcast.693), channel_id=1, source_target_pairs={{0,34},{2,32},{32,66},{34,64},{64,98},{66,96},{96,2},{98,0},{1,35}... | collective-permute-start | bytes 2949128 | tf_op jit(solution)/shard_map/ppermute | solution.py:85
  432.9 83.1 %collective-permute-start.12 = (bf16[5,384,256]{2,1,0:T(8,128)(2,1)S(1)}, bf16[5,384,256]{2,1,0:T(8,128)(2,1)S(1)}, u32[]{:S(2)}, u32[]{:S(2)}) collective-permute-start(bf16[5,384,256]{2,1,0:T(8,128)(2,1)S(1)} %bitcast.694), channel_id=1, source_target_pairs={{0,66},{2,64},{32,98},{34,96},{64,2},{66,0},{96,34},{98,32},{1,67}... | collective-permute-start | bytes 2949128 | tf_op jit(solution)/shard_map/ppermute | solution.py:85
  438.5 77.5 %collective-permute-start.13 = (bf16[5,384,256]{2,1,0:T(8,128)(2,1)S(1)}, bf16[5,384,256]{2,1,0:T(8,128)(2,1)S(1)}, u32[]{:S(2)}, u32[]{:S(2)}) collective-permute-start(bf16[5,384,256]{2,1,0:T(8,128)(2,1)S(1)} %bitcast.695), channel_id=1, source_target_pairs={{0,98},{2,96},{32,2},{34,0},{64,34},{66,32},{96,66},{98,64},{1,99}... | collective-permute-start | bytes 2949128 | tf_op jit(solution)/shard_map/ppermute | solution.py:85
  569.2 20.3 %copy-start.2 = (f32[5,1536,1,8,26]{1,4,3,2,0:T(8,128)S(1)}, f32[5,1536,1,8,26]{1,4,3,2,0:T(8,128)}, u32[]{:S(2)}) copy-start(f32[5,1536,1,8,26]{1,4,3,2,0:T(8,128)} %get-tuple-element.25) | copy-start | bytes 19169284
  576.2 10.6 %collective-permute-start.14 = (f32[8,5,26,1536]{3,0,2,1:T(8,128)S(1)}, f32[8,5,26,1536]{3,0,2,1:T(8,128)S(1)}, u32[]{:S(2)}, u32[]{:S(2)}) collective-permute-start(f32[8,5,26,1536]{3,0,2,1:T(8,128)S(1)} %copy.273), channel_id=1, source_target_pairs={{0,1},{1,0},{2,3},{3,2},{4,5},{5,4},{6,7},{7,6},{8,9},{9,8},{10,11... | collective-permute-start | bytes 19169288 | tf_op jit(solution)/shard_map/ppermute | solution.py:211
  596.0 10.5 %copy-start.77 = (bf16[128,8]{0,1:T(8,128)(2,1)S(1)}, bf16[128,8]{0,1:T(8,128)(2,1)}, u32[]{:S(2)}) copy-start(bf16[128,8]{0,1:T(8,128)(2,1)} %param.23) | copy-start | bytes 6148
  596.0 10.6 %copy-start.71 = (s32[1024,1]{0,1:T(1,128)S(1)}, s32[1024,1]{0,1:T(1,128)}, u32[]{:S(2)}) copy-start(s32[1024,1]{0,1:T(1,128)} %copy-done.70) | copy-start | bytes 12292
  599.1 63.8 %all-to-all-start.1 = ((bf16[8,5,26,1536]{3,2,1,0:T(8,128)(2,1)}), bf16[8,5,26,1536]{3,2,1,0:T(8,128)(2,1)}, u32[]{:S(2)}, u32[]{:S(2)}) async-start(bf16[8,5,26,1536]{3,2,1,0:T(8,128)(2,1)} %copy.274), calls=%async_computation.1 | async-start | bytes 7864320 | tf_op jit(solution)/shard_map/all_to_all | solution.py:213
  669.0 22.0 %copy-start.1 = (bf16[1536,512]{1,0:T(8,128)(2,1)S(1)}, bf16[1536,512]{1,0:T(8,128)(2,1)}, u32[]{:S(2)}) copy-start(bf16[1536,512]{1,0:T(8,128)(2,1)} %param.16) | copy-start | bytes 4718596
  (48 other events, 132.5 us)
Sparse Core Ops, SparseCore 0:
  10.3 47.4 all-gather.7
  60.6 52.1 all-gather.5
  330.5 17.1 all-gather.9

commit v5 on v4

--- a/solution.py
+++ b/solution.py
@@ -122,8 +122,6 @@
     length = cache_len[0]
     cache_rows = cache_kv[0]
     cache_all = lax.all_gather(cache_rows, EXP_AXES, axis=0, tiled=True)
-    gate_up_full = spread_pieces(w_gate_up[0], 1)
-    down_full = spread_pieces(w_down[0], 2)
     req_index = lax.axis_index("req")
     chunk_order = (req_index - jnp.arange(lax.axis_size("req"), dtype=jnp.int32)) % lax.axis_size("req")
     normed = rms_scale(hidden_in, attn_gain)
@@ -158,6 +156,9 @@
           kv_width,
       )
     new_all = lax.all_gather(new_kv, EXP_AXES, axis=0, tiled=True)
+    gate_up_local, down_local, new_all = lax.optimization_barrier((w_gate_up[0], w_down[0], new_all))
+    gate_up_full = spread_pieces(gate_up_local, 1)
+    down_full = spread_pieces(down_local, 2)
     for offset in range(0, new_all.shape[0], key_block):
         block_size = min(key_block, new_all.shape[0] - offset)
         new_pos = offset + jnp.arange(block_size, dtype=jnp.int32)
@@ -195,7 +196,8 @@
     blocks = EXPERTS // block_experts
     outgoing = moe_in[slot_token.reshape(blocks, block_experts, MOST)]
     arrived = lax.all_to_all(outgoing, ("x", "zhi"), split_axis=0, concat_axis=0, tiled=True)
-    arrived = lax.all_gather(arrived, "core", axis=0)
+    swap = [(0, 1), (1, 0)]
+    arrived = jnp.stack([arrived, lax.ppermute(arrived, "core", swap)], axis=0)
     gate_up = jnp.einsum(
         "askmd,pkdf->aspkmf", arrived, gate_up_full, preferred_element_type=jnp.float32
     )
@@ -206,10 +208,7 @@
         "aspkmf,pkfd->aspkmd", activated, down_full, preferred_element_type=jnp.float32
     ).astype(jnp.bfloat16)
     computed = jnp.sum(computed, axis=2, dtype=jnp.float32)
-    mine = lax.dynamic_index_in_dim(computed, core, axis=0, keepdims=False)
-    theirs = lax.dynamic_index_in_dim(computed, 1 - core, axis=0, keepdims=False)
-    theirs = lax.ppermute(theirs, "core", [(0, 1), (1, 0)])
-    computed = (mine + theirs).astype(jnp.bfloat16)
+    computed = (computed[0] + lax.ppermute(computed[1], "core", swap)).astype(jnp.bfloat16)
     returned = lax.all_to_all(computed, ("x", "zhi"), split_axis=0, concat_axis=0, tiled=True)
     summed = returned.astype(jnp.float32).reshape(EXPERTS * MOST, width)
     picked = summed[slot_index] * expert_weights.reshape(-1).astype(jnp.float32)[:, None]

time: 709 us -> 726 us (1.024)
  waiting for transfers between devices: 277 us -> 351 us
  blocking collectives: 53.2 us -> 0 us
  starting transfers between devices: 32.4 us -> 45.1 us
  local copies, waits for them, and re-layouts: 121 us -> 113 us
  other arithmetic: 74.4 us -> 66.5 us
    all_to_all x0 -> x1, waiting for transfers between devices: none -> 55.8 us  [shards(): lax.all_to_all(outgoing, ('x', 'zhi'), split_axis=0, concat_axis=0, tiled...]
    all_to_all x1 -> x0, blocking collectives: 53.2 us -> none  [shards(): lax.all_to_all(outgoing, ('x', 'zhi'), split_axis=0, concat_axis=0, tiled...]
    reduce_sum x0 -> x1, local copies, waits for them, and re-layouts: none -> 18.3 us  [shards(): computed = jnp.sum(computed, axis=2, dtype=jnp.float32)]
    ppermute x14, waiting for transfers between devices: 150 us -> 168 us  [spread_pieces(): chunks.append(lax.ppermute(local, ('req', 'zlo'), perm))]
    another operation x1 -> x0, local copies, waits for them, and re-layouts: 14.1 us -> none
    all_gather x1 -> x0, local copies, waits for them, and re-layouts: 9.76 us -> none  [shards(): arrived = lax.all_gather(arrived, 'core', axis=0)]
    ppermute x14, starting transfers between devices: 24.6 us -> 34.1 us  [spread_pieces(): chunks.append(lax.ppermute(local, ('req', 'zlo'), perm))]
  transfers between devices with their start and end apart: 19 -> 20, of which waited for: 10 -> 13; matrix products, arithmetic and copies ran while one was open for 8% -> 8% of each run, Pallas kernels for 0% -> 0%
where the time goes in v5:
time: 726 us; the launch traced here: 714 us
  waiting for transfers between devices  351 us (48%)
  matrix products  123 us (17%)
  local copies, waits for them, and re-layouts  113 us (16%)
  other arithmetic  66.5 us (9%)
  starting transfers between devices  45.1 us (6%)
  between operations  16.2 us (2%)
    ppermute x14, waiting for transfers between devices, spread_pieces(): chunks.append(lax.ppermute(local, ('req', 'zlo'), perm))  168 us
    all_to_all x1, waiting for transfers between devices, shards(): lax.all_to_all(computed, ('x', 'zhi'), split_axis=0, concat_axis=0, tiled...  56.2 us
    all_to_all x1, waiting for transfers between devices, shards(): lax.all_to_all(outgoing, ('x', 'zhi'), split_axis=0, concat_axis=0, tiled...  55.8 us
    dot_general x11, matrix products, attend_block(): jnp.einsum('kgtr,rkd->kgtd', weights.astype(jnp.bfloat16), value_heads, p...  44.4 us
    dot_general x11, matrix products, attend_block(): jnp.einsum('tkgd,rkd->kgtr', queries, key_heads, preferred_element_type=j...  42.5 us
    reduce_sum x11, other arithmetic, attend_block(): new_sum = run_sum * factor + jnp.sum(weights, axis=-1)  40.8 us
    ppermute x14, starting transfers between devices, spread_pieces(): chunks.append(lax.ppermute(local, ('req', 'zlo'), perm))  34.1 us
    all_gather x1, waiting for transfers between devices, shards(): new_all = lax.all_gather(new_kv, EXP_AXES, axis=0, tiled=True)  32.3 us
  transfers between devices with their start and end apart: 20, of which 13 were waited for; matrix products, arithmetic and copies ran while one was open for 8% of the time, Pallas kernels for 0%

profile of v5, /device:TPU:0, one launch (start us, length us, event | category | flops | bytes accessed | tf_op | source)
XLA Modules:
  0.0 714.0 jit_solution(586528087716946995)
XLA Ops:
  17.7 4.3 scatter_custom_fusion
  24.6 4.3 fusion.261
  30.1 27.6 %all-gather.6.cloned.1.call-done = bf16[1,1536,1024]{2,1,0:T(8,128)(2,1)} async-done(((bf16[1,48,1024]{2,1,0:T(8,128)(2,1)}), bf16[1,1536,1024]{2,1,0:T(8,128)(2,1)}) %all-gather.6.cloned.1.call-update) | async-done | bytes 3145744 | tf_op jit(solution)/shard_map/all_gather | solution.py:124
  57.7 3.2 fusion.267
  66.7 4.4 bitcast_reduce_fusion.2
  71.1 5.0 bitcast_reduce_fusion
  76.1 4.3 bitcast_reduce_fusion.1
  80.4 32.3 %all-gather.4.cloned.1.call-done = bf16[4096,1024]{1,0:T(8,128)(2,1)} async-done(((bf16[128,1024]{1,0:T(8,128)(2,1)}), bf16[4096,1024]{1,0:T(8,128)(2,1)}) %all-gather.4.cloned.1.call-update) | async-done | bytes 8388624 | tf_op jit(solution)/shard_map/all_gather | solution.py:158
  112.7 5.9 fusion.266
  137.1 4.9 fusion.16
  143.4 3.8 fusion.20
  147.2 3.8 fusion.19
  151.0 3.7 fusion.18
  154.8 3.8 fusion.17
  158.6 3.8 fusion.15
  162.4 3.8 fusion.21
  167.5 2.8 fusion.22
  170.3 2.8 fusion.96
  175.1 4.5 fusion.24
  179.6 5.4 fusion.99
  187.1 4.5 fusion.26
  191.6 5.4 fusion.102
  198.0 4.5 fusion.28
  202.5 5.4 fusion.105
  208.2 4.8 fusion.30
  213.0 5.4 fusion.108
  218.6 3.9 fusion.32
  222.5 5.3 fusion.111
  228.0 3.9 fusion.34
  231.9 5.3 fusion.114
  237.4 4.0 fusion.36
  241.5 3.9 fusion.117
  245.5 4.2 fusion.38
  262.8 5.2 gather_fusion.1
  268.0 5.5 reshape.947
  273.5 5.2 all-to-all-start
  279.4 55.8 %all-to-all-done = bf16[8,5,26,1536]{3,2,1,0:T(8,128)(2,1)} async-done(((bf16[8,5,26,1536]{3,2,1,0:T(8,128)(2,1)}), bf16[8,5,26,1536]{3,2,1,0:T(8,128)(2,1)}, u32[]{:S(2)}, u32[]{:S(2)}) %all-to-all-start) | async-done | bytes 3194912 | tf_op jit(solution)/shard_map/all_to_all | solution.py:198
  335.3 3.9 copy.274
  341.0 3.4 collective-permute-start.5
  346.7 19.4 %collective-permute-done.4 = bf16[5,128,384]{2,1,0:T(8,128)(2,1)S(1)} collective-permute-done((bf16[5,128,384]{2,1,0:T(8,128)(2,1)S(1)}, bf16[5,128,384]{2,1,0:T(8,128)(2,1)S(1)}, u32[]{:S(2)}, u32[]{:S(2)}) %collective-permute-start.4) | collective-permute-done | bytes 491552 | tf_op jit(solution)/shard_map/ppermute | solution.py:85
  366.1 16.0 %collective-permute-done.5 = bf16[5,128,384]{2,1,0:T(8,128)(2,1)S(1)} collective-permute-done((bf16[5,128,384]{2,1,0:T(8,128)(2,1)S(1)}, bf16[5,128,384]{2,1,0:T(8,128)(2,1)S(1)}, u32[]{:S(2)}, u32[]{:S(2)}) %collective-permute-start.5) | collective-permute-done | bytes 491552 | tf_op jit(solution)/shard_map/ppermute | solution.py:85
  382.2 9.4 %collective-permute-start.8 = (bf16[5,384,256]{2,1,0:T(8,128)(2,1)S(1)}, bf16[5,384,256]{2,1,0:T(8,128)(2,1)S(1)}, u32[]{:S(2)}, u32[]{:S(2)}) collective-permute-start(bf16[5,384,256]{2,1,0:T(8,128)(2,1)S(1)} %bitcast.699), channel_id=1, source_target_pairs={{0,64},{2,66},{32,96},{34,98},{64,0},{66,2},{96,32},{98,34},{1,65}... | collective-permute-start | bytes 2949128 | tf_op jit(solution)/shard_map/ppermute | solution.py:85
  392.9 10.4 %collective-permute-done.1 = bf16[5,128,384]{2,1,0:T(8,128)(2,1)S(1)} collective-permute-done((bf16[5,128,384]{2,1,0:T(8,128)(2,1)S(1)}, bf16[5,128,384]{2,1,0:T(8,128)(2,1)S(1)}, u32[]{:S(2)}, u32[]{:S(2)}) %collective-permute-start.1) | collective-permute-done | bytes 491552 | tf_op jit(solution)/shard_map/ppermute | solution.py:85
  403.3 39.0 %collective-permute-done.2 = bf16[5,128,384]{2,1,0:T(8,128)(2,1)S(1)} collective-permute-done((bf16[5,128,384]{2,1,0:T(8,128)(2,1)S(1)}, bf16[5,128,384]{2,1,0:T(8,128)(2,1)S(1)}, u32[]{:S(2)}, u32[]{:S(2)}) %collective-permute-start.2) | collective-permute-done | bytes 491552 | tf_op jit(solution)/shard_map/ppermute | solution.py:85
  442.8 11.7 %collective-permute-start.11 = (bf16[5,384,256]{2,1,0:T(8,128)(2,1)S(1)}, bf16[5,384,256]{2,1,0:T(8,128)(2,1)S(1)}, u32[]{:S(2)}, u32[]{:S(2)}) collective-permute-start(bf16[5,384,256]{2,1,0:T(8,128)(2,1)S(1)} %bitcast.702), channel_id=1, source_target_pairs={{0,34},{2,32},{32,66},{34,64},{64,98},{66,96},{96,2},{98,0},{1,35}... | collective-permute-start | bytes 2949128 | tf_op jit(solution)/shard_map/ppermute | solution.py:85
  455.2 3.4 collective-permute-start.13
  458.9 2.5 maximum_bitcast_fusion.13
  463.7 23.6 %collective-permute-done.10 = bf16[5,384,256]{2,1,0:T(8,128)(2,1)S(1)} collective-permute-done((bf16[5,384,256]{2,1,0:T(8,128)(2,1)S(1)}, bf16[5,384,256]{2,1,0:T(8,128)(2,1)S(1)}, u32[]{:S(2)}, u32[]{:S(2)}) %collective-permute-start.10) | collective-permute-done | bytes 983072 | tf_op jit(solution)/shard_map/ppermute | solution.py:85
  487.3 27.1 %collective-permute-done.11 = bf16[5,384,256]{2,1,0:T(8,128)(2,1)S(1)} collective-permute-done((bf16[5,384,256]{2,1,0:T(8,128)(2,1)S(1)}, bf16[5,384,256]{2,1,0:T(8,128)(2,1)S(1)}, u32[]{:S(2)}, u32[]{:S(2)}) %collective-permute-start.11) | collective-permute-done | bytes 983072 | tf_op jit(solution)/shard_map/ppermute | solution.py:85
  514.5 30.7 %collective-permute-done.12 = bf16[5,384,256]{2,1,0:T(8,128)(2,1)S(1)} collective-permute-done((bf16[5,384,256]{2,1,0:T(8,128)(2,1)S(1)}, bf16[5,384,256]{2,1,0:T(8,128)(2,1)S(1)}, u32[]{:S(2)}, u32[]{:S(2)}) %collective-permute-start.12) | collective-permute-done | bytes 983072 | tf_op jit(solution)/shard_map/ppermute | solution.py:85
  547.4 4.5 copy.329
  551.9 3.1 copy.328
  555.0 12.1 %fusion.84 = f32[2,8,2,5,26,256]{5,4,1,0,2,3:T(8,128)} fusion(bf16[1,8,5,26,1536]{4,3,1,0,2:T(8,128)(2,1)} %bitcast.675, bf16[1,8,5,26,1536]{4,3,1,0,2:T(8,128)(2,1)} %bitcast.676, bf16[1,5,1536,256]{3,2,0,1:T(8,128)(2,1)} %maximum_bitcast_fusion.7, bf16[1,5,1536,256]{3,2,0,1:T(8,128)(2,1)} %maximum_bitcast_fusion.6), kind=kOutput, calls=%fused_computation.118 | convolution fusion | flops 3300065280 | bytes 18513920 | tf_op jit(solution)/shard_map/askmd,pkdf->aspkmf/dot_general | solution.py:201
  567.1 14.5 %convert_reduce_fusion = f32[5,1536,2,8,26]{1,4,3,2,0:T(8,128)} fusion(bf16[1,5,128,1536]{3,2,1,0:T(8,128)(2,1)} %maximum_bitcast_fusion.13, bf16[1,5,128,1536]{3,2,1,0:T(8,128)(2,1)S(1)} %maximum_bitcast_fusion.12, f32[2,8,2,5,26,256]{5,4,1,0,2,3:T(8,128)} %fusion.84), kind=kOutput, calls=%fused_computation.5 | convolution fusion | flops 1662812160 | bytes 20971520 | tf_op jit(solution)/shard_map/aspkmf,pkfd->aspkmd/dot_general | solution.py:207
  581.6 18.3 %copy.327 = f32[5,1536,2,8,26]{1,3,4,0,2:T(8,128)} copy(f32[5,1536,2,8,26]{1,4,3,2,0:T(8,128)} %convert_reduce_fusion) | data formatting | bytes 25559040 | tf_op jit(solution)/shard_map/reduce_sum | solution.py:210
  599.9 3.4 slice_bitcast_fusion
  603.4 10.4 %collective-permute-done.15 = f32[8,5,26,1536]{3,0,2,1:T(8,128)} collective-permute-done((f32[8,5,26,1536]{3,0,2,1:T(8,128)S(1)}, f32[8,5,26,1536]{3,0,2,1:T(8,128)}, u32[]{:S(2)}, u32[]{:S(2)}) %collective-permute-start.15) | collective-permute-done | bytes 6389792 | tf_op jit(solution)/shard_map/ppermute | solution.py:211
  613.8 3.9 fusion.6
  617.8 3.1 copy.278
  620.9 5.6 all-to-all-start.1
  626.6 56.2 %all-to-all-done.1 = bf16[8,5,26,1536]{3,2,1,0:T(8,128)(2,1)} async-done(((bf16[8,5,26,1536]{3,2,1,0:T(8,128)(2,1)}), bf16[8,5,26,1536]{3,2,1,0:T(8,128)(2,1)}, u32[]{:S(2)}, u32[]{:S(2)}) %all-to-all-start.1) | async-done | bytes 3194912 | tf_op jit(solution)/shard_map/all_to_all | solution.py:212
  682.8 6.2 reshape.937
  689.0 10.7 %gather_fusion.2 = f32[1024,1536]{1,0:T(8,128)} fusion(f32[1040,1536]{1,0:T(8,128)} %reshape.937, s32[1024]{0:T(1024)S(1)} %broadcast_clamp_fusion), kind=kCustom, calls=%fused_computation.2 | custom fusion | bytes 12587008 | tf_op jit(solution)/shard_map/gather | solution.py:214
  699.7 5.1 fusion.7
  (293 shorter events, 73.3 us)
Async XLA Ops:
  7.2 17.4 %copy-start.3 = (bf16[128,1536]{1,0:T(8,128)(2,1)S(1)}, bf16[128,1536]{1,0:T(8,128)(2,1)}, u32[]{:S(2)}) copy-start(bf16[128,1536]{1,0:T(8,128)(2,1)} %param.13) | copy-start | bytes 1179652
  7.2 8.2 %copy-start.72 = (bf16[1536]{0:T(1024)(128)(2,1)S(1)}, bf16[1536]{0:T(1024)(128)(2,1)}, u32[]{:S(2)}) copy-start(bf16[1536]{0:T(1024)(128)(2,1)} %param.21) | copy-start | bytes 9220
  7.2 9.5 %copy-start.65 = (s32[128,8]{0,1:T(8,128)S(1)}, s32[128,8]{0,1:T(8,128)}, u32[]{:S(2)}) copy-start(s32[128,8]{0,1:T(8,128)} %param.22) | copy-start | bytes 12292
  7.2 50.5 %all-gather.6.cloned.1.call-start = ((), (), s32[]{:S(2)}) async-start(), calls=%async_computation.3 | async-start | bytes 3244032 | tf_op jit(solution)/shard_map/all_gather | solution.py:124
  7.9 104.8 %all-gather.4.cloned.1.call-start = ((), (), s32[]{:S(2)}) async-start(), calls=%async_computation.2 | async-start | bytes 8650752 | tf_op jit(solution)/shard_map/all_gather | solution.py:158
  66.7 9.4 %copy-start.69 = (pred[512]{0:T(512)(128)(4,1)S(1)}, pred[512]{0:T(512)(128)(4,1)}, u32[]{:S(2)}) copy-start(pred[512]{0:T(512)(128)(4,1)} %broadcast_compare_fusion.8) | copy-start | bytes 1540
  137.1 4.9 copy-start.12
  137.1 5.0 copy-start.23
  137.1 6.2 copy-start.11
  142.1 24.7 %copy-start.35 = (f32[8,3,128]{2,1,0:T(4,128)}, f32[8,3,128]{2,1,0:T(4,128)S(1)}, u32[]{:S(2)}) copy-start(f32[8,3,128]{2,1,0:T(4,128)S(1)} %get-tuple-element.80) | copy-start | bytes 36868
  142.1 5.1 copy-start.10
  142.1 5.1 copy-start.14
  143.4 23.4 %copy-start.37 = (f32[8,3,128]{2,1,0:T(4,128)}, f32[8,3,128]{2,1,0:T(4,128)S(1)}, u32[]{:S(2)}) copy-start(f32[8,3,128]{2,1,0:T(4,128)S(1)} %get-tuple-element.84) | copy-start | bytes 36868
  143.4 7.6 %copy-start.9 = (bf16[512,512]{0,1:T(8,128)(2,1)S(1)}, bf16[512,512]{0,1:T(8,128)(2,1)}, u32[]{:S(2)}) copy-start(bf16[512,512]{0,1:T(8,128)(2,1)} %copy.256) | copy-start | bytes 1572868
  143.4 7.6 %copy-start.16 = (pred[128,512]{1,0:T(8,128)(4,1)S(1)}, pred[128,512]{1,0:T(8,128)(4,1)}, u32[]{:S(2)}) copy-start(pred[128,512]{1,0:T(8,128)(4,1)} %get-tuple-element.65) | copy-start | bytes 196612
  147.2 19.6 %copy-start.40 = (f32[8,3,128]{2,1,0:T(4,128)}, f32[8,3,128]{2,1,0:T(4,128)S(1)}, u32[]{:S(2)}) copy-start(f32[8,3,128]{2,1,0:T(4,128)S(1)} %get-tuple-element.72) | copy-start | bytes 36868
  147.2 7.6 %copy-start.8 = (bf16[512,512]{0,1:T(8,128)(2,1)S(1)}, bf16[512,512]{0,1:T(8,128)(2,1)}, u32[]{:S(2)}) copy-start(bf16[512,512]{0,1:T(8,128)(2,1)} %copy.253) | copy-start | bytes 1572868
  147.2 7.6 %copy-start.18 = (pred[128,512]{1,0:T(8,128)(4,1)S(1)}, pred[128,512]{1,0:T(8,128)(4,1)}, u32[]{:S(2)}) copy-start(pred[128,512]{1,0:T(8,128)(4,1)} %get-tuple-element.64) | copy-start | bytes 196612
  151.0 15.8 %copy-start.42 = (f32[8,3,128]{2,1,0:T(4,128)}, f32[8,3,128]{2,1,0:T(4,128)S(1)}, u32[]{:S(2)}) copy-start(f32[8,3,128]{2,1,0:T(4,128)S(1)} %get-tuple-element.74) | copy-start | bytes 36868
  151.0 7.5 %copy-start.7 = (bf16[512,512]{0,1:T(8,128)(2,1)S(1)}, bf16[512,512]{0,1:T(8,128)(2,1)}, u32[]{:S(2)}) copy-start(bf16[512,512]{0,1:T(8,128)(2,1)} %copy.247) | copy-start | bytes 1572868
  151.0 7.5 %copy-start.21 = (pred[128,512]{1,0:T(8,128)(4,1)S(1)}, pred[128,512]{1,0:T(8,128)(4,1)}, u32[]{:S(2)}) copy-start(pred[128,512]{1,0:T(8,128)(4,1)} %get-tuple-element.69) | copy-start | bytes 196612
  154.7 12.1 %copy-start.44 = (f32[8,3,128]{2,1,0:T(4,128)}, f32[8,3,128]{2,1,0:T(4,128)S(1)}, u32[]{:S(2)}) copy-start(f32[8,3,128]{2,1,0:T(4,128)S(1)} %get-tuple-element.76) | copy-start | bytes 36868
  154.8 7.6 %copy-start.6 = (bf16[512,512]{0,1:T(8,128)(2,1)S(1)}, bf16[512,512]{0,1:T(8,128)(2,1)}, u32[]{:S(2)}) copy-start(bf16[512,512]{0,1:T(8,128)(2,1)} %copy.265) | copy-start | bytes 1572868
  158.5 7.6 %copy-start.33 = (f32[8,3,128]{2,1,0:T(4,128)S(1)}, f32[8,3,128]{2,1,0:T(4,128)}, u32[]{:S(2)}) copy-start(f32[8,3,128]{2,1,0:T(4,128)} %get-tuple-element.88) | copy-start | bytes 36868
  158.5 7.6 %copy-start.48 = (f32[8,3,128]{2,1,0:T(4,128)S(1)}, f32[8,3,128]{2,1,0:T(4,128)}, u32[]{:S(2)}) copy-start(f32[8,3,128]{2,1,0:T(4,128)} %get-tuple-element.86) | copy-start | bytes 36868
  162.4 7.9 %copy-start.27 = (bf16[512,512]{0,1:T(8,128)(2,1)S(1)}, bf16[512,512]{0,1:T(8,128)(2,1)}, u32[]{:S(2)}) copy-start(bf16[512,512]{0,1:T(8,128)(2,1)} %copy.246) | copy-start | bytes 1572868
  167.5 78.0 %copy-start.54 = (f32[8,3,128]{2,1,0:T(4,128)}, f32[8,3,128]{2,1,0:T(4,128)S(1)}, u32[]{:S(2)}) copy-start(f32[8,3,128]{2,1,0:T(4,128)S(1)} %get-tuple-element.59) | copy-start | bytes 36868
  179.6 7.5 %copy-start.20 = (pred[128,512]{1,0:T(8,128)(4,1)S(1)}, pred[128,512]{1,0:T(8,128)(4,1)}, u32[]{:S(2)}) copy-start(pred[128,512]{1,0:T(8,128)(4,1)} %get-tuple-element.63) | copy-start | bytes 196612
  191.6 6.5 copy-start.19
  202.5 5.6 copy-start.17
  213.0 5.6 copy-start.15
  237.4 14.2 %slice-start = ((s8[6291456]{0:T(1024)(128)(4,1)}), s8[4194304]{0:T(1024)(128)(4,1)S(1)}, s32[]{:S(2)}) async-start(s8[6291456]{0:T(1024)(128)(4,1)} %bitcast.667), calls=%async_computation.4 | async-start | bytes 8388608
  241.4 8.3 %slice-start.2 = ((s8[6291456]{0:T(1024)(128)(4,1)}), s8[4194304]{0:T(1024)(128)(4,1)S(1)}, s32[]{:S(2)}) async-start(s8[6291456]{0:T(1024)(128)(4,1)} %bitcast.669), calls=%async_computation.6 | async-start | bytes 8388608
  241.5 8.3 %slice-start.3 = ((s8[6291456]{0:T(1024)(128)(4,1)}), s8[2097152]{0:T(1024)(128)(4,1)S(1)}, s32[]{:S(2)}) async-start(s8[6291456]{0:T(1024)(128)(4,1)} %bitcast.669), calls=%async_computation.7 | async-start | bytes 4194304
  241.5 10.2 %slice-start.1 = ((s8[6291456]{0:T(1024)(128)(4,1)}), s8[2097152]{0:T(1024)(128)(4,1)S(1)}, s32[]{:S(2)}) async-start(s8[6291456]{0:T(1024)(128)(4,1)} %bitcast.667), calls=%async_computation.5 | async-start | bytes 4194304
  245.5 6.2 copy-start.49
  245.5 6.2 copy-start.68
  245.5 8.2 %slice-start.4 = ((s8[6291456]{0:T(1024)(128)(4,1)}), s8[4194304]{0:T(1024)(128)(4,1)S(1)}, s32[]{:S(2)}) async-start(s8[6291456]{0:T(1024)(128)(4,1)} %bitcast.671), calls=%async_computation.8 | async-start | bytes 8388608
  268.0 10.7 %copy-start.31 = (bf16[1,5,128,384]{3,2,1,0:T(8,128)(2,1)S(1)}, bf16[1,5,128,384]{3,2,1,0:T(8,128)(2,1)}, u32[]{:S(2)}) copy-start(bf16[1,5,128,384]{3,2,1,0:T(8,128)(2,1)} %param.25) | copy-start | bytes 1474564
  273.5 108.7 %copy-start.13 = (bf16[1,5,384,256]{3,2,1,0:T(8,128)(2,1)S(1)}, bf16[1,5,384,256]{3,2,1,0:T(8,128)(2,1)}, u32[]{:S(2)}) copy-start(bf16[1,5,384,256]{3,2,1,0:T(8,128)(2,1)} %param.24) | copy-start | bytes 2949124
  273.5 61.8 %all-to-all-start = ((bf16[8,5,26,1536]{3,2,1,0:T(8,128)(2,1)}), bf16[8,5,26,1536]{3,2,1,0:T(8,128)(2,1)}, u32[]{:S(2)}, u32[]{:S(2)}) async-start(bf16[8,5,26,1536]{3,2,1,0:T(8,128)(2,1)} %reshape.947), calls=%async_computation | async-start | bytes 7864320 | tf_op jit(solution)/shard_map/all_to_all | solution.py:198
  278.7 67.4 %collective-permute-start.3 = (bf16[5,128,384]{2,1,0:T(8,128)(2,1)S(1)}, bf16[5,128,384]{2,1,0:T(8,128)(2,1)S(1)}, u32[]{:S(2)}, u32[]{:S(2)}) collective-permute-start(bf16[5,128,384]{2,1,0:T(8,128)(2,1)S(1)} %bitcast.718), channel_id=1, source_target_pairs={{0,2},{2,0},{32,34},{34,32},{64,66},{66,64},{96,98},{98,96},{1,3},... | collective-permute-start | bytes 1474568 | tf_op jit(solution)/shard_map/ppermute | solution.py:85
  339.2 212.7 %collective-permute-start.14 = (bf16[8,5,26,1536]{3,0,2,1:T(8,128)(2,1)S(1)}, bf16[8,5,26,1536]{3,0,2,1:T(8,128)(2,1)S(1)}, u32[]{:S(2)}, u32[]{:S(2)}) collective-permute-start(bf16[8,5,26,1536]{3,0,2,1:T(8,128)(2,1)S(1)} %copy.274), channel_id=1, source_target_pairs={{0,1},{1,0},{2,3},{3,2},{4,5},{5,4},{6,7},{7,6},{8,9},{9,8},{10,11... | collective-permute-start | bytes 9584648 | tf_op jit(solution)/shard_map/ppermute | solution.py:200
  339.2 26.9 %collective-permute-start.4 = (bf16[5,128,384]{2,1,0:T(8,128)(2,1)S(1)}, bf16[5,128,384]{2,1,0:T(8,128)(2,1)S(1)}, u32[]{:S(2)}, u32[]{:S(2)}) collective-permute-start(bf16[5,128,384]{2,1,0:T(8,128)(2,1)S(1)} %bitcast.719), channel_id=1, source_target_pairs={{0,34},{2,32},{32,66},{34,64},{64,98},{66,96},{96,2},{98,0},{1,35}... | collective-permute-start | bytes 1474568 | tf_op jit(solution)/shard_map/ppermute | solution.py:85
  341.0 41.1 %collective-permute-start.5 = (bf16[5,128,384]{2,1,0:T(8,128)(2,1)S(1)}, bf16[5,128,384]{2,1,0:T(8,128)(2,1)S(1)}, u32[]{:S(2)}, u32[]{:S(2)}) collective-permute-start(bf16[5,128,384]{2,1,0:T(8,128)(2,1)S(1)} %bitcast.720), channel_id=1, source_target_pairs={{0,66},{2,64},{32,98},{34,96},{64,2},{66,0},{96,34},{98,32},{1,67}... | collective-permute-start | bytes 1474568 | tf_op jit(solution)/shard_map/ppermute | solution.py:85
  344.4 37.7 %collective-permute-start.6 = (bf16[5,128,384]{2,1,0:T(8,128)(2,1)S(1)}, bf16[5,128,384]{2,1,0:T(8,128)(2,1)S(1)}, u32[]{:S(2)}, u32[]{:S(2)}) collective-permute-start(bf16[5,128,384]{2,1,0:T(8,128)(2,1)S(1)} %bitcast.721), channel_id=1, source_target_pairs={{0,98},{2,96},{32,2},{34,0},{64,34},{66,32},{96,66},{98,64},{1,99}... | collective-permute-start | bytes 1474568 | tf_op jit(solution)/shard_map/ppermute | solution.py:85
  346.1 109.1 %copy-start.32 = (bf16[5,128,384]{2,1,0:T(8,128)(2,1)}, bf16[5,128,384]{2,1,0:T(8,128)(2,1)S(1)}, u32[]{:S(2)}) copy-start(bf16[5,128,384]{2,1,0:T(8,128)(2,1)S(1)} %collective-permute-done.3) | copy-start | bytes 1474564
  346.1 46.6 %collective-permute-start = (bf16[5,128,384]{2,1,0:T(8,128)(2,1)S(1)}, bf16[5,128,384]{2,1,0:T(8,128)(2,1)S(1)}, u32[]{:S(2)}, u32[]{:S(2)}) collective-permute-start(bf16[5,128,384]{2,1,0:T(8,128)(2,1)S(1)} %bitcast.722), channel_id=1, source_target_pairs={{0,32},{2,34},{32,64},{34,66},{64,96},{66,98},{96,0},{98,2},{1,33}... | collective-permute-start | bytes 1474568 | tf_op jit(solution)/shard_map/ppermute | solution.py:85
  366.1 37.2 %collective-permute-start.1 = (bf16[5,128,384]{2,1,0:T(8,128)(2,1)S(1)}, bf16[5,128,384]{2,1,0:T(8,128)(2,1)S(1)}, u32[]{:S(2)}, u32[]{:S(2)}) collective-permute-start(bf16[5,128,384]{2,1,0:T(8,128)(2,1)S(1)} %bitcast.723), channel_id=1, source_target_pairs={{0,64},{2,66},{32,96},{34,98},{64,0},{66,2},{96,32},{98,34},{1,65}... | collective-permute-start | bytes 1474568 | tf_op jit(solution)/shard_map/ppermute | solution.py:85
  382.2 60.6 %collective-permute-start.7 = (bf16[5,384,256]{2,1,0:T(8,128)(2,1)S(1)}, bf16[5,384,256]{2,1,0:T(8,128)(2,1)S(1)}, u32[]{:S(2)}, u32[]{:S(2)}) collective-permute-start(bf16[5,384,256]{2,1,0:T(8,128)(2,1)S(1)} %bitcast.698), channel_id=1, source_target_pairs={{0,32},{2,34},{32,64},{34,66},{64,96},{66,98},{96,0},{98,2},{1,33}... | collective-permute-start | bytes 2949128 | tf_op jit(solution)/shard_map/ppermute | solution.py:85
  382.2 72.3 %collective-permute-start.8 = (bf16[5,384,256]{2,1,0:T(8,128)(2,1)S(1)}, bf16[5,384,256]{2,1,0:T(8,128)(2,1)S(1)}, u32[]{:S(2)}, u32[]{:S(2)}) collective-permute-start(bf16[5,384,256]{2,1,0:T(8,128)(2,1)S(1)} %bitcast.699), channel_id=1, source_target_pairs={{0,64},{2,66},{32,96},{34,98},{64,0},{66,2},{96,32},{98,34},{1,65}... | collective-permute-start | bytes 2949128 | tf_op jit(solution)/shard_map/ppermute | solution.py:85
  392.7 62.5 %collective-permute-start.9 = (bf16[5,384,256]{2,1,0:T(8,128)(2,1)S(1)}, bf16[5,384,256]{2,1,0:T(8,128)(2,1)S(1)}, u32[]{:S(2)}, u32[]{:S(2)}) collective-permute-start(bf16[5,384,256]{2,1,0:T(8,128)(2,1)S(1)} %bitcast.700), channel_id=1, source_target_pairs={{0,96},{2,98},{32,0},{34,2},{64,32},{66,34},{96,64},{98,66},{1,97}... | collective-permute-start | bytes 2949128 | tf_op jit(solution)/shard_map/ppermute | solution.py:85
  403.3 39.0 %collective-permute-start.2 = (bf16[5,128,384]{2,1,0:T(8,128)(2,1)S(1)}, bf16[5,128,384]{2,1,0:T(8,128)(2,1)S(1)}, u32[]{:S(2)}, u32[]{:S(2)}) collective-permute-start(bf16[5,128,384]{2,1,0:T(8,128)(2,1)S(1)} %bitcast.724), channel_id=1, source_target_pairs={{0,96},{2,98},{32,0},{34,2},{64,32},{66,34},{96,64},{98,66},{1,97}... | collective-permute-start | bytes 1474568 | tf_op jit(solution)/shard_map/ppermute | solution.py:85
  442.3 45.0 %collective-permute-start.10 = (bf16[5,384,256]{2,1,0:T(8,128)(2,1)S(1)}, bf16[5,384,256]{2,1,0:T(8,128)(2,1)S(1)}, u32[]{:S(2)}, u32[]{:S(2)}) collective-permute-start(bf16[5,384,256]{2,1,0:T(8,128)(2,1)S(1)} %bitcast.701), channel_id=1, source_target_pairs={{0,2},{2,0},{32,34},{34,32},{64,66},{66,64},{96,98},{98,96},{1,3},... | collective-permute-start | bytes 2949128 | tf_op jit(solution)/shard_map/ppermute | solution.py:85
  442.8 71.7 %collective-permute-start.11 = (bf16[5,384,256]{2,1,0:T(8,128)(2,1)S(1)}, bf16[5,384,256]{2,1,0:T(8,128)(2,1)S(1)}, u32[]{:S(2)}, u32[]{:S(2)}) collective-permute-start(bf16[5,384,256]{2,1,0:T(8,128)(2,1)S(1)} %bitcast.702), channel_id=1, source_target_pairs={{0,34},{2,32},{32,66},{34,64},{64,98},{66,96},{96,2},{98,0},{1,35}... | collective-permute-start | bytes 2949128 | tf_op jit(solution)/shard_map/ppermute | solution.py:85
  454.5 90.7 %collective-permute-start.12 = (bf16[5,384,256]{2,1,0:T(8,128)(2,1)S(1)}, bf16[5,384,256]{2,1,0:T(8,128)(2,1)S(1)}, u32[]{:S(2)}, u32[]{:S(2)}) collective-permute-start(bf16[5,384,256]{2,1,0:T(8,128)(2,1)S(1)} %bitcast.703), channel_id=1, source_target_pairs={{0,66},{2,64},{32,98},{34,96},{64,2},{66,0},{96,34},{98,32},{1,67}... | collective-permute-start | bytes 2949128 | tf_op jit(solution)/shard_map/ppermute | solution.py:85
  455.2 89.9 %collective-permute-start.13 = (bf16[5,384,256]{2,1,0:T(8,128)(2,1)S(1)}, bf16[5,384,256]{2,1,0:T(8,128)(2,1)S(1)}, u32[]{:S(2)}, u32[]{:S(2)}) collective-permute-start(bf16[5,384,256]{2,1,0:T(8,128)(2,1)S(1)} %bitcast.704), channel_id=1, source_target_pairs={{0,98},{2,96},{32,2},{34,0},{64,34},{66,32},{96,66},{98,64},{1,99}... | collective-permute-start | bytes 2949128 | tf_op jit(solution)/shard_map/ppermute | solution.py:85
  599.9 14.0 %copy-start.2 = (f32[5,1536,2,8,26]{1,3,4,0,2:T(8,128)S(1)}, f32[5,1536,2,8,26]{1,3,4,0,2:T(8,128)}, u32[]{:S(2)}) copy-start(f32[5,1536,2,8,26]{1,3,4,0,2:T(8,128)} %copy.327) | copy-start | bytes 38338564
  603.3 10.5 %collective-permute-start.15 = (f32[8,5,26,1536]{3,0,2,1:T(8,128)S(1)}, f32[8,5,26,1536]{3,0,2,1:T(8,128)}, u32[]{:S(2)}, u32[]{:S(2)}) collective-permute-start(f32[8,5,26,1536]{3,0,2,1:T(8,128)S(1)} %slice_bitcast_fusion), channel_id=1, source_target_pairs={{0,1},{1,0},{2,3},{3,2},{4,5},{5,4},{6,7},{7,6},{8,9},{9,8},{10,11... | collective-permute-start | bytes 19169288 | tf_op jit(solution)/shard_map/ppermute | solution.py:211
  617.8 8.7 %copy-start.73 = (bf16[128,8]{0,1:T(8,128)(2,1)S(1)}, bf16[128,8]{0,1:T(8,128)(2,1)}, u32[]{:S(2)}) copy-start(bf16[128,8]{0,1:T(8,128)(2,1)} %param.23) | copy-start | bytes 6148
  617.8 8.8 %copy-start.67 = (s32[1024,1]{0,1:T(1,128)S(1)}, s32[1024,1]{0,1:T(1,128)}, u32[]{:S(2)}) copy-start(s32[1024,1]{0,1:T(1,128)} %copy-done.66) | copy-start | bytes 12292
  620.9 61.9 %all-to-all-start.1 = ((bf16[8,5,26,1536]{3,2,1,0:T(8,128)(2,1)}), bf16[8,5,26,1536]{3,2,1,0:T(8,128)(2,1)}, u32[]{:S(2)}, u32[]{:S(2)}) async-start(bf16[8,5,26,1536]{3,2,1,0:T(8,128)(2,1)} %copy.278), calls=%async_computation.1 | async-start | bytes 7864320 | tf_op jit(solution)/shard_map/all_to_all | solution.py:212
  689.0 18.0 %copy-start.1 = (bf16[1536,512]{1,0:T(8,128)(2,1)S(1)}, bf16[1536,512]{1,0:T(8,128)(2,1)}, u32[]{:S(2)}) copy-start(bf16[1536,512]{1,0:T(8,128)(2,1)} %param.16) | copy-start | bytes 4718596
  699.7 6.5 copy-start.5
  (45 other events, 121.4 us)
Sparse Core Ops, SparseCore 0:
  10.3 47.4 all-gather.5
  60.6 52.1 all-gather.3

commit v6 on v5

--- a/solution.py
+++ b/solution.py
@@ -1,6 +1,8 @@
 import jax
 import jax.numpy as jnp
 from jax import lax
+from jax.experimental import pallas as pl
+from jax.experimental.pallas import tpu as pltpu
 from jax.sharding import Mesh, PartitionSpec as P
 
 
@@ -15,7 +17,6 @@
 residual_scale = 1.0
 norm_eps = 1e-06
 neg_fill = -1e30
-key_block = 512
 EXP_AXES = ("x", "zhi", "zlo", "core")
 
 
@@ -42,29 +43,70 @@
     return turned.reshape(row_count, head_count * head_dim).astype(jnp.bfloat16)
 
 
-def attend_block(running, queries, block_rows, visible, kv_width):
-    run_max, run_sum, run_acc = running
-    kv_heads = run_max.shape[0]
-    head_dim = run_acc.shape[-1]
-    block_size = block_rows.shape[0]
-    key_heads = block_rows[:, :kv_width].reshape(block_size, kv_heads, head_dim)
-    value_heads = block_rows[:, kv_width:].reshape(block_size, kv_heads, head_dim)
-    scores = (
-        jnp.einsum("tkgd,rkd->kgtr", queries, key_heads, preferred_element_type=jnp.float32)
-        * attn_scale
-    )
-    scores = jnp.where(visible[None, None], scores, neg_fill)
-    new_max = jnp.maximum(run_max, jnp.max(scores, axis=-1))
-    weights = jnp.where(visible[None, None], jnp.exp(scores - new_max[..., None]), 0.0)
-    factor = jnp.exp(run_max - new_max)
-    new_sum = run_sum * factor + jnp.sum(weights, axis=-1)
-    new_acc = run_acc * factor[..., None] + jnp.einsum(
-        "kgtr,rkd->kgtd",
-        weights.astype(jnp.bfloat16),
-        value_heads,
-        preferred_element_type=jnp.float32,
-    )
-    return (new_max, new_sum, new_acc)
+INTERPRET = False
+
+
+def attend(query, cache_all, new_all, bounds, kv_heads, group_size):
+    rows = query.shape[0]
+    heads_per_step = 128 // HEAD_DIM
+    steps = kv_heads // heads_per_step
+    q_width = heads_per_step * group_size * HEAD_DIM
+    cache_count = cache_all.shape[0]
+    new_count = new_all.shape[0]
+
+    def kernel(bounds_ref, q_ref, kc_ref, vc_ref, kn_ref, vn_ref, o_ref):
+        length = bounds_ref[0]
+        first = bounds_ref[1]
+        seen_cache = lax.broadcasted_iota(jnp.int32, (rows, cache_count), 1) < length
+        seen_new = lax.broadcasted_iota(jnp.int32, (rows, new_count), 1) <= (
+            lax.broadcasted_iota(jnp.int32, (rows, new_count), 0) + first
+        )
+        pieces = []
+        for hh in range(heads_per_step):
+            lanes = slice(hh * HEAD_DIM, (hh + 1) * HEAD_DIM)
+            kc = kc_ref[:, lanes]
+            vc = vc_ref[:, lanes]
+            kn = kn_ref[:, lanes]
+            vn = vn_ref[:, lanes]
+            for g in range(group_size):
+                col = (hh * group_size + g) * HEAD_DIM
+                q = q_ref[:, col : col + HEAD_DIM]
+                dims = (((1,), (1,)), ((), ()))
+                s_c = lax.dot_general(q, kc, dims, preferred_element_type=jnp.float32) * attn_scale
+                s_n = lax.dot_general(q, kn, dims, preferred_element_type=jnp.float32) * attn_scale
+                s_c = jnp.where(seen_cache, s_c, neg_fill)
+                s_n = jnp.where(seen_new, s_n, neg_fill)
+                top = jnp.maximum(
+                    jnp.max(s_c, axis=1, keepdims=True), jnp.max(s_n, axis=1, keepdims=True)
+                )
+                p_c = jnp.where(seen_cache, jnp.exp(s_c - top), 0.0)
+                p_n = jnp.where(seen_new, jnp.exp(s_n - top), 0.0)
+                total = jnp.sum(p_c, axis=1, keepdims=True) + jnp.sum(p_n, axis=1, keepdims=True)
+                acc = jnp.dot(p_c.astype(jnp.bfloat16), vc, preferred_element_type=jnp.float32)
+                acc = acc + jnp.dot(p_n.astype(jnp.bfloat16), vn, preferred_element_type=jnp.float32)
+                pieces.append((acc / total).astype(jnp.bfloat16))
+        o_ref[...] = jnp.concatenate(pieces, axis=1)
+
+    value_block = kv_heads * HEAD_DIM // 128
+    grid_spec = pltpu.PrefetchScalarGridSpec(
+        num_scalar_prefetch=1,
+        grid=(steps,),
+        in_specs=[
+            pl.BlockSpec((rows, q_width), lambda i, b: (0, i)),
+            pl.BlockSpec((cache_count, 128), lambda i, b: (0, i)),
+            pl.BlockSpec((cache_count, 128), lambda i, b: (0, value_block + i)),
+            pl.BlockSpec((new_count, 128), lambda i, b: (0, i)),
+            pl.BlockSpec((new_count, 128), lambda i, b: (0, value_block + i)),
+        ],
+        out_specs=pl.BlockSpec((rows, q_width), lambda i, b: (0, i)),
+    )
+    return pl.pallas_call(
+        kernel,
+        grid_spec=grid_spec,
+        out_shape=jax.ShapeDtypeStruct((rows, query.shape[1]), jnp.bfloat16),
+        compiler_params=pltpu.CompilerParams(dimension_semantics=("arbitrary",)),
+        interpret=INTERPRET,
+    )(bounds, query, cache_all, cache_all, new_all, new_all)
 
 
 def spread_pieces(local, width_axis):
@@ -138,44 +180,12 @@
     )
     values_new = jnp.dot(normed, w_value, preferred_element_type=jnp.float32).astype(jnp.bfloat16)
     new_kv = jnp.concatenate([keys_new, values_new], axis=1)
-    queries = query.reshape(rows_here, kv_heads, group_size, HEAD_DIM)
-    initial = (
-        jnp.full((kv_heads, group_size, rows_here), neg_fill, jnp.float32),
-        jnp.zeros((kv_heads, group_size, rows_here), jnp.float32),
-        jnp.zeros((kv_heads, group_size, rows_here, HEAD_DIM), jnp.float32),
-    )
-    running = initial
-    for offset in range(0, cache_all.shape[0], key_block):
-      block_size = min(key_block, cache_all.shape[0] - offset)
-      cache_pos = offset + jnp.arange(block_size, dtype=jnp.int32)
-      running = attend_block(
-          running,
-          queries,
-          cache_all[offset : offset + block_size],
-          jnp.broadcast_to((cache_pos < length)[None, :], (rows_here, block_size)),
-          kv_width,
-      )
     new_all = lax.all_gather(new_kv, EXP_AXES, axis=0, tiled=True)
     gate_up_local, down_local, new_all = lax.optimization_barrier((w_gate_up[0], w_down[0], new_all))
     gate_up_full = spread_pieces(gate_up_local, 1)
     down_full = spread_pieces(down_local, 2)
-    for offset in range(0, new_all.shape[0], key_block):
-        block_size = min(key_block, new_all.shape[0] - offset)
-        new_pos = offset + jnp.arange(block_size, dtype=jnp.int32)
-        running = attend_block(
-            running,
-            queries,
-            new_all[offset : offset + block_size],
-            new_pos[None, :] <= query_pos[:, None],
-            kv_width,
-        )
-    _, run_sum, run_acc = running
-    context = (
-        (run_acc / run_sum[..., None])
-        .transpose(2, 0, 1, 3)
-        .reshape(rows_here, head_count * HEAD_DIM)
-        .astype(jnp.bfloat16)
-    )
+    bounds = jnp.stack([length, position_exp * rows_here]).astype(jnp.int32)
+    context = attend(query, cache_all, new_all, bounds, kv_heads, group_size)
     projected = jnp.dot(context, w_out, preferred_element_type=jnp.float32)
     attended = (hidden_in.astype(jnp.float32) + residual_scale * projected).astype(jnp.bfloat16)
     moe_in = rms_scale(attended, moe_gain)

time: 726 us -> 601 us (0.83)
  matrix products: 123 us -> 38.3 us
  other arithmetic: 66.5 us -> 21 us
  Pallas kernels: 0 us -> 41.8 us
  local copies, waits for them, and re-layouts: 113 us -> 72.3 us
  waiting for transfers between devices: 351 us -> 366 us
    dot_general x22 -> x0, matrix products: 86.9 us -> none  [the longest x11 44.4 us: attend_block(): jnp.einsum('kgtr,rkd->kgtd', weights.astype(jnp.bfloat16), value_heads, p...]
    pallas_call x0 -> x1, Pallas kernels: none -> 41.8 us  [attend(): pl.pallas_call(kernel, grid_spec=grid_spec, out_shape=jax.ShapeDtypeStruc...]
    reduce_sum x11 -> x0, other arithmetic: 40.8 us -> none  [attend_block(): new_sum = run_sum * factor + jnp.sum(weights, axis=-1)]
    slice x24 -> x0, local copies, waits for them, and re-layouts: 39.3 us -> none  [the longest x13 21.2 us: attend_block(): block_rows[:, kv_width:].reshape(block_size, kv_heads, head_dim)]
    all_gather x1, waiting for transfers between devices: 27.6 us -> 46.7 us  [shards(): cache_all = lax.all_gather(cache_rows, EXP_AXES, axis=0, tiled=True)]
    ppermute x14, waiting for transfers between devices: 168 us -> 154 us  [spread_pieces(): chunks.append(lax.ppermute(local, ('req', 'zlo'), perm))]
    all_gather x1, waiting for transfers between devices: 32.3 us -> 42.5 us  [shards(): new_all = lax.all_gather(new_kv, EXP_AXES, axis=0, tiled=True)]
    ppermute x14, starting transfers between devices: 34.1 us -> 24.8 us  [spread_pieces(): chunks.append(lax.ppermute(local, ('req', 'zlo'), perm))]
  transfers between devices with their start and end apart: 20 -> 20, of which waited for: 13 -> 11; matrix products, arithmetic and copies ran while one was open for 8% -> 5% of each run, Pallas kernels for 0% -> 0%
where the time goes in v6:
time: 601 us; the launch traced here: 594 us
  waiting for transfers between devices  366 us (61%)
  local copies, waits for them, and re-layouts  72.3 us (12%)
  Pallas kernels  41.8 us (7%)
  starting transfers between devices  39 us (6%)
  matrix products  38.3 us (6%)
  other arithmetic  21 us (3%)
  between operations  15.7 us (3%)
    ppermute x14, waiting for transfers between devices, spread_pieces(): chunks.append(lax.ppermute(local, ('req', 'zlo'), perm))  154 us
    all_to_all x1, waiting for transfers between devices, shards(): lax.all_to_all(computed, ('x', 'zhi'), split_axis=0, concat_axis=0, tiled...  56.2 us
    all_to_all x1, waiting for transfers between devices, shards(): lax.all_to_all(outgoing, ('x', 'zhi'), split_axis=0, concat_axis=0, tiled...  54.9 us
    all_gather x1, waiting for transfers between devices, shards(): cache_all = lax.all_gather(cache_rows, EXP_AXES, axis=0, tiled=True)  46.7 us
    all_gather x1, waiting for transfers between devices, shards(): new_all = lax.all_gather(new_kv, EXP_AXES, axis=0, tiled=True)  42.5 us
    pallas_call x1, Pallas kernels, attend(): pl.pallas_call(kernel, grid_spec=grid_spec, out_shape=jax.ShapeDtypeStruc...  41.8 us
    ppermute x14, starting transfers between devices, spread_pieces(): chunks.append(lax.ppermute(local, ('req', 'zlo'), perm))  24.8 us
    reduce_sum x1, local copies, waits for them, and re-layouts, shards(): computed = jnp.sum(computed, axis=2, dtype=jnp.float32)  18.4 us
  transfers between devices with their start and end apart: 20, of which 11 were waited for; matrix products, arithmetic and copies ran while one was open for 5% of the time, Pallas kernels for 0%

profile of v6, /device:TPU:0, one launch (start us, length us, event | category | flops | bytes accessed | tf_op | source)
XLA Modules:
  0.0 593.9 jit_solution(18019295072511579484)
XLA Ops:
  8.0 0.7 convert_element_type.77
  8.7 1.2 fusion.18
  9.9 0.1 multiply_cosine_fusion
  10.1 1.8 fusion.37
  12.0 2.0 convolution_convert_fusion
  14.0 0.7 pad_maximum_fusion.1
  14.8 0.7 all-gather.6.cloned.1.call-update
  15.5 4.3 fusion.39
  20.0 0.9 copy.91.q_ref
  21.5 0.6 fusion.17
  22.1 4.8 scatter_custom_fusion
  27.2 0.6 pad_add_fusion.bounds_ref
  27.8 42.5 %all-gather.4.cloned.1.call-done.kn_ref.vn_ref = bf16[4096,1024]{1,0:T(8,128)(2,1)} async-done(((bf16[128,1024]{1,0:T(8,128)(2,1)}), bf16[4096,1024]{1,0:T(8,128)(2,1)}) %all-gather.4.cloned.1.call-update) | async-done | bytes 8388624 | tf_op jit(solution)/shard_map/all_gather | solution.py:183
  70.3 46.7 %all-gather.6.cloned.1.call-done = bf16[1,1536,1024]{2,1,0:T(8,128)(2,1)} async-done(((bf16[1,48,1024]{2,1,0:T(8,128)(2,1)}), bf16[1,1536,1024]{2,1,0:T(8,128)(2,1)}) %all-gather.6.cloned.1.call-update) | async-done | bytes 3145744 | tf_op jit(solution)/shard_map/all_gather | solution.py:166
  117.0 41.8 %shard_map.140 = bf16[128,1536]{1,0:T(8,128)(2,1)} custom-call(s32[2]{0:T(128)} %pad_add_fusion.bounds_ref, bf16[128,1536]{1,0:T(8,128)(2,1)} %copy.91.q_ref, bf16[1536,1024]{1,0:T(8,128)(2,1)} %bitcast.86, bf16[1536,1024]{1,0:T(8,128)(2,1)} %bitcast.87, bf16[4096,1024]{1,0:T(8,128)(2,1)} %all-gather.4.cloned.1.call-done.kn_ref.vn_ref, ...), custom_call_target="tpu_custom_call" | custom-call | tf_op jit(solution)/shard_map/pallas_call | solution.py:103
  158.8 3.3 fusion.21
  162.2 0.2 fusion.23
  162.4 0.6 gather_fusion
  163.1 5.2 gather_fusion.1
  168.3 5.5 reshape.254
  173.7 5.1 all-to-all-start
  178.9 1.6 collective-permute-start
  180.5 54.9 %all-to-all-done = bf16[8,5,26,1536]{3,2,1,0:T(8,128)(2,1)} async-done(((bf16[8,5,26,1536]{3,2,1,0:T(8,128)(2,1)}), bf16[8,5,26,1536]{3,2,1,0:T(8,128)(2,1)}, u32[]{:S(2)}, u32[]{:S(2)}) %all-to-all-start) | async-done | bytes 3194912 | tf_op jit(solution)/shard_map/all_to_all | solution.py:208
  235.4 3.9 copy.98
  239.4 3.1 collective-permute-start.1
  242.5 1.1 collective-permute-start.2
  243.6 1.1 collective-permute-start.3
  244.7 1.3 collective-permute-start.4
  246.0 9.1 %collective-permute-done.1 = bf16[5,128,384]{2,1,0:T(8,128)(2,1)S(1)} collective-permute-done((bf16[5,128,384]{2,1,0:T(8,128)(2,1)S(1)}, bf16[5,128,384]{2,1,0:T(8,128)(2,1)S(1)}, u32[]{:S(2)}, u32[]{:S(2)}) %collective-permute-start.1) | collective-permute-done | bytes 491552 | tf_op jit(solution)/shard_map/ppermute | solution.py:127
  255.1 3.5 collective-permute-start.5
  258.6 7.1 %collective-permute-done.2 = bf16[5,128,384]{2,1,0:T(8,128)(2,1)S(1)} collective-permute-done((bf16[5,128,384]{2,1,0:T(8,128)(2,1)S(1)}, bf16[5,128,384]{2,1,0:T(8,128)(2,1)S(1)}, u32[]{:S(2)}, u32[]{:S(2)}) %collective-permute-start.2) | collective-permute-done | bytes 491552 | tf_op jit(solution)/shard_map/ppermute | solution.py:127
  265.7 1.3 collective-permute-start.7
  267.0 10.6 %collective-permute-done.3 = bf16[5,128,384]{2,1,0:T(8,128)(2,1)S(1)} collective-permute-done((bf16[5,128,384]{2,1,0:T(8,128)(2,1)S(1)}, bf16[5,128,384]{2,1,0:T(8,128)(2,1)S(1)}, u32[]{:S(2)}, u32[]{:S(2)}) %collective-permute-start.3) | collective-permute-done | bytes 491552 | tf_op jit(solution)/shard_map/ppermute | solution.py:127
  277.7 3.6 collective-permute-start.9
  281.3 1.0 collective-permute-start.6
  282.3 46.6 %collective-permute-done.6 = bf16[5,128,384]{2,1,0:T(8,128)(2,1)S(1)} collective-permute-done((bf16[5,128,384]{2,1,0:T(8,128)(2,1)S(1)}, bf16[5,128,384]{2,1,0:T(8,128)(2,1)S(1)}, u32[]{:S(2)}, u32[]{:S(2)}) %collective-permute-start.6) | collective-permute-done | bytes 491552 | tf_op jit(solution)/shard_map/ppermute | solution.py:127
  328.9 1.0 collective-permute-start.10
  329.9 1.9 collective-permute-start.11
  331.8 3.1 collective-permute-start.12
  334.9 1.3 collective-permute-start.13
  336.2 1.2 maximum_bitcast_fusion.12
  337.4 1.5 maximum_bitcast_fusion.13
  338.9 2.3 maximum_bitcast_fusion.6
  341.2 73.0 %collective-permute-done.10 = bf16[5,384,256]{2,1,0:T(8,128)(2,1)S(1)} collective-permute-done((bf16[5,384,256]{2,1,0:T(8,128)(2,1)S(1)}, bf16[5,384,256]{2,1,0:T(8,128)(2,1)S(1)}, u32[]{:S(2)}, u32[]{:S(2)}) %collective-permute-start.10) | collective-permute-done | bytes 983072 | tf_op jit(solution)/shard_map/ppermute | solution.py:127
  414.2 7.8 %collective-permute-done.12 = bf16[5,384,256]{2,1,0:T(8,128)(2,1)S(1)} collective-permute-done((bf16[5,384,256]{2,1,0:T(8,128)(2,1)S(1)}, bf16[5,384,256]{2,1,0:T(8,128)(2,1)S(1)}, u32[]{:S(2)}, u32[]{:S(2)}) %collective-permute-start.12) | collective-permute-done | bytes 983072 | tf_op jit(solution)/shard_map/ppermute | solution.py:127
  422.0 2.3 maximum_bitcast_fusion.7
  424.3 4.4 copy.123
  428.8 3.1 copy.122
  431.9 12.0 %fusion.12 = f32[2,8,2,5,26,256]{5,4,1,0,2,3:T(8,128)} fusion(bf16[1,8,5,26,1536]{4,3,1,0,2:T(8,128)(2,1)} %bitcast.88, bf16[1,8,5,26,1536]{4,3,1,0,2:T(8,128)(2,1)} %bitcast.89, bf16[1,5,1536,256]{3,2,0,1:T(8,128)(2,1)} %maximum_bitcast_fusion.7, bf16[1,5,1536,256]{3,2,0,1:T(8,128)(2,1)} %maximum_bitcast_fusion.6), kind=kOutput, calls=%fused_computation.32 | convolution fusion | flops 3300065280 | bytes 18513920 | tf_op jit(solution)/shard_map/askmd,pkdf->aspkmf/dot_general | solution.py:211
  443.9 14.3 %convert_reduce_fusion = f32[5,1536,2,8,26]{1,4,3,2,0:T(8,128)} fusion(bf16[1,5,128,1536]{3,2,1,0:T(8,128)(2,1)} %maximum_bitcast_fusion.13, bf16[1,5,128,1536]{3,2,1,0:T(8,128)(2,1)S(1)} %maximum_bitcast_fusion.12, f32[2,8,2,5,26,256]{5,4,1,0,2,3:T(8,128)} %fusion.12), kind=kOutput, calls=%fused_computation.5 | convolution fusion | flops 1662812160 | bytes 20971520 | tf_op jit(solution)/shard_map/aspkmf,pkfd->aspkmd/dot_general | solution.py:217
  458.2 18.4 %copy.121 = f32[5,1536,2,8,26]{1,3,4,0,2:T(8,128)} copy(f32[5,1536,2,8,26]{1,4,3,2,0:T(8,128)} %convert_reduce_fusion) | data formatting | bytes 25559040 | tf_op jit(solution)/shard_map/reduce_sum | solution.py:220
  476.6 3.4 slice_bitcast_fusion
  480.1 10.4 %collective-permute-done.15 = f32[8,5,26,1536]{3,0,2,1:T(8,128)} collective-permute-done((f32[8,5,26,1536]{3,0,2,1:T(8,128)S(1)}, f32[8,5,26,1536]{3,0,2,1:T(8,128)}, u32[]{:S(2)}, u32[]{:S(2)}) %collective-permute-start.15) | collective-permute-done | bytes 6389792 | tf_op jit(solution)/shard_map/ppermute | solution.py:221
  490.5 3.9 fusion.6
  494.5 3.0 copy.102
  497.5 8.7 %all-to-all-start.1 = ((bf16[8,5,26,1536]{3,2,1,0:T(8,128)(2,1)}), bf16[8,5,26,1536]{3,2,1,0:T(8,128)(2,1)}, u32[]{:S(2)}, u32[]{:S(2)}) async-start(bf16[8,5,26,1536]{3,2,1,0:T(8,128)(2,1)} %copy.102), calls=%async_computation.1 | async-start | bytes 7864320 | tf_op jit(solution)/shard_map/all_to_all | solution.py:222
  506.3 56.2 %all-to-all-done.1 = bf16[8,5,26,1536]{3,2,1,0:T(8,128)(2,1)} async-done(((bf16[8,5,26,1536]{3,2,1,0:T(8,128)(2,1)}), bf16[8,5,26,1536]{3,2,1,0:T(8,128)(2,1)}, u32[]{:S(2)}, u32[]{:S(2)}) %all-to-all-start.1) | async-done | bytes 3194912 | tf_op jit(solution)/shard_map/all_to_all | solution.py:222
  562.5 6.2 %reshape.244 = f32[1040,1536]{1,0:T(8,128)} reshape(bf16[8,5,26,1536]{3,2,1,0:T(8,128)(2,1)} %all-to-all-done.1) | data formatting | bytes 9584640 | tf_op jit(solution)/shard_map/reshape | solution.py:223
  568.7 10.6 %gather_fusion.2 = f32[1024,1536]{1,0:T(8,128)} fusion(f32[1040,1536]{1,0:T(8,128)} %reshape.244, s32[1024]{0:T(1024)S(1)} %broadcast_clamp_fusion), kind=kCustom, calls=%fused_computation.2 | custom fusion | bytes 12587008 | tf_op jit(solution)/shard_map/gather | solution.py:224
  579.3 5.2 fusion.7
  584.5 0.3 copy.104
  584.8 0.3 copy.105
  585.0 0.6 gather_fusion.3
  585.7 0.8 fusion.24
  (71 shorter events, 1.8 us)
Async XLA Ops:
  7.2 2.9 copy-start
  7.2 8.3 %copy-start.3 = (bf16[128,1536]{1,0:T(8,128)(2,1)S(1)}, bf16[128,1536]{1,0:T(8,128)(2,1)}, u32[]{:S(2)}) copy-start(bf16[128,1536]{1,0:T(8,128)(2,1)} %param.13) | copy-start | bytes 1179652
  7.2 63.1 %all-gather.4.cloned.1.call-start = ((), (), s32[]{:S(2)}) async-start(), calls=%async_computation.2 | async-start | bytes 8650752 | tf_op jit(solution)/shard_map/all_gather | solution.py:183
  14.8 102.2 %all-gather.6.cloned.1.call-start = ((), (), s32[]{:S(2)}) async-start(), calls=%async_computation.3 | async-start | bytes 3244032 | tf_op jit(solution)/shard_map/all_gather | solution.py:166
  15.5 5.5 copy-start.10
  15.5 5.6 copy-start.9
  162.1 0.9 copy-start.4
  173.7 5.2 copy-start.7
  173.7 61.7 %all-to-all-start = ((bf16[8,5,26,1536]{3,2,1,0:T(8,128)(2,1)}), bf16[8,5,26,1536]{3,2,1,0:T(8,128)(2,1)}, u32[]{:S(2)}, u32[]{:S(2)}) async-start(bf16[8,5,26,1536]{3,2,1,0:T(8,128)(2,1)} %reshape.254), calls=%async_computation | async-start | bytes 7864320 | tf_op jit(solution)/shard_map/all_to_all | solution.py:208
  178.9 86.8 %copy-start.6 = (bf16[1,5,384,256]{3,2,1,0:T(8,128)(2,1)S(1)}, bf16[1,5,384,256]{3,2,1,0:T(8,128)(2,1)}, u32[]{:S(2)}) copy-start(bf16[1,5,384,256]{3,2,1,0:T(8,128)(2,1)} %param.24) | copy-start | bytes 2949124
  178.9 65.8 %collective-permute-start = (bf16[5,128,384]{2,1,0:T(8,128)(2,1)S(1)}, bf16[5,128,384]{2,1,0:T(8,128)(2,1)S(1)}, u32[]{:S(2)}, u32[]{:S(2)}) collective-permute-start(bf16[5,128,384]{2,1,0:T(8,128)(2,1)S(1)} %bitcast.109), channel_id=1, source_target_pairs={{0,32},{2,34},{32,64},{34,66},{64,96},{66,98},{96,0},{98,2},{1,33}... | collective-permute-start | bytes 1474568 | tf_op jit(solution)/shard_map/ppermute | solution.py:127
  239.3 189.5 %collective-permute-start.14 = (bf16[8,5,26,1536]{3,0,2,1:T(8,128)(2,1)S(1)}, bf16[8,5,26,1536]{3,0,2,1:T(8,128)(2,1)S(1)}, u32[]{:S(2)}, u32[]{:S(2)}) collective-permute-start(bf16[8,5,26,1536]{3,0,2,1:T(8,128)(2,1)S(1)} %copy.98), channel_id=1, source_target_pairs={{0,1},{1,0},{2,3},{3,2},{4,5},{5,4},{6,7},{7,6},{8,9},{9,8},{10,11... | collective-permute-start | bytes 9584648 | tf_op jit(solution)/shard_map/ppermute | solution.py:210
  239.4 15.7 %collective-permute-start.1 = (bf16[5,128,384]{2,1,0:T(8,128)(2,1)S(1)}, bf16[5,128,384]{2,1,0:T(8,128)(2,1)S(1)}, u32[]{:S(2)}, u32[]{:S(2)}) collective-permute-start(bf16[5,128,384]{2,1,0:T(8,128)(2,1)S(1)} %bitcast.110), channel_id=1, source_target_pairs={{0,64},{2,66},{32,96},{34,98},{64,0},{66,2},{96,32},{98,34},{1,65}... | collective-permute-start | bytes 1474568 | tf_op jit(solution)/shard_map/ppermute | solution.py:127
  242.5 23.2 %collective-permute-start.2 = (bf16[5,128,384]{2,1,0:T(8,128)(2,1)S(1)}, bf16[5,128,384]{2,1,0:T(8,128)(2,1)S(1)}, u32[]{:S(2)}, u32[]{:S(2)}) collective-permute-start(bf16[5,128,384]{2,1,0:T(8,128)(2,1)S(1)} %bitcast.111), channel_id=1, source_target_pairs={{0,96},{2,98},{32,0},{34,2},{64,32},{66,34},{96,64},{98,66},{1,97}... | collective-permute-start | bytes 1474568 | tf_op jit(solution)/shard_map/ppermute | solution.py:127
  243.6 34.1 %collective-permute-start.3 = (bf16[5,128,384]{2,1,0:T(8,128)(2,1)S(1)}, bf16[5,128,384]{2,1,0:T(8,128)(2,1)S(1)}, u32[]{:S(2)}, u32[]{:S(2)}) collective-permute-start(bf16[5,128,384]{2,1,0:T(8,128)(2,1)S(1)} %bitcast.112), channel_id=1, source_target_pairs={{0,2},{2,0},{32,34},{34,32},{64,66},{66,64},{96,98},{98,96},{1,3},... | collective-permute-start | bytes 1474568 | tf_op jit(solution)/shard_map/ppermute | solution.py:127
  244.7 90.2 %copy-start.8 = (bf16[5,128,384]{2,1,0:T(8,128)(2,1)}, bf16[5,128,384]{2,1,0:T(8,128)(2,1)S(1)}, u32[]{:S(2)}) copy-start(bf16[5,128,384]{2,1,0:T(8,128)(2,1)S(1)} %collective-permute-done) | copy-start | bytes 1474564
  244.7 33.0 %collective-permute-start.4 = (bf16[5,128,384]{2,1,0:T(8,128)(2,1)S(1)}, bf16[5,128,384]{2,1,0:T(8,128)(2,1)S(1)}, u32[]{:S(2)}, u32[]{:S(2)}) collective-permute-start(bf16[5,128,384]{2,1,0:T(8,128)(2,1)S(1)} %bitcast.113), channel_id=1, source_target_pairs={{0,34},{2,32},{32,66},{34,64},{64,98},{66,96},{96,2},{98,0},{1,35}... | collective-permute-start | bytes 1474568 | tf_op jit(solution)/shard_map/ppermute | solution.py:127
  255.1 26.1 %collective-permute-start.5 = (bf16[5,128,384]{2,1,0:T(8,128)(2,1)S(1)}, bf16[5,128,384]{2,1,0:T(8,128)(2,1)S(1)}, u32[]{:S(2)}, u32[]{:S(2)}) collective-permute-start(bf16[5,128,384]{2,1,0:T(8,128)(2,1)S(1)} %bitcast.114), channel_id=1, source_target_pairs={{0,66},{2,64},{32,98},{34,96},{64,2},{66,0},{96,34},{98,32},{1,67}... | collective-permute-start | bytes 1474568 | tf_op jit(solution)/shard_map/ppermute | solution.py:127
  265.7 64.2 %collective-permute-start.7 = (bf16[5,384,256]{2,1,0:T(8,128)(2,1)S(1)}, bf16[5,384,256]{2,1,0:T(8,128)(2,1)S(1)}, u32[]{:S(2)}, u32[]{:S(2)}) collective-permute-start(bf16[5,384,256]{2,1,0:T(8,128)(2,1)S(1)} %bitcast.100), channel_id=1, source_target_pairs={{0,32},{2,34},{32,64},{34,66},{64,96},{66,98},{96,0},{98,2},{1,33}... | collective-permute-start | bytes 2949128 | tf_op jit(solution)/shard_map/ppermute | solution.py:127
  277.7 54.1 %collective-permute-start.8 = (bf16[5,384,256]{2,1,0:T(8,128)(2,1)S(1)}, bf16[5,384,256]{2,1,0:T(8,128)(2,1)S(1)}, u32[]{:S(2)}, u32[]{:S(2)}) collective-permute-start(bf16[5,384,256]{2,1,0:T(8,128)(2,1)S(1)} %bitcast.101), channel_id=1, source_target_pairs={{0,64},{2,66},{32,96},{34,98},{64,0},{66,2},{96,32},{98,34},{1,65}... | collective-permute-start | bytes 2949128 | tf_op jit(solution)/shard_map/ppermute | solution.py:127
  277.7 57.2 %collective-permute-start.9 = (bf16[5,384,256]{2,1,0:T(8,128)(2,1)S(1)}, bf16[5,384,256]{2,1,0:T(8,128)(2,1)S(1)}, u32[]{:S(2)}, u32[]{:S(2)}) collective-permute-start(bf16[5,384,256]{2,1,0:T(8,128)(2,1)S(1)} %bitcast.102), channel_id=1, source_target_pairs={{0,96},{2,98},{32,0},{34,2},{64,32},{66,34},{96,64},{98,66},{1,97}... | collective-permute-start | bytes 2949128 | tf_op jit(solution)/shard_map/ppermute | solution.py:127
  281.3 47.7 %collective-permute-start.6 = (bf16[5,128,384]{2,1,0:T(8,128)(2,1)S(1)}, bf16[5,128,384]{2,1,0:T(8,128)(2,1)S(1)}, u32[]{:S(2)}, u32[]{:S(2)}) collective-permute-start(bf16[5,128,384]{2,1,0:T(8,128)(2,1)S(1)} %bitcast.115), channel_id=1, source_target_pairs={{0,98},{2,96},{32,2},{34,0},{64,34},{66,32},{96,66},{98,64},{1,99}... | collective-permute-start | bytes 1474568 | tf_op jit(solution)/shard_map/ppermute | solution.py:127
  328.9 85.3 %collective-permute-start.10 = (bf16[5,384,256]{2,1,0:T(8,128)(2,1)S(1)}, bf16[5,384,256]{2,1,0:T(8,128)(2,1)S(1)}, u32[]{:S(2)}, u32[]{:S(2)}) collective-permute-start(bf16[5,384,256]{2,1,0:T(8,128)(2,1)S(1)} %bitcast.103), channel_id=1, source_target_pairs={{0,2},{2,0},{32,34},{34,32},{64,66},{66,64},{96,98},{98,96},{1,3},... | collective-permute-start | bytes 2949128 | tf_op jit(solution)/shard_map/ppermute | solution.py:127
  329.9 84.4 %collective-permute-start.11 = (bf16[5,384,256]{2,1,0:T(8,128)(2,1)S(1)}, bf16[5,384,256]{2,1,0:T(8,128)(2,1)S(1)}, u32[]{:S(2)}, u32[]{:S(2)}) collective-permute-start(bf16[5,384,256]{2,1,0:T(8,128)(2,1)S(1)} %bitcast.104), channel_id=1, source_target_pairs={{0,34},{2,32},{32,66},{34,64},{64,98},{66,96},{96,2},{98,0},{1,35}... | collective-permute-start | bytes 2949128 | tf_op jit(solution)/shard_map/ppermute | solution.py:127
  331.8 90.2 %collective-permute-start.12 = (bf16[5,384,256]{2,1,0:T(8,128)(2,1)S(1)}, bf16[5,384,256]{2,1,0:T(8,128)(2,1)S(1)}, u32[]{:S(2)}, u32[]{:S(2)}) collective-permute-start(bf16[5,384,256]{2,1,0:T(8,128)(2,1)S(1)} %bitcast.105), channel_id=1, source_target_pairs={{0,66},{2,64},{32,98},{34,96},{64,2},{66,0},{96,34},{98,32},{1,67}... | collective-permute-start | bytes 2949128 | tf_op jit(solution)/shard_map/ppermute | solution.py:127
  334.9 87.1 %collective-permute-start.13 = (bf16[5,384,256]{2,1,0:T(8,128)(2,1)S(1)}, bf16[5,384,256]{2,1,0:T(8,128)(2,1)S(1)}, u32[]{:S(2)}, u32[]{:S(2)}) collective-permute-start(bf16[5,384,256]{2,1,0:T(8,128)(2,1)S(1)} %bitcast.106), channel_id=1, source_target_pairs={{0,98},{2,96},{32,2},{34,0},{64,34},{66,32},{96,66},{98,64},{1,99}... | collective-permute-start | bytes 2949128 | tf_op jit(solution)/shard_map/ppermute | solution.py:127
  476.6 14.0 %copy-start.2 = (f32[5,1536,2,8,26]{1,3,4,0,2:T(8,128)S(1)}, f32[5,1536,2,8,26]{1,3,4,0,2:T(8,128)}, u32[]{:S(2)}) copy-start(f32[5,1536,2,8,26]{1,3,4,0,2:T(8,128)} %copy.121) | copy-start | bytes 38338564
  480.0 10.5 %collective-permute-start.15 = (f32[8,5,26,1536]{3,0,2,1:T(8,128)S(1)}, f32[8,5,26,1536]{3,0,2,1:T(8,128)}, u32[]{:S(2)}, u32[]{:S(2)}) collective-permute-start(f32[8,5,26,1536]{3,0,2,1:T(8,128)S(1)} %slice_bitcast_fusion), channel_id=1, source_target_pairs={{0,1},{1,0},{2,3},{3,2},{4,5},{5,4},{6,7},{7,6},{8,9},{9,8},{10,11... | collective-permute-start | bytes 19169288 | tf_op jit(solution)/shard_map/ppermute | solution.py:221
  497.5 8.7 %copy-start.11 = (bf16[128,8]{0,1:T(8,128)(2,1)S(1)}, bf16[128,8]{0,1:T(8,128)(2,1)}, u32[]{:S(2)}) copy-start(bf16[128,8]{0,1:T(8,128)(2,1)} %param.23) | copy-start | bytes 6148
  497.5 65.1 %all-to-all-start.1 = ((bf16[8,5,26,1536]{3,2,1,0:T(8,128)(2,1)}), bf16[8,5,26,1536]{3,2,1,0:T(8,128)(2,1)}, u32[]{:S(2)}, u32[]{:S(2)}) async-start(bf16[8,5,26,1536]{3,2,1,0:T(8,128)(2,1)} %copy.102), calls=%async_computation.1 | async-start | bytes 7864320 | tf_op jit(solution)/shard_map/all_to_all | solution.py:222
  579.3 7.3 %copy-start.1 = (bf16[1536,512]{1,0:T(8,128)(2,1)S(1)}, bf16[1536,512]{1,0:T(8,128)(2,1)}, u32[]{:S(2)}) copy-start(bf16[1536,512]{1,0:T(8,128)(2,1)} %param.16) | copy-start | bytes 4718596
  584.5 1.3 copy-start.5
Sparse Core Ops, SparseCore 0:
  14.9 55.3 all-gather.3
  72.5 44.4 all-gather.5

commit v7 on v6

--- a/solution.py
+++ b/solution.py
@@ -46,44 +46,31 @@
 INTERPRET = False
 
 
-def attend(query, cache_all, new_all, bounds, kv_heads, group_size):
+def attend(query, keys, limit, bounds, kv_heads, group_size):
     rows = query.shape[0]
     heads_per_step = 128 // HEAD_DIM
     steps = kv_heads // heads_per_step
     q_width = heads_per_step * group_size * HEAD_DIM
-    cache_count = cache_all.shape[0]
-    new_count = new_all.shape[0]
-
-    def kernel(bounds_ref, q_ref, kc_ref, vc_ref, kn_ref, vn_ref, o_ref):
-        length = bounds_ref[0]
-        first = bounds_ref[1]
-        seen_cache = lax.broadcasted_iota(jnp.int32, (rows, cache_count), 1) < length
-        seen_new = lax.broadcasted_iota(jnp.int32, (rows, new_count), 1) <= (
-            lax.broadcasted_iota(jnp.int32, (rows, new_count), 0) + first
-        )
+    key_count = keys.shape[0]
+
+    def kernel(bounds_ref, lim_ref, q_ref, k_ref, v_ref, o_ref):
+        first = bounds_ref[0]
+        seen = lim_ref[...] <= lax.broadcasted_iota(jnp.int32, (rows, key_count), 0) + first
         pieces = []
         for hh in range(heads_per_step):
             lanes = slice(hh * HEAD_DIM, (hh + 1) * HEAD_DIM)
-            kc = kc_ref[:, lanes]
-            vc = vc_ref[:, lanes]
-            kn = kn_ref[:, lanes]
-            vn = vn_ref[:, lanes]
+            k = k_ref[:, lanes]
+            v = v_ref[:, lanes]
             for g in range(group_size):
                 col = (hh * group_size + g) * HEAD_DIM
                 q = q_ref[:, col : col + HEAD_DIM]
                 dims = (((1,), (1,)), ((), ()))
-                s_c = lax.dot_general(q, kc, dims, preferred_element_type=jnp.float32) * attn_scale
-                s_n = lax.dot_general(q, kn, dims, preferred_element_type=jnp.float32) * attn_scale
-                s_c = jnp.where(seen_cache, s_c, neg_fill)
-                s_n = jnp.where(seen_new, s_n, neg_fill)
-                top = jnp.maximum(
-                    jnp.max(s_c, axis=1, keepdims=True), jnp.max(s_n, axis=1, keepdims=True)
-                )
-                p_c = jnp.where(seen_cache, jnp.exp(s_c - top), 0.0)
-                p_n = jnp.where(seen_new, jnp.exp(s_n - top), 0.0)
-                total = jnp.sum(p_c, axis=1, keepdims=True) + jnp.sum(p_n, axis=1, keepdims=True)
-                acc = jnp.dot(p_c.astype(jnp.bfloat16), vc, preferred_element_type=jnp.float32)
-                acc = acc + jnp.dot(p_n.astype(jnp.bfloat16), vn, preferred_element_type=jnp.float32)
+                scores = lax.dot_general(q, k, dims, preferred_element_type=jnp.float32) * attn_scale
+                scores = jnp.where(seen, scores, neg_fill)
+                top = jnp.max(scores, axis=1, keepdims=True)
+                probs = jnp.where(seen, jnp.exp(scores - top), 0.0)
+                total = jnp.sum(probs, axis=1, keepdims=True)
+                acc = jnp.dot(probs.astype(jnp.bfloat16), v, preferred_element_type=jnp.float32)
                 pieces.append((acc / total).astype(jnp.bfloat16))
         o_ref[...] = jnp.concatenate(pieces, axis=1)
 
@@ -92,11 +79,10 @@
         num_scalar_prefetch=1,
         grid=(steps,),
         in_specs=[
+            pl.BlockSpec((1, key_count), lambda i, b: (0, 0)),
             pl.BlockSpec((rows, q_width), lambda i, b: (0, i)),
-            pl.BlockSpec((cache_count, 128), lambda i, b: (0, i)),
-            pl.BlockSpec((cache_count, 128), lambda i, b: (0, value_block + i)),
-            pl.BlockSpec((new_count, 128), lambda i, b: (0, i)),
-            pl.BlockSpec((new_count, 128), lambda i, b: (0, value_block + i)),
+            pl.BlockSpec((key_count, 128), lambda i, b: (0, i)),
+            pl.BlockSpec((key_count, 128), lambda i, b: (0, value_block + i)),
         ],
         out_specs=pl.BlockSpec((rows, q_width), lambda i, b: (0, i)),
     )
@@ -106,7 +92,7 @@
         out_shape=jax.ShapeDtypeStruct((rows, query.shape[1]), jnp.bfloat16),
         compiler_params=pltpu.CompilerParams(dimension_semantics=("arbitrary",)),
         interpret=INTERPRET,
-    )(bounds, query, cache_all, cache_all, new_all, new_all)
+    )(bounds, limit, query, keys, keys)
 
 
 def spread_pieces(local, width_axis):
@@ -163,7 +149,7 @@
     ) * lax.axis_size("core") + core
     length = cache_len[0]
     cache_rows = cache_kv[0]
-    cache_all = lax.all_gather(cache_rows, EXP_AXES, axis=0, tiled=True)
+    cache_count = cache_rows.shape[0]
     req_index = lax.axis_index("req")
     chunk_order = (req_index - jnp.arange(lax.axis_size("req"), dtype=jnp.int32)) % lax.axis_size("req")
     normed = rms_scale(hidden_in, attn_gain)
@@ -180,12 +166,23 @@
     )
     values_new = jnp.dot(normed, w_value, preferred_element_type=jnp.float32).astype(jnp.bfloat16)
     new_kv = jnp.concatenate([keys_new, values_new], axis=1)
-    new_all = lax.all_gather(new_kv, EXP_AXES, axis=0, tiled=True)
-    gate_up_local, down_local, new_all = lax.optimization_barrier((w_gate_up[0], w_down[0], new_all))
+    joined = jnp.concatenate([cache_rows, new_kv], axis=0)
+    piece = lax.all_gather(joined, EXP_AXES, axis=0, tiled=True)
+    gate_up_local, down_local, piece = lax.optimization_barrier((w_gate_up[0], w_down[0], piece))
     gate_up_full = spread_pieces(gate_up_local, 1)
     down_full = spread_pieces(down_local, 2)
-    bounds = jnp.stack([length, position_exp * rows_here]).astype(jnp.int32)
-    context = attend(query, cache_all, new_all, bounds, kv_heads, group_size)
+    shard_rows = cache_count + rows_here
+    key_index = jnp.arange(piece.shape[0], dtype=jnp.int32)
+    owner = key_index // shard_rows
+    within = key_index - owner * shard_rows
+    cache_pos = owner * cache_count + within
+    new_pos = owner * rows_here + within - cache_count
+    never = jnp.int32(2**30)
+    limit = jnp.where(
+        within < cache_count, jnp.where(cache_pos < length, jnp.int32(-1), never), new_pos
+    )
+    bounds = (position_exp * rows_here).astype(jnp.int32).reshape(1)
+    context = attend(query, piece, limit.reshape(1, -1), bounds, kv_heads, group_size)
     projected = jnp.dot(context, w_out, preferred_element_type=jnp.float32)
     attended = (hidden_in.astype(jnp.float32) + residual_scale * projected).astype(jnp.bfloat16)
     moe_in = rms_scale(attended, moe_gain)

time: 601 us -> 560 us (0.932)
  waiting for transfers between devices: 366 us -> 326 us
    all_gather x2 -> x1, waiting for transfers between devices: 89.2 us -> 50.5 us  [shards(): piece = lax.all_gather(joined, EXP_AXES, axis=0, tiled=True)]
  transfers between devices with their start and end apart: 20 -> 19, of which waited for: 11 -> 10; matrix products, arithmetic and copies ran while one was open for 5% -> 5% of each run, Pallas kernels for 0% -> 0%
where the time goes in v7:
time: 560 us; the launch traced here: 554 us
  waiting for transfers between devices  326 us (58%)
  local copies, waits for them, and re-layouts  72.3 us (13%)
  starting transfers between devices  40.4 us (7%)
  Pallas kernels  39.8 us (7%)
  matrix products  38.3 us (7%)
  other arithmetic  21.2 us (4%)
  between operations  15.7 us (3%)
    ppermute x14, waiting for transfers between devices, spread_pieces(): chunks.append(lax.ppermute(local, ('req', 'zlo'), perm))  154 us
    all_to_all x1, waiting for transfers between devices, shards(): lax.all_to_all(computed, ('x', 'zhi'), split_axis=0, concat_axis=0, tiled...  56.2 us
    all_to_all x1, waiting for transfers between devices, shards(): lax.all_to_all(outgoing, ('x', 'zhi'), split_axis=0, concat_axis=0, tiled...  54.7 us
    all_gather x1, waiting for transfers between devices, shards(): piece = lax.all_gather(joined, EXP_AXES, axis=0, tiled=True)  50.5 us
    pallas_call x1, Pallas kernels, attend(): pl.pallas_call(kernel, grid_spec=grid_spec, out_shape=jax.ShapeDtypeStruc...  39.8 us
    ppermute x14, starting transfers between devices, spread_pieces(): chunks.append(lax.ppermute(local, ('req', 'zlo'), perm))  26.8 us
    reduce_sum x1, local copies, waits for them, and re-layouts, shards(): computed = jnp.sum(computed, axis=2, dtype=jnp.float32)  18.3 us
    dot_general x1, matrix products, shards(): jnp.einsum('aspkmf,pkfd->aspkmd', activated, down_full, preferred_element...  14.3 us
  transfers between devices with their start and end apart: 19, of which 10 were waited for; matrix products, arithmetic and copies ran while one was open for 5% of the time, Pallas kernels for 0%

profile of v7, /device:TPU:0, one launch (start us, length us, event | category | flops | bytes accessed | tf_op | source)
XLA Modules:
  0.0 553.7 jit_solution(11709536315086488219)
XLA Ops:
  8.1 0.7 convert_element_type.77
  8.7 1.2 fusion.18
  9.9 0.1 multiply_cosine_fusion
  10.1 1.8 fusion.37
  11.9 0.1 copy.90
  12.0 2.0 convolution_convert_fusion
  14.0 0.8 maximum_maximum_fusion
  14.9 4.3 fusion.39
  19.4 0.9 copy.91.q_ref
  20.8 0.6 fusion.17
  21.4 4.8 scatter_custom_fusion
  26.5 0.7 compare_select_fusion.2.lim_ref
  27.2 50.5 %all-gather.2.cloned.1.call-done.k_ref.v_ref = bf16[5632,1024]{1,0:T(8,128)(2,1)} async-done(((bf16[176,1024]{1,0:T(8,128)(2,1)}), bf16[5632,1024]{1,0:T(8,128)(2,1)}) %all-gather.2.cloned.1.call-update) | async-done | bytes 11534352 | tf_op jit(solution)/shard_map/all_gather | solution.py:170
  77.7 39.8 %shard_map.140 = bf16[128,1536]{1,0:T(8,128)(2,1)} custom-call(s32[1]{0:T(128)} %bitcast.bounds_ref, s32[1,5632]{1,0:T(1,128)} %compare_select_fusion.2.lim_ref, bf16[128,1536]{1,0:T(8,128)(2,1)} %copy.91.q_ref, bf16[5632,1024]{1,0:T(8,128)(2,1)} %all-gather.2.cloned.1.call-done.k_ref.v_ref, bf16[5632,1024]{1,0:T(8,128)(2,1)} %all-gather.2.cloned.1.call-done.k_ref.v_ref), custom_call_target="tpu_custom_call" | custom-call | tf_op jit(solution)/shard_map/pallas_call | solution.py:89
  117.5 3.3 fusion.21
  120.9 0.2 fusion.23
  121.1 0.6 gather_fusion
  121.9 5.2 gather_fusion.1
  127.0 5.5 reshape.329
  132.5 5.2 all-to-all-start
  137.7 1.7 collective-permute-start
  139.4 54.7 %all-to-all-done = bf16[8,5,26,1536]{3,2,1,0:T(8,128)(2,1)} async-done(((bf16[8,5,26,1536]{3,2,1,0:T(8,128)(2,1)}), bf16[8,5,26,1536]{3,2,1,0:T(8,128)(2,1)}, u32[]{:S(2)}, u32[]{:S(2)}) %all-to-all-start) | async-done | bytes 3194912 | tf_op jit(solution)/shard_map/all_to_all | solution.py:205
  194.2 3.9 copy.98
  198.2 3.1 collective-permute-start.1
  201.3 1.1 collective-permute-start.2
  202.4 0.7 collective-permute-start.3
  203.2 1.6 collective-permute-start.4
  204.8 9.1 %collective-permute-done.1 = bf16[5,128,384]{2,1,0:T(8,128)(2,1)S(1)} collective-permute-done((bf16[5,128,384]{2,1,0:T(8,128)(2,1)S(1)}, bf16[5,128,384]{2,1,0:T(8,128)(2,1)S(1)}, u32[]{:S(2)}, u32[]{:S(2)}) %collective-permute-start.1) | collective-permute-done | bytes 491552 | tf_op jit(solution)/shard_map/ppermute | solution.py:113
  213.9 3.2 collective-permute-start.5
  217.1 7.4 %collective-permute-done.2 = bf16[5,128,384]{2,1,0:T(8,128)(2,1)S(1)} collective-permute-done((bf16[5,128,384]{2,1,0:T(8,128)(2,1)S(1)}, bf16[5,128,384]{2,1,0:T(8,128)(2,1)S(1)}, u32[]{:S(2)}, u32[]{:S(2)}) %collective-permute-start.2) | collective-permute-done | bytes 491552 | tf_op jit(solution)/shard_map/ppermute | solution.py:113
  224.5 1.4 collective-permute-start.7
  225.9 10.6 %collective-permute-done.3 = bf16[5,128,384]{2,1,0:T(8,128)(2,1)S(1)} collective-permute-done((bf16[5,128,384]{2,1,0:T(8,128)(2,1)S(1)}, bf16[5,128,384]{2,1,0:T(8,128)(2,1)S(1)}, u32[]{:S(2)}, u32[]{:S(2)}) %collective-permute-start.3) | collective-permute-done | bytes 491552 | tf_op jit(solution)/shard_map/ppermute | solution.py:113
  236.5 1.1 collective-permute-start.8
  237.6 2.4 collective-permute-start.9
  240.0 0.7 collective-permute-start.6
  240.8 47.6 %collective-permute-done.6 = bf16[5,128,384]{2,1,0:T(8,128)(2,1)S(1)} collective-permute-done((bf16[5,128,384]{2,1,0:T(8,128)(2,1)S(1)}, bf16[5,128,384]{2,1,0:T(8,128)(2,1)S(1)}, u32[]{:S(2)}, u32[]{:S(2)}) %collective-permute-start.6) | collective-permute-done | bytes 491552 | tf_op jit(solution)/shard_map/ppermute | solution.py:113
  288.4 2.5 collective-permute-start.10
  290.9 2.2 collective-permute-start.11
  293.1 2.8 collective-permute-start.12
  295.9 2.0 collective-permute-start.13
  297.9 1.2 maximum_bitcast_fusion.12
  299.2 1.5 maximum_bitcast_fusion.13
  300.7 2.3 maximum_bitcast_fusion.6
  303.0 72.3 %collective-permute-done.10 = bf16[5,384,256]{2,1,0:T(8,128)(2,1)S(1)} collective-permute-done((bf16[5,384,256]{2,1,0:T(8,128)(2,1)S(1)}, bf16[5,384,256]{2,1,0:T(8,128)(2,1)S(1)}, u32[]{:S(2)}, u32[]{:S(2)}) %collective-permute-start.10) | collective-permute-done | bytes 983072 | tf_op jit(solution)/shard_map/ppermute | solution.py:113
  375.3 7.1 %collective-permute-done.12 = bf16[5,384,256]{2,1,0:T(8,128)(2,1)S(1)} collective-permute-done((bf16[5,384,256]{2,1,0:T(8,128)(2,1)S(1)}, bf16[5,384,256]{2,1,0:T(8,128)(2,1)S(1)}, u32[]{:S(2)}, u32[]{:S(2)}) %collective-permute-start.12) | collective-permute-done | bytes 983072 | tf_op jit(solution)/shard_map/ppermute | solution.py:113
  382.4 2.3 maximum_bitcast_fusion.7
  384.7 4.4 copy.123
  389.1 3.1 copy.122
  392.2 12.0 %fusion.12 = f32[2,8,2,5,26,256]{5,4,1,0,2,3:T(8,128)} fusion(bf16[1,8,5,26,1536]{4,3,1,0,2:T(8,128)(2,1)} %bitcast.87, bf16[1,8,5,26,1536]{4,3,1,0,2:T(8,128)(2,1)} %bitcast.88, bf16[1,5,1536,256]{3,2,0,1:T(8,128)(2,1)} %maximum_bitcast_fusion.7, bf16[1,5,1536,256]{3,2,0,1:T(8,128)(2,1)} %maximum_bitcast_fusion.6), kind=kOutput, calls=%fused_computation.32 | convolution fusion | flops 3300065280 | bytes 18513920 | tf_op jit(solution)/shard_map/askmd,pkdf->aspkmf/dot_general | solution.py:208
  404.2 14.3 %convert_reduce_fusion = f32[5,1536,2,8,26]{1,4,3,2,0:T(8,128)} fusion(bf16[1,5,128,1536]{3,2,1,0:T(8,128)(2,1)} %maximum_bitcast_fusion.13, bf16[1,5,128,1536]{3,2,1,0:T(8,128)(2,1)S(1)} %maximum_bitcast_fusion.12, f32[2,8,2,5,26,256]{5,4,1,0,2,3:T(8,128)} %fusion.12), kind=kOutput, calls=%fused_computation.5 | convolution fusion | flops 1662812160 | bytes 20971520 | tf_op jit(solution)/shard_map/aspkmf,pkfd->aspkmd/dot_general | solution.py:214
  418.6 18.3 %copy.121 = f32[5,1536,2,8,26]{1,3,4,0,2:T(8,128)} copy(f32[5,1536,2,8,26]{1,4,3,2,0:T(8,128)} %convert_reduce_fusion) | data formatting | bytes 25559040 | tf_op jit(solution)/shard_map/reduce_sum | solution.py:217
  436.9 3.4 slice_bitcast_fusion
  440.5 10.4 %collective-permute-done.15 = f32[8,5,26,1536]{3,0,2,1:T(8,128)} collective-permute-done((f32[8,5,26,1536]{3,0,2,1:T(8,128)S(1)}, f32[8,5,26,1536]{3,0,2,1:T(8,128)}, u32[]{:S(2)}, u32[]{:S(2)}) %collective-permute-start.15) | collective-permute-done | bytes 6389792 | tf_op jit(solution)/shard_map/ppermute | solution.py:218
  450.9 3.9 fusion.6
  454.8 3.0 copy.102
  457.8 8.2 %all-to-all-start.1 = ((bf16[8,5,26,1536]{3,2,1,0:T(8,128)(2,1)}), bf16[8,5,26,1536]{3,2,1,0:T(8,128)(2,1)}, u32[]{:S(2)}, u32[]{:S(2)}) async-start(bf16[8,5,26,1536]{3,2,1,0:T(8,128)(2,1)} %copy.102), calls=%async_computation.1 | async-start | bytes 7864320 | tf_op jit(solution)/shard_map/all_to_all | solution.py:219
  466.2 56.2 %all-to-all-done.1 = bf16[8,5,26,1536]{3,2,1,0:T(8,128)(2,1)} async-done(((bf16[8,5,26,1536]{3,2,1,0:T(8,128)(2,1)}), bf16[8,5,26,1536]{3,2,1,0:T(8,128)(2,1)}, u32[]{:S(2)}, u32[]{:S(2)}) %all-to-all-start.1) | async-done | bytes 3194912 | tf_op jit(solution)/shard_map/all_to_all | solution.py:219
  522.4 6.2 %reshape.319 = f32[1040,1536]{1,0:T(8,128)} reshape(bf16[8,5,26,1536]{3,2,1,0:T(8,128)(2,1)} %all-to-all-done.1) | data formatting | bytes 9584640 | tf_op jit(solution)/shard_map/reshape | solution.py:220
  528.6 10.6 %gather_fusion.2 = f32[1024,1536]{1,0:T(8,128)} fusion(f32[1040,1536]{1,0:T(8,128)} %reshape.319, s32[1024]{0:T(1024)S(1)} %broadcast_clamp_fusion), kind=kCustom, calls=%fused_computation.2 | custom fusion | bytes 12587008 | tf_op jit(solution)/shard_map/gather | solution.py:221
  539.1 5.2 fusion.7
  544.3 0.3 copy.104
  544.6 0.3 copy.105
  544.8 0.6 gather_fusion.3
  545.5 0.8 fusion.24
  (70 shorter events, 1.6 us)
Async XLA Ops:
  7.2 2.9 copy-start
  7.2 7.7 %copy-start.3 = (bf16[128,1536]{1,0:T(8,128)(2,1)S(1)}, bf16[128,1536]{1,0:T(8,128)(2,1)}, u32[]{:S(2)}) copy-start(bf16[128,1536]{1,0:T(8,128)(2,1)} %param.13) | copy-start | bytes 1179652
  7.2 6.8 %copy-start.9 = (bf16[1,48,1024]{2,1,0:T(8,128)(2,1)S(1)}, bf16[1,48,1024]{2,1,0:T(8,128)(2,1)}, u32[]{:S(2)}) copy-start(bf16[1,48,1024]{2,1,0:T(8,128)(2,1)} %param.19) | copy-start | bytes 294916
  7.2 70.5 %all-gather.2.cloned.1.call-start = ((), (), s32[]{:S(2)}) async-start(), calls=%async_computation.2 | async-start | bytes 11894784 | tf_op jit(solution)/shard_map/all_gather | solution.py:170
  14.8 5.5 copy-start.11
  14.9 5.6 %copy-start.10 = (s32[128,8]{0,1:T(8,128)S(1)}, s32[128,8]{0,1:T(8,128)}, u32[]{:S(2)}) copy-start(s32[128,8]{0,1:T(8,128)} %param.22) | copy-start | bytes 12292
  120.9 0.9 copy-start.4
  132.5 5.2 copy-start.7
  132.5 61.7 %all-to-all-start = ((bf16[8,5,26,1536]{3,2,1,0:T(8,128)(2,1)}), bf16[8,5,26,1536]{3,2,1,0:T(8,128)(2,1)}, u32[]{:S(2)}, u32[]{:S(2)}) async-start(bf16[8,5,26,1536]{3,2,1,0:T(8,128)(2,1)} %reshape.329), calls=%async_computation | async-start | bytes 7864320 | tf_op jit(solution)/shard_map/all_to_all | solution.py:205
  137.7 86.8 %copy-start.6 = (bf16[1,5,384,256]{3,2,1,0:T(8,128)(2,1)S(1)}, bf16[1,5,384,256]{3,2,1,0:T(8,128)(2,1)}, u32[]{:S(2)}) copy-start(bf16[1,5,384,256]{3,2,1,0:T(8,128)(2,1)} %param.24) | copy-start | bytes 2949124
  137.7 65.5 %collective-permute-start = (bf16[5,128,384]{2,1,0:T(8,128)(2,1)S(1)}, bf16[5,128,384]{2,1,0:T(8,128)(2,1)S(1)}, u32[]{:S(2)}, u32[]{:S(2)}) collective-permute-start(bf16[5,128,384]{2,1,0:T(8,128)(2,1)S(1)} %bitcast.108), channel_id=1, source_target_pairs={{0,32},{2,34},{32,64},{34,66},{64,96},{66,98},{96,0},{98,2},{1,33}... | collective-permute-start | bytes 1474568 | tf_op jit(solution)/shard_map/ppermute | solution.py:113
  198.1 191.1 %collective-permute-start.14 = (bf16[8,5,26,1536]{3,0,2,1:T(8,128)(2,1)S(1)}, bf16[8,5,26,1536]{3,0,2,1:T(8,128)(2,1)S(1)}, u32[]{:S(2)}, u32[]{:S(2)}) collective-permute-start(bf16[8,5,26,1536]{3,0,2,1:T(8,128)(2,1)S(1)} %copy.98), channel_id=1, source_target_pairs={{0,1},{1,0},{2,3},{3,2},{4,5},{5,4},{6,7},{7,6},{8,9},{9,8},{10,11... | collective-permute-start | bytes 9584648 | tf_op jit(solution)/shard_map/ppermute | solution.py:207
  198.2 15.7 %collective-permute-start.1 = (bf16[5,128,384]{2,1,0:T(8,128)(2,1)S(1)}, bf16[5,128,384]{2,1,0:T(8,128)(2,1)S(1)}, u32[]{:S(2)}, u32[]{:S(2)}) collective-permute-start(bf16[5,128,384]{2,1,0:T(8,128)(2,1)S(1)} %bitcast.109), channel_id=1, source_target_pairs={{0,64},{2,66},{32,96},{34,98},{64,0},{66,2},{96,32},{98,34},{1,65}... | collective-permute-start | bytes 1474568 | tf_op jit(solution)/shard_map/ppermute | solution.py:113
  201.3 23.2 %collective-permute-start.2 = (bf16[5,128,384]{2,1,0:T(8,128)(2,1)S(1)}, bf16[5,128,384]{2,1,0:T(8,128)(2,1)S(1)}, u32[]{:S(2)}, u32[]{:S(2)}) collective-permute-start(bf16[5,128,384]{2,1,0:T(8,128)(2,1)S(1)} %bitcast.110), channel_id=1, source_target_pairs={{0,96},{2,98},{32,0},{34,2},{64,32},{66,34},{96,64},{98,66},{1,97}... | collective-permute-start | bytes 1474568 | tf_op jit(solution)/shard_map/ppermute | solution.py:113
  202.4 34.1 %collective-permute-start.3 = (bf16[5,128,384]{2,1,0:T(8,128)(2,1)S(1)}, bf16[5,128,384]{2,1,0:T(8,128)(2,1)S(1)}, u32[]{:S(2)}, u32[]{:S(2)}) collective-permute-start(bf16[5,128,384]{2,1,0:T(8,128)(2,1)S(1)} %bitcast.111), channel_id=1, source_target_pairs={{0,2},{2,0},{32,34},{34,32},{64,66},{66,64},{96,98},{98,96},{1,3},... | collective-permute-start | bytes 1474568 | tf_op jit(solution)/shard_map/ppermute | solution.py:113
  203.2 92.7 %copy-start.8 = (bf16[5,128,384]{2,1,0:T(8,128)(2,1)}, bf16[5,128,384]{2,1,0:T(8,128)(2,1)S(1)}, u32[]{:S(2)}) copy-start(bf16[5,128,384]{2,1,0:T(8,128)(2,1)S(1)} %collective-permute-done) | copy-start | bytes 1474564
  203.2 34.4 %collective-permute-start.4 = (bf16[5,128,384]{2,1,0:T(8,128)(2,1)S(1)}, bf16[5,128,384]{2,1,0:T(8,128)(2,1)S(1)}, u32[]{:S(2)}, u32[]{:S(2)}) collective-permute-start(bf16[5,128,384]{2,1,0:T(8,128)(2,1)S(1)} %bitcast.112), channel_id=1, source_target_pairs={{0,34},{2,32},{32,66},{34,64},{64,98},{66,96},{96,2},{98,0},{1,35}... | collective-permute-start | bytes 1474568 | tf_op jit(solution)/shard_map/ppermute | solution.py:113
  213.9 26.2 %collective-permute-start.5 = (bf16[5,128,384]{2,1,0:T(8,128)(2,1)S(1)}, bf16[5,128,384]{2,1,0:T(8,128)(2,1)S(1)}, u32[]{:S(2)}, u32[]{:S(2)}) collective-permute-start(bf16[5,128,384]{2,1,0:T(8,128)(2,1)S(1)} %bitcast.113), channel_id=1, source_target_pairs={{0,66},{2,64},{32,98},{34,96},{64,2},{66,0},{96,34},{98,32},{1,67}... | collective-permute-start | bytes 1474568 | tf_op jit(solution)/shard_map/ppermute | solution.py:113
  224.5 66.4 %collective-permute-start.7 = (bf16[5,384,256]{2,1,0:T(8,128)(2,1)S(1)}, bf16[5,384,256]{2,1,0:T(8,128)(2,1)S(1)}, u32[]{:S(2)}, u32[]{:S(2)}) collective-permute-start(bf16[5,384,256]{2,1,0:T(8,128)(2,1)S(1)} %bitcast.99), channel_id=1, source_target_pairs={{0,32},{2,34},{32,64},{34,66},{64,96},{66,98},{96,0},{98,2},{1,33}... | collective-permute-start | bytes 2949128 | tf_op jit(solution)/shard_map/ppermute | solution.py:113
  236.5 56.6 %collective-permute-start.8 = (bf16[5,384,256]{2,1,0:T(8,128)(2,1)S(1)}, bf16[5,384,256]{2,1,0:T(8,128)(2,1)S(1)}, u32[]{:S(2)}, u32[]{:S(2)}) collective-permute-start(bf16[5,384,256]{2,1,0:T(8,128)(2,1)S(1)} %bitcast.100), channel_id=1, source_target_pairs={{0,64},{2,66},{32,96},{34,98},{64,0},{66,2},{96,32},{98,34},{1,65}... | collective-permute-start | bytes 2949128 | tf_op jit(solution)/shard_map/ppermute | solution.py:113
  237.6 58.3 %collective-permute-start.9 = (bf16[5,384,256]{2,1,0:T(8,128)(2,1)S(1)}, bf16[5,384,256]{2,1,0:T(8,128)(2,1)S(1)}, u32[]{:S(2)}, u32[]{:S(2)}) collective-permute-start(bf16[5,384,256]{2,1,0:T(8,128)(2,1)S(1)} %bitcast.101), channel_id=1, source_target_pairs={{0,96},{2,98},{32,0},{34,2},{64,32},{66,34},{96,64},{98,66},{1,97}... | collective-permute-start | bytes 2949128 | tf_op jit(solution)/shard_map/ppermute | solution.py:113
  240.0 48.3 %collective-permute-start.6 = (bf16[5,128,384]{2,1,0:T(8,128)(2,1)S(1)}, bf16[5,128,384]{2,1,0:T(8,128)(2,1)S(1)}, u32[]{:S(2)}, u32[]{:S(2)}) collective-permute-start(bf16[5,128,384]{2,1,0:T(8,128)(2,1)S(1)} %bitcast.114), channel_id=1, source_target_pairs={{0,98},{2,96},{32,2},{34,0},{64,34},{66,32},{96,66},{98,64},{1,99}... | collective-permute-start | bytes 1474568 | tf_op jit(solution)/shard_map/ppermute | solution.py:113
  288.4 86.9 %collective-permute-start.10 = (bf16[5,384,256]{2,1,0:T(8,128)(2,1)S(1)}, bf16[5,384,256]{2,1,0:T(8,128)(2,1)S(1)}, u32[]{:S(2)}, u32[]{:S(2)}) collective-permute-start(bf16[5,384,256]{2,1,0:T(8,128)(2,1)S(1)} %bitcast.102), channel_id=1, source_target_pairs={{0,2},{2,0},{32,34},{34,32},{64,66},{66,64},{96,98},{98,96},{1,3},... | collective-permute-start | bytes 2949128 | tf_op jit(solution)/shard_map/ppermute | solution.py:113
  290.9 84.4 %collective-permute-start.11 = (bf16[5,384,256]{2,1,0:T(8,128)(2,1)S(1)}, bf16[5,384,256]{2,1,0:T(8,128)(2,1)S(1)}, u32[]{:S(2)}, u32[]{:S(2)}) collective-permute-start(bf16[5,384,256]{2,1,0:T(8,128)(2,1)S(1)} %bitcast.103), channel_id=1, source_target_pairs={{0,34},{2,32},{32,66},{34,64},{64,98},{66,96},{96,2},{98,0},{1,35}... | collective-permute-start | bytes 2949128 | tf_op jit(solution)/shard_map/ppermute | solution.py:113
  293.1 89.3 %collective-permute-start.12 = (bf16[5,384,256]{2,1,0:T(8,128)(2,1)S(1)}, bf16[5,384,256]{2,1,0:T(8,128)(2,1)S(1)}, u32[]{:S(2)}, u32[]{:S(2)}) collective-permute-start(bf16[5,384,256]{2,1,0:T(8,128)(2,1)S(1)} %bitcast.104), channel_id=1, source_target_pairs={{0,66},{2,64},{32,98},{34,96},{64,2},{66,0},{96,34},{98,32},{1,67}... | collective-permute-start | bytes 2949128 | tf_op jit(solution)/shard_map/ppermute | solution.py:113
  295.9 86.5 %collective-permute-start.13 = (bf16[5,384,256]{2,1,0:T(8,128)(2,1)S(1)}, bf16[5,384,256]{2,1,0:T(8,128)(2,1)S(1)}, u32[]{:S(2)}, u32[]{:S(2)}) collective-permute-start(bf16[5,384,256]{2,1,0:T(8,128)(2,1)S(1)} %bitcast.105), channel_id=1, source_target_pairs={{0,98},{2,96},{32,2},{34,0},{64,34},{66,32},{96,66},{98,64},{1,99}... | collective-permute-start | bytes 2949128 | tf_op jit(solution)/shard_map/ppermute | solution.py:113
  436.9 14.0 %copy-start.2 = (f32[5,1536,2,8,26]{1,3,4,0,2:T(8,128)S(1)}, f32[5,1536,2,8,26]{1,3,4,0,2:T(8,128)}, u32[]{:S(2)}) copy-start(f32[5,1536,2,8,26]{1,3,4,0,2:T(8,128)} %copy.121) | copy-start | bytes 38338564
  440.4 10.5 %collective-permute-start.15 = (f32[8,5,26,1536]{3,0,2,1:T(8,128)S(1)}, f32[8,5,26,1536]{3,0,2,1:T(8,128)}, u32[]{:S(2)}, u32[]{:S(2)}) collective-permute-start(f32[8,5,26,1536]{3,0,2,1:T(8,128)S(1)} %slice_bitcast_fusion), channel_id=1, source_target_pairs={{0,1},{1,0},{2,3},{3,2},{4,5},{5,4},{6,7},{7,6},{8,9},{9,8},{10,11... | collective-permute-start | bytes 19169288 | tf_op jit(solution)/shard_map/ppermute | solution.py:218
  457.8 8.2 %copy-start.12 = (bf16[128,8]{0,1:T(8,128)(2,1)S(1)}, bf16[128,8]{0,1:T(8,128)(2,1)}, u32[]{:S(2)}) copy-start(bf16[128,8]{0,1:T(8,128)(2,1)} %param.23) | copy-start | bytes 6148
  457.8 64.5 %all-to-all-start.1 = ((bf16[8,5,26,1536]{3,2,1,0:T(8,128)(2,1)}), bf16[8,5,26,1536]{3,2,1,0:T(8,128)(2,1)}, u32[]{:S(2)}, u32[]{:S(2)}) async-start(bf16[8,5,26,1536]{3,2,1,0:T(8,128)(2,1)} %copy.102), calls=%async_computation.1 | async-start | bytes 7864320 | tf_op jit(solution)/shard_map/all_to_all | solution.py:219
  539.1 7.3 %copy-start.1 = (bf16[1536,512]{1,0:T(8,128)(2,1)S(1)}, bf16[1536,512]{1,0:T(8,128)(2,1)}, u32[]{:S(2)}) copy-start(bf16[1536,512]{1,0:T(8,128)(2,1)} %param.16) | copy-start | bytes 4718596
  544.3 1.3 copy-start.5
Sparse Core Ops, SparseCore 0:
  14.9 62.7 all-gather.1

commit v8 on v7

--- a/solution.py
+++ b/solution.py
@@ -95,24 +95,32 @@
     )(bounds, limit, query, keys, keys)
 
 
-def spread_pieces(local, width_axis):
+def spread_pieces(gate_up_local, down_local):
     req_count = lax.axis_size("req")
     pair = lax.axis_size("zlo")
-    stacked = []
+    split = gate_up_local.size
+    flat = jnp.concatenate([gate_up_local.reshape(-1), down_local.reshape(-1)])
+    gate_up_rows, down_rows = [], []
     for dz in range(pair):
-        chunks = []
+        gate_up_chunks, down_chunks = [], []
         for dr in range(req_count):
             if dr == 0 and dz == 0:
-                chunks.append(local)
-                continue
-            perm = [
-                (a * pair + z, ((a + dr) % req_count) * pair + (z + dz) % pair)
-                for a in range(req_count)
-                for z in range(pair)
-            ]
-            chunks.append(lax.ppermute(local, ("req", "zlo"), perm))
-        stacked.append(jnp.concatenate(chunks, axis=width_axis))
-    return jnp.stack(stacked, axis=0)
+                got = flat
+            else:
+                perm = [
+                    (a * pair + z, ((a + dr) % req_count) * pair + (z + dz) % pair)
+                    for a in range(req_count)
+                    for z in range(pair)
+                ]
+                got = lax.ppermute(flat, ("req", "zlo"), perm)
+            gate_up_chunks.append(got[:split].reshape(gate_up_local.shape))
+            down_chunks.append(got[split:].reshape(down_local.shape))
+        gate_up_rows.append(jnp.concatenate(gate_up_chunks, axis=1))
+        down_rows.append(jnp.concatenate(down_chunks, axis=2))
+    experts, width, both = gate_up_rows[0].shape
+    gate_up_full = jnp.stack(gate_up_rows, axis=2).reshape(experts, width, pair * both)
+    down_full = jnp.stack(down_rows, axis=1).reshape(experts, pair * down_local.shape[1], width)
+    return gate_up_full, down_full
 
 
 def in_chunk_order(rows, chunk_order):
@@ -169,8 +177,7 @@
     joined = jnp.concatenate([cache_rows, new_kv], axis=0)
     piece = lax.all_gather(joined, EXP_AXES, axis=0, tiled=True)
     gate_up_local, down_local, piece = lax.optimization_barrier((w_gate_up[0], w_down[0], piece))
-    gate_up_full = spread_pieces(gate_up_local, 1)
-    down_full = spread_pieces(down_local, 2)
+    gate_up_full, down_full = spread_pieces(gate_up_local, down_local)
     shard_rows = cache_count + rows_here
     key_index = jnp.arange(piece.shape[0], dtype=jnp.int32)
     owner = key_index // shard_rows
@@ -187,8 +194,8 @@
     attended = (hidden_in.astype(jnp.float32) + residual_scale * projected).astype(jnp.bfloat16)
     moe_in = rms_scale(attended, moe_gain)
     moe_in = in_chunk_order(moe_in, chunk_order)
-    block_experts = gate_up_full.shape[1]
-    slice_width = down_full.shape[2]
+    block_experts = gate_up_full.shape[0]
+    slice_width = w_down.shape[2]
     flat_ids = expert_ids.reshape(-1)
     matches = (flat_ids[:, None] == jnp.arange(EXPERTS, dtype=jnp.int32)[None, :]).astype(jnp.int32)
     pair_count = flat_ids.shape[0]
@@ -204,18 +211,19 @@
     outgoing = moe_in[slot_token.reshape(blocks, block_experts, MOST)]
     arrived = lax.all_to_all(outgoing, ("x", "zhi"), split_axis=0, concat_axis=0, tiled=True)
     swap = [(0, 1), (1, 0)]
-    arrived = jnp.stack([arrived, lax.ppermute(arrived, "core", swap)], axis=0)
-    gate_up = jnp.einsum(
-        "askmd,pkdf->aspkmf", arrived, gate_up_full, preferred_element_type=jnp.float32
-    )
-    activated = (jax.nn.silu(gate_up[..., :slice_width]) * gate_up[..., slice_width:]).astype(
-        jnp.bfloat16
-    )
-    computed = jnp.einsum(
-        "aspkmf,pkfd->aspkmd", activated, down_full, preferred_element_type=jnp.float32
-    ).astype(jnp.bfloat16)
-    computed = jnp.sum(computed, axis=2, dtype=jnp.float32)
-    computed = (computed[0] + lax.ppermute(computed[1], "core", swap)).astype(jnp.bfloat16)
+
+    def experts_on(rows_in):
+        gate_up = jnp.einsum("skmd,kdf->skmf", rows_in, gate_up_full, preferred_element_type=jnp.float32)
+        gate_up = gate_up.reshape(gate_up.shape[:-1] + (-1, 2 * slice_width))
+        activated = (jax.nn.silu(gate_up[..., :slice_width]) * gate_up[..., slice_width:]).astype(
+            jnp.bfloat16
+        )
+        activated = activated.reshape(activated.shape[:-2] + (-1,))
+        return jnp.einsum("skmf,kfd->skmd", activated, down_full, preferred_element_type=jnp.float32)
+
+    theirs = experts_on(lax.ppermute(arrived, "core", swap)).astype(jnp.bfloat16)
+    theirs = lax.ppermute(theirs, "core", swap)
+    computed = (experts_on(arrived) + theirs.astype(jnp.float32)).astype(jnp.bfloat16)
     returned = lax.all_to_all(computed, ("x", "zhi"), split_axis=0, concat_axis=0, tiled=True)
     summed = returned.astype(jnp.float32).reshape(EXPERTS * MOST, width)
     picked = summed[slot_index] * expert_weights.reshape(-1).astype(jnp.float32)[:, None]

time: 560 us -> 612 us (1.093)
  the two profiles are of different devices: /device:TPU:0 before, /device:TPU:8 now
where the time goes in v8:
time: 612 us; the launch traced here: 605 us
  waiting for transfers between devices  280 us (46%)
  local copies, waits for them, and re-layouts  185 us (30%)
  Pallas kernels  40.4 us (7%)
  starting transfers between devices  30.9 us (5%)
  matrix products  30 us (5%)
  other arithmetic  22.5 us (4%)
  between operations  15.8 us (3%)
    ppermute x7, waiting for transfers between devices, spread_pieces(): got = lax.ppermute(flat, ('req', 'zlo'), perm)  172 us
    all_to_all x1, waiting for transfers between devices, shards(): lax.all_to_all(computed, ('x', 'zhi'), split_axis=0, concat_axis=0, tiled...  56.6 us
    all_gather x1, waiting for transfers between devices, shards(): piece = lax.all_gather(joined, EXP_AXES, axis=0, tiled=True)  50.8 us
    another operation x1, local copies, waits for them, and re-layouts, spread_pieces(): jnp.stack(gate_up_rows, axis=2).reshape(experts, width, pair * both)  50.6 us
    pallas_call x1, Pallas kernels, attend(): pl.pallas_call(kernel, grid_spec=grid_spec, out_shape=jax.ShapeDtypeStruc...  40.4 us
    slice x14, local copies, waits for them, and re-layouts, spread_pieces(): down_chunks.append(got[split:].reshape(down_local.shape))  25.4 us
    ppermute x7, starting transfers between devices, spread_pieces(): got = lax.ppermute(flat, ('req', 'zlo'), perm)  19.6 us
    slice x7, local copies, waits for them, and re-layouts, spread_pieces(): gate_up_chunks.append(got[:split].reshape(gate_up_local.shape))  14.7 us
  transfers between devices with their start and end apart: 12, of which 5 were waited for; matrix products, arithmetic and copies ran while one was open for 27% of the time, Pallas kernels for 0%

profile of v8, /device:TPU:8, one launch (start us, length us, event | category | flops | bytes accessed | tf_op | source)
XLA Modules:
  0.0 604.5 jit_solution(6787471628617641814)
XLA Ops:
  9.9 1.5 convolution_convert_fusion.1
  11.4 2.3 fusion.48
  16.0 4.3 scatter_custom_fusion
  20.6 4.4 fusion.50
  26.8 50.8 %all-gather.2.cloned.1.call-done.k_ref.v_ref = bf16[5632,1024]{1,0:T(8,128)(2,1)} async-done(((bf16[176,1024]{1,0:T(8,128)(2,1)}), bf16[5632,1024]{1,0:T(8,128)(2,1)}) %all-gather.2.cloned.1.call-update) | async-done | bytes 11534352 | tf_op jit(solution)/shard_map/all_gather | solution.py:178
  77.8 40.4 %shard_map.140 = bf16[128,1536]{1,0:T(8,128)(2,1)} custom-call(s32[1]{0:T(128)} %bitcast.bounds_ref, s32[1,5632]{1,0:T(1,128)} %compare_select_fusion.2.lim_ref, bf16[128,1536]{1,0:T(8,128)(2,1)} %copy.82.q_ref, bf16[5632,1024]{1,0:T(8,128)(2,1)} %all-gather.2.cloned.1.call-done.k_ref.v_ref, bf16[5632,1024]{1,0:T(8,128)(2,1)} %all-gather.2.cloned.1.call-done.k_ref.v_ref), custom_call_target="tpu_custom_call" | custom-call | tf_op jit(solution)/shard_map/pallas_call | solution.py:89
  118.2 3.4 fusion.29
  124.6 5.4 gather_fusion.1
  130.0 5.5 reshape.452
  135.5 5.0 all-to-all-start
  141.9 3.3 collective-permute-start.5
  145.1 1.8 collective-permute-start.4
  146.9 1.5 collective-permute-start.3
  148.6 107.2 %collective-permute-done.6 = bf16[737280]{0:T(1024)(128)(2,1)} collective-permute-done((bf16[737280]{0:T(1024)(128)(2,1)}, bf16[737280]{0:T(1024)(128)(2,1)}, u32[]{:S(2)}, u32[]{:S(2)}) %collective-permute-start.6) | collective-permute-done | bytes 1474592 | tf_op jit(solution)/shard_map/ppermute | solution.py:115
  255.9 12.2 %collective-permute-start.1 = (bf16[737280]{0:T(1024)(128)(2,1)}, bf16[737280]{0:T(1024)(128)(2,1)}, u32[]{:S(2)}, u32[]{:S(2)}) collective-permute-start(bf16[737280]{0:T(1024)(128)(2,1)} %constant_dynamic-update-slice_fusion), channel_id=1, source_target_pairs={{0,64},{2,66},{32,96},{34,98},{64,0},{66,2},{96,32},{98,34},{1,65}... | collective-permute-start | bytes 4423688 | tf_op jit(solution)/shard_map/ppermute | solution.py:115
  268.0 46.3 %collective-permute-done.5 = bf16[737280]{0:T(1024)(128)(2,1)} collective-permute-done((bf16[737280]{0:T(1024)(128)(2,1)}, bf16[737280]{0:T(1024)(128)(2,1)}, u32[]{:S(2)}, u32[]{:S(2)}) %collective-permute-start.5) | collective-permute-done | bytes 1474592 | tf_op jit(solution)/shard_map/ppermute | solution.py:115
  314.3 5.6 copy.95
  324.8 2.2 slice.189
  327.0 1.6 reshape.429
  328.6 1.8 slice.182
  330.5 2.0 slice.151
  332.5 2.2 slice.188
  334.8 2.2 reshape.428
  337.0 1.8 slice.181
  338.8 2.0 slice.149
  340.9 2.2 slice.187
  343.1 2.3 reshape.427
  345.3 1.8 slice.180
  347.2 2.1 slice.147
  349.2 2.3 slice.186
  351.5 2.2 reshape.426
  353.6 1.8 slice.179
  355.5 2.0 slice.145
  357.5 18.8 %collective-permute-done.1 = bf16[737280]{0:T(1024)(128)(2,1)} collective-permute-done((bf16[737280]{0:T(1024)(128)(2,1)}, bf16[737280]{0:T(1024)(128)(2,1)}, u32[]{:S(2)}, u32[]{:S(2)}) %collective-permute-start.1) | collective-permute-done | bytes 1474592 | tf_op jit(solution)/shard_map/ppermute | solution.py:115
  376.3 2.2 slice.185
  378.6 2.2 reshape.425
  380.8 1.8 slice.178
  382.6 2.0 slice.143
  384.7 2.3 slice.184
  386.9 2.2 reshape.424
  389.1 1.8 slice.177
  390.9 2.0 slice.141
  393.0 1.7 maximum_bitcast_fusion.2
  394.7 1.7 maximum_bitcast_fusion.3
  396.7 2.3 copy.83
  399.5 2.3 maximum_bitcast_fusion
  401.8 2.3 maximum_bitcast_fusion.1
  404.1 4.0 pad_maximum_fusion
  408.1 50.6 %copy.84 = bf16[5,1536,2,256]{3,2,1,0:T(2,128)(2,1)} copy(bf16[5,1536,2,256]{3,1,0,2:T(8,128)(2,1)S(1)} %pad_maximum_fusion) | data formatting | bytes 15728640 | tf_op jit(solution)/shard_map/stack | solution.py:121
  458.7 13.6 %reshape.484 = bf16[5,1536,512,1]{2,1,0,3:T(8,128)(2,1)} reshape(bf16[5,1536,2,256]{3,2,1,0:T(2,128)(2,1)} %copy.84) | data formatting | bytes 15728640 | tf_op jit(solution)/shard_map/reshape | solution.py:121
  472.3 7.9 %fusion.16 = f32[8,5,26,512]{3,2,0,1:T(8,128)} fusion(bf16[8,5,26,1536]{3,0,2,1:T(8,128)(2,1)} %collective-permute-done.7, bf16[5,1536,512,1]{2,1,0,3:T(8,128)(2,1)} %reshape.484), kind=kOutput, calls=%fused_computation.28 | convolution fusion | flops 1635778560 | bytes 13189120 | tf_op jit(solution)/shard_map/skmd,kdf->skmf/dot_general | solution.py:216
  480.2 3.9 reshape.488
  484.1 1.9 fusion.53
  488.0 3.5 copy.101
  491.6 5.9 fusion.11
  497.5 3.9 reshape.487
  501.4 1.9 fusion.52
  504.1 3.0 fusion.4
  507.1 3.0 copy.102
  510.1 6.3 %all-to-all-start.1 = ((bf16[8,5,26,1536]{3,2,1,0:T(8,128)(2,1)}), bf16[8,5,26,1536]{3,2,1,0:T(8,128)(2,1)}, u32[]{:S(2)}, u32[]{:S(2)}) async-start(bf16[8,5,26,1536]{3,2,1,0:T(8,128)(2,1)} %copy.102), calls=%async_computation.1 | async-start | bytes 7864320 | tf_op jit(solution)/shard_map/all_to_all | solution.py:227
  516.6 56.6 %all-to-all-done.1 = bf16[8,5,26,1536]{3,2,1,0:T(8,128)(2,1)} async-done(((bf16[8,5,26,1536]{3,2,1,0:T(8,128)(2,1)}), bf16[8,5,26,1536]{3,2,1,0:T(8,128)(2,1)}, u32[]{:S(2)}, u32[]{:S(2)}) %all-to-all-start.1) | async-done | bytes 3194912 | tf_op jit(solution)/shard_map/all_to_all | solution.py:227
  573.1 6.2 %reshape.442 = f32[1040,1536]{1,0:T(8,128)} reshape(bf16[8,5,26,1536]{3,2,1,0:T(8,128)(2,1)} %all-to-all-done.1) | data formatting | bytes 9584640 | tf_op jit(solution)/shard_map/reshape | solution.py:228
  579.3 10.6 %gather_fusion.2 = f32[1024,1536]{1,0:T(8,128)} fusion(f32[1040,1536]{1,0:T(8,128)} %reshape.442, s32[1024]{0:T(1024)S(1)} %broadcast_clamp_fusion), kind=kCustom, calls=%fused_computation.2 | custom fusion | bytes 12587008 | tf_op jit(solution)/shard_map/gather | solution.py:229
  589.9 5.2 fusion.5
  (113 shorter events, 21.7 us)
Async XLA Ops:
  7.2 2.7 copy-start
  7.2 6.9 %copy-start.15 = (bf16[1,48,1024]{2,1,0:T(8,128)(2,1)S(1)}, bf16[1,48,1024]{2,1,0:T(8,128)(2,1)}, u32[]{:S(2)}) copy-start(bf16[1,48,1024]{2,1,0:T(8,128)(2,1)} %param.19) | copy-start | bytes 294916
  7.2 7.8 %copy-start.17 = (bf16[1536]{0:T(1024)(128)(2,1)S(1)}, bf16[1536]{0:T(1024)(128)(2,1)}, u32[]{:S(2)}) copy-start(bf16[1536]{0:T(1024)(128)(2,1)} %param.21) | copy-start | bytes 9220
  7.2 7.8 %copy-start.16 = (s32[128,8]{0,1:T(8,128)S(1)}, s32[128,8]{0,1:T(8,128)}, u32[]{:S(2)}) copy-start(s32[128,8]{0,1:T(8,128)} %param.22) | copy-start | bytes 12292
  7.2 70.4 %all-gather.2.cloned.1.call-start = ((), (), s32[]{:S(2)}) async-start(), calls=%async_computation.2 | async-start | bytes 11894784 | tf_op jit(solution)/shard_map/all_gather | solution.py:178
  9.9 10.6 %copy-start.2 = (bf16[128,1536]{1,0:T(8,128)(2,1)S(1)}, bf16[128,1536]{1,0:T(8,128)(2,1)}, u32[]{:S(2)}) copy-start(bf16[128,1536]{1,0:T(8,128)(2,1)} %param.13) | copy-start | bytes 1179652
  20.6 57.0 %copy-start.13 = (bf16[1,5,128,384]{3,2,1,0:T(8,128)(2,1)S(1)}, bf16[1,5,128,384]{3,2,1,0:T(8,128)(2,1)}, u32[]{:S(2)}) copy-start(bf16[1,5,128,384]{3,2,1,0:T(8,128)(2,1)} %param.25) | copy-start | bytes 1474564
  118.2 4.4 copy-start.5
  121.6 3.0 copy-start.11
  135.5 178.9 %all-to-all-start = ((bf16[8,5,26,1536]{3,2,1,0:T(8,128)(2,1)}), bf16[8,5,26,1536]{3,2,1,0:T(8,128)(2,1)}, u32[]{:S(2)}, u32[]{:S(2)}) async-start(bf16[8,5,26,1536]{3,2,1,0:T(8,128)(2,1)} %reshape.452), calls=%async_computation | async-start | bytes 7864320 | tf_op jit(solution)/shard_map/all_to_all | solution.py:212
  141.3 114.6 %collective-permute-start.6 = (bf16[737280]{0:T(1024)(128)(2,1)}, bf16[737280]{0:T(1024)(128)(2,1)}, u32[]{:S(2)}, u32[]{:S(2)}) collective-permute-start(bf16[737280]{0:T(1024)(128)(2,1)} %constant_dynamic-update-slice_fusion), channel_id=1, source_target_pairs={{0,98},{2,96},{32,2},{34,0},{64,34},{66,32},{96,66},{98,64},{1,99}... | collective-permute-start | bytes 4423688 | tf_op jit(solution)/shard_map/ppermute | solution.py:115
  141.9 172.5 %collective-permute-start.5 = (bf16[737280]{0:T(1024)(128)(2,1)}, bf16[737280]{0:T(1024)(128)(2,1)}, u32[]{:S(2)}, u32[]{:S(2)}) collective-permute-start(bf16[737280]{0:T(1024)(128)(2,1)} %constant_dynamic-update-slice_fusion), channel_id=1, source_target_pairs={{0,66},{2,64},{32,98},{34,96},{64,2},{66,0},{96,34},{98,32},{1,67}... | collective-permute-start | bytes 4423688 | tf_op jit(solution)/shard_map/ppermute | solution.py:115
  145.1 174.8 %collective-permute-start.4 = (bf16[737280]{0:T(1024)(128)(2,1)}, bf16[737280]{0:T(1024)(128)(2,1)S(1)}, u32[]{:S(2)}, u32[]{:S(2)}) collective-permute-start(bf16[737280]{0:T(1024)(128)(2,1)} %constant_dynamic-update-slice_fusion), channel_id=1, source_target_pairs={{0,34},{2,32},{32,66},{34,64},{64,98},{66,96},{96,2},{98,0},{1,35}... | collective-permute-start | bytes 4423688 | tf_op jit(solution)/shard_map/ppermute | solution.py:115
  146.9 193.9 %collective-permute-start.3 = (bf16[737280]{0:T(1024)(128)(2,1)}, bf16[737280]{0:T(1024)(128)(2,1)}, u32[]{:S(2)}, u32[]{:S(2)}) collective-permute-start(bf16[737280]{0:T(1024)(128)(2,1)} %constant_dynamic-update-slice_fusion), channel_id=1, source_target_pairs={{0,2},{2,0},{32,34},{34,32},{64,66},{66,64},{96,98},{98,96},{1,3},... | collective-permute-start | bytes 4423688 | tf_op jit(solution)/shard_map/ppermute | solution.py:115
  148.4 200.8 %collective-permute-start.2 = (bf16[737280]{0:T(1024)(128)(2,1)}, bf16[737280]{0:T(1024)(128)(2,1)}, u32[]{:S(2)}, u32[]{:S(2)}) collective-permute-start(bf16[737280]{0:T(1024)(128)(2,1)} %constant_dynamic-update-slice_fusion), channel_id=1, source_target_pairs={{0,96},{2,98},{32,0},{34,2},{64,32},{66,34},{96,64},{98,66},{1,97}... | collective-permute-start | bytes 4423688 | tf_op jit(solution)/shard_map/ppermute | solution.py:115
  255.9 120.5 %collective-permute-start.1 = (bf16[737280]{0:T(1024)(128)(2,1)}, bf16[737280]{0:T(1024)(128)(2,1)}, u32[]{:S(2)}, u32[]{:S(2)}) collective-permute-start(bf16[737280]{0:T(1024)(128)(2,1)} %constant_dynamic-update-slice_fusion), channel_id=1, source_target_pairs={{0,64},{2,66},{32,96},{34,98},{64,0},{66,2},{96,32},{98,34},{1,65}... | collective-permute-start | bytes 4423688 | tf_op jit(solution)/shard_map/ppermute | solution.py:115
  314.3 70.3 %collective-permute-start = (bf16[737280]{0:T(1024)(128)(2,1)}, bf16[737280]{0:T(1024)(128)(2,1)}, u32[]{:S(2)}, u32[]{:S(2)}) collective-permute-start(bf16[737280]{0:T(1024)(128)(2,1)} %constant_dynamic-update-slice_fusion), channel_id=1, source_target_pairs={{0,32},{2,34},{32,64},{34,66},{64,96},{66,98},{96,0},{98,2},{1,33}... | collective-permute-start | bytes 4423688 | tf_op jit(solution)/shard_map/ppermute | solution.py:115
  319.9 1.1 copy-start.14
  321.1 151.2 %collective-permute-start.7 = (bf16[8,5,26,1536]{3,0,2,1:T(8,128)(2,1)}, bf16[8,5,26,1536]{3,0,2,1:T(8,128)(2,1)}, u32[]{:S(2)}, u32[]{:S(2)}) collective-permute-start(bf16[8,5,26,1536]{3,0,2,1:T(8,128)(2,1)} %copy.95), channel_id=1, source_target_pairs={{0,1},{1,0},{2,3},{3,2},{4,5},{5,4},{6,7},{7,6},{8,9},{9,8},{10,11... | collective-permute-start | bytes 9584648 | tf_op jit(solution)/shard_map/ppermute | solution.py:224
  396.7 2.4 copy-start.8
  396.7 2.4 copy-start.9
  396.7 2.8 copy-start.10
  399.5 2.3 copy-start.6
  399.5 2.3 copy-start.7
  484.1 2.8 copy-start.3
  486.0 5.6 slice-start
  486.9 4.7 slice-start.1
  491.6 11.7 %collective-permute-start.8 = (bf16[8,5,26,1536]{3,0,2,1:T(8,128)(2,1)}, bf16[8,5,26,1536]{3,0,2,1:T(8,128)(2,1)}, u32[]{:S(2)}, u32[]{:S(2)}) collective-permute-start(bf16[8,5,26,1536]{3,0,2,1:T(8,128)(2,1)} %copy.101), channel_id=1, source_target_pairs={{0,1},{1,0},{2,3},{3,2},{4,5},{5,4},{6,7},{7,6},{8,9},{9,8},{10,11... | collective-permute-start | bytes 9584648 | tf_op jit(solution)/shard_map/ppermute | solution.py:225
  501.4 2.8 copy-start.4
  510.1 6.3 %copy-start.18 = (bf16[128,8]{0,1:T(8,128)(2,1)S(1)}, bf16[128,8]{0,1:T(8,128)(2,1)}, u32[]{:S(2)}) copy-start(bf16[128,8]{0,1:T(8,128)(2,1)} %param.23) | copy-start | bytes 6148
  510.1 63.0 %all-to-all-start.1 = ((bf16[8,5,26,1536]{3,2,1,0:T(8,128)(2,1)}), bf16[8,5,26,1536]{3,2,1,0:T(8,128)(2,1)}, u32[]{:S(2)}, u32[]{:S(2)}) async-start(bf16[8,5,26,1536]{3,2,1,0:T(8,128)(2,1)} %copy.102), calls=%async_computation.1 | async-start | bytes 7864320 | tf_op jit(solution)/shard_map/all_to_all | solution.py:227
  589.9 7.3 %copy-start.1 = (bf16[1536,512]{1,0:T(8,128)(2,1)S(1)}, bf16[1536,512]{1,0:T(8,128)(2,1)}, u32[]{:S(2)}) copy-start(bf16[1536,512]{1,0:T(8,128)(2,1)} %param.17) | copy-start | bytes 4718596
  595.1 1.3 copy-start.12
Sparse Core Ops, SparseCore 0:
  15.0 62.5 all-gather.1

commit v9 on v7

--- a/solution.py
+++ b/solution.py
@@ -204,18 +204,17 @@
     outgoing = moe_in[slot_token.reshape(blocks, block_experts, MOST)]
     arrived = lax.all_to_all(outgoing, ("x", "zhi"), split_axis=0, concat_axis=0, tiled=True)
     swap = [(0, 1), (1, 0)]
-    arrived = jnp.stack([arrived, lax.ppermute(arrived, "core", swap)], axis=0)
-    gate_up = jnp.einsum(
-        "askmd,pkdf->aspkmf", arrived, gate_up_full, preferred_element_type=jnp.float32
-    )
-    activated = (jax.nn.silu(gate_up[..., :slice_width]) * gate_up[..., slice_width:]).astype(
-        jnp.bfloat16
-    )
-    computed = jnp.einsum(
-        "aspkmf,pkfd->aspkmd", activated, down_full, preferred_element_type=jnp.float32
-    ).astype(jnp.bfloat16)
-    computed = jnp.sum(computed, axis=2, dtype=jnp.float32)
-    computed = (computed[0] + lax.ppermute(computed[1], "core", swap)).astype(jnp.bfloat16)
+
+    def experts_on(rows_in):
+        gate_up = jnp.einsum("skmd,pkdf->spkmf", rows_in, gate_up_full, preferred_element_type=jnp.float32)
+        activated = (jax.nn.silu(gate_up[..., :slice_width]) * gate_up[..., slice_width:]).astype(
+            jnp.bfloat16
+        )
+        return jnp.einsum("spkmf,pkfd->skmd", activated, down_full, preferred_element_type=jnp.float32)
+
+    theirs = experts_on(lax.ppermute(arrived, "core", swap)).astype(jnp.bfloat16)
+    theirs = lax.ppermute(theirs, "core", swap)
+    computed = (experts_on(arrived) + theirs.astype(jnp.float32)).astype(jnp.bfloat16)
     returned = lax.all_to_all(computed, ("x", "zhi"), split_axis=0, concat_axis=0, tiled=True)
     summed = returned.astype(jnp.float32).reshape(EXPERTS * MOST, width)
     picked = summed[slot_index] * expert_weights.reshape(-1).astype(jnp.float32)[:, None]

time: 560 us -> 528 us (0.943)
  the two profiles are of different devices: /device:TPU:0 before, /device:TPU:8 now
where the time goes in v9:
time: 528 us; the launch traced here: 523 us
  waiting for transfers between devices  332 us (63%)
  local copies, waits for them, and re-layouts  51.7 us (10%)
  Pallas kernels  40.1 us (8%)
  starting transfers between devices  35.3 us (7%)
  matrix products  31.7 us (6%)
  other arithmetic  16.4 us (3%)
  between operations  15.4 us (3%)
    ppermute x14, waiting for transfers between devices, spread_pieces(): chunks.append(lax.ppermute(local, ('req', 'zlo'), perm))  161 us
    all_to_all x1, waiting for transfers between devices, shards(): lax.all_to_all(outgoing, ('x', 'zhi'), split_axis=0, concat_axis=0, tiled...  63.3 us
    all_to_all x1, waiting for transfers between devices, shards(): lax.all_to_all(computed, ('x', 'zhi'), split_axis=0, concat_axis=0, tiled...  56.8 us
    all_gather x1, waiting for transfers between devices, shards(): piece = lax.all_gather(joined, EXP_AXES, axis=0, tiled=True)  50.9 us
    pallas_call x1, Pallas kernels, attend(): pl.pallas_call(kernel, grid_spec=grid_spec, out_shape=jax.ShapeDtypeStruc...  40.1 us
    ppermute x14, starting transfers between devices, spread_pieces(): chunks.append(lax.ppermute(local, ('req', 'zlo'), perm))  25.2 us
    dot_general x2, matrix products, experts_on(): jnp.einsum('skmd,pkdf->spkmf', rows_in, gate_up_full, preferred_element_t...  11.5 us
    gather x2, local copies, waits for them, and re-layouts, shards(): outgoing = moe_in[slot_token.reshape(blocks, block_experts, MOST)]  10.6 us
  transfers between devices with their start and end apart: 19, of which 9 were waited for; matrix products, arithmetic and copies ran while one was open for 5% of the time, Pallas kernels for 0%

profile of v9, /device:TPU:8, one launch (start us, length us, event | category | flops | bytes accessed | tf_op | source)
XLA Modules:
  0.0 522.9 jit_solution(14042354301649888249)
XLA Ops:
  8.0 1.2 fusion.24
  9.2 0.7 convert_element_type.81
  9.9 1.5 convolution_convert_fusion
  11.4 2.3 fusion.49
  13.7 0.1 multiply_cosine_fusion
  13.9 0.1 copy.77
  14.1 0.8 maximum_maximum_fusion
  15.4 0.6 fusion.23
  16.0 4.3 scatter_custom_fusion
  20.4 0.1 reshape.330
  20.6 4.3 fusion.51
  24.9 0.1 subtract_convert_fusion
  25.1 0.9 copy.78.q_ref
  26.0 0.7 compare_select_fusion.2.lim_ref
  26.7 50.9 %all-gather.2.cloned.1.call-done.k_ref.v_ref = bf16[5632,1024]{1,0:T(8,128)(2,1)} async-done(((bf16[176,1024]{1,0:T(8,128)(2,1)}), bf16[5632,1024]{1,0:T(8,128)(2,1)}) %all-gather.2.cloned.1.call-update) | async-done | bytes 11534352 | tf_op jit(solution)/shard_map/all_gather | solution.py:170
  77.6 40.1 %shard_map.140 = bf16[128,1536]{1,0:T(8,128)(2,1)} custom-call(s32[1]{0:T(128)} %bitcast.bounds_ref, s32[1,5632]{1,0:T(1,128)} %compare_select_fusion.2.lim_ref, bf16[128,1536]{1,0:T(8,128)(2,1)} %copy.78.q_ref, bf16[5632,1024]{1,0:T(8,128)(2,1)} %all-gather.2.cloned.1.call-done.k_ref.v_ref, bf16[5632,1024]{1,0:T(8,128)(2,1)} %all-gather.2.cloned.1.call-done.k_ref.v_ref), custom_call_target="tpu_custom_call" | custom-call | tf_op jit(solution)/shard_map/pallas_call | solution.py:89
  117.7 3.3 fusion.27
  121.1 0.2 fusion.29
  121.3 0.6 gather_fusion
  122.1 5.2 gather_fusion.1
  127.2 5.5 %reshape.329 = bf16[8,5,26,1536]{3,2,1,0:T(8,128)(2,1)} reshape(bf16[1040,1536]{1,0:T(8,128)(2,1)} %gather_fusion.1) | data formatting | bytes 6389760 | tf_op jit(solution)/shard_map/gather | solution.py:204
  132.7 5.1 all-to-all-start
  137.9 1.1 collective-permute-start.6
  139.0 63.3 %all-to-all-done = bf16[8,5,26,1536]{3,2,1,0:T(8,128)(2,1)} async-done(((bf16[8,5,26,1536]{3,2,1,0:T(8,128)(2,1)}), bf16[8,5,26,1536]{3,2,1,0:T(8,128)(2,1)}, u32[]{:S(2)}, u32[]{:S(2)}) %all-to-all-start) | async-done | bytes 3194912 | tf_op jit(solution)/shard_map/all_to_all | solution.py:205
  202.3 3.9 copy.88
  206.3 4.9 collective-permute-start.5
  211.3 1.3 collective-permute-start.3
  212.5 2.2 collective-permute-start.2
  214.8 9.2 %collective-permute-done.5 = bf16[5,128,384]{2,1,0:T(8,128)(2,1)S(1)} collective-permute-done((bf16[5,128,384]{2,1,0:T(8,128)(2,1)S(1)}, bf16[5,128,384]{2,1,0:T(8,128)(2,1)S(1)}, u32[]{:S(2)}, u32[]{:S(2)}) %collective-permute-start.5) | collective-permute-done | bytes 491552 | tf_op jit(solution)/shard_map/ppermute | solution.py:113
  223.9 6.5 %collective-permute-start.1 = (bf16[5,128,384]{2,1,0:T(8,128)(2,1)S(1)}, bf16[5,128,384]{2,1,0:T(8,128)(2,1)S(1)}, u32[]{:S(2)}, u32[]{:S(2)}) collective-permute-start(bf16[5,128,384]{2,1,0:T(8,128)(2,1)S(1)} %bitcast.119), channel_id=1, source_target_pairs={{0,64},{2,66},{32,96},{34,98},{64,0},{66,2},{96,32},{98,34},{1,65}... | collective-permute-start | bytes 1474568 | tf_op jit(solution)/shard_map/ppermute | solution.py:113
  230.4 3.8 collective-permute-done.4
  234.2 9.9 %collective-permute-done.3 = bf16[5,128,384]{2,1,0:T(8,128)(2,1)S(1)} collective-permute-done((bf16[5,128,384]{2,1,0:T(8,128)(2,1)S(1)}, bf16[5,128,384]{2,1,0:T(8,128)(2,1)S(1)}, u32[]{:S(2)}, u32[]{:S(2)}) %collective-permute-start.3) | collective-permute-done | bytes 491552 | tf_op jit(solution)/shard_map/ppermute | solution.py:113
  244.1 2.8 collective-permute-start.8
  246.9 1.3 collective-permute-start
  248.2 52.0 %collective-permute-done = bf16[5,128,384]{2,1,0:T(8,128)(2,1)S(1)} collective-permute-done((bf16[5,128,384]{2,1,0:T(8,128)(2,1)S(1)}, bf16[5,128,384]{2,1,0:T(8,128)(2,1)S(1)}, u32[]{:S(2)}, u32[]{:S(2)}) %collective-permute-start) | collective-permute-done | bytes 491552 | tf_op jit(solution)/shard_map/ppermute | solution.py:113
  300.2 1.2 collective-permute-start.13
  301.4 2.1 collective-permute-start.12
  303.5 0.8 collective-permute-start.11
  304.4 0.9 collective-permute-start.10
  305.3 1.5 maximum_bitcast_fusion.5
  306.8 1.5 maximum_bitcast_fusion.6
  308.2 0.7 maximum_bitcast_fusion.3
  308.9 43.2 %collective-permute-done.13 = bf16[5,384,256]{2,1,0:T(8,128)(2,1)S(1)} collective-permute-done((bf16[5,384,256]{2,1,0:T(8,128)(2,1)S(1)}, bf16[5,384,256]{2,1,0:T(8,128)(2,1)S(1)}, u32[]{:S(2)}, u32[]{:S(2)}) %collective-permute-start.13) | collective-permute-done | bytes 983072 | tf_op jit(solution)/shard_map/ppermute | solution.py:113
  352.1 43.1 %collective-permute-done.12 = bf16[5,384,256]{2,1,0:T(8,128)(2,1)S(1)} collective-permute-done((bf16[5,384,256]{2,1,0:T(8,128)(2,1)S(1)}, bf16[5,384,256]{2,1,0:T(8,128)(2,1)S(1)}, u32[]{:S(2)}, u32[]{:S(2)}) %collective-permute-start.12) | collective-permute-done | bytes 983072 | tf_op jit(solution)/shard_map/ppermute | solution.py:113
  395.2 0.7 maximum_bitcast_fusion.4
  395.9 1.7 copy-done.10
  397.6 5.6 %fusion.16 = f32[8,2,5,26,256]{4,3,0,1,2:T(8,128)} fusion(bf16[8,5,26,1536,1]{3,0,2,1,4:T(8,128)(2,1)} %bitcast.126, bf16[1,5,1536,256]{3,2,0,1:T(8,128)(2,1)S(1)} %maximum_bitcast_fusion.4, bf16[1,5,1536,256]{3,2,0,1:T(8,128)(2,1)S(1)} %maximum_bitcast_fusion.3), kind=kOutput, calls=%fused_computation.28 | convolution fusion | flops 1651507200 | bytes 13189120 | tf_op jit(solution)/shard_map/skmd,pkdf->spkmf/dot_general | solution.py:209
  403.2 4.1 fusion.9
  407.3 3.5 copy.91
  410.9 5.9 %fusion.13 = f32[8,2,5,26,256]{4,3,0,1,2:T(8,128)} fusion(bf16[1,5,1536,256]{3,2,0,1:T(8,128)(2,1)S(1)} %maximum_bitcast_fusion.4, bf16[1,5,1536,256]{3,2,0,1:T(8,128)(2,1)S(1)} %maximum_bitcast_fusion.3, bf16[8,5,26,1536]{3,2,1,0:T(8,128)(2,1)} %all-to-all-done), kind=kOutput, calls=%fused_computation.27 | convolution fusion | flops 1651507200 | bytes 13189120 | tf_op jit(solution)/shard_map/skmd,pkdf->spkmf/dot_general | solution.py:209
  416.8 2.1 fusion.20
  418.8 4.1 fusion
  423.0 3.0 copy.92
  426.0 4.9 all-to-all-start.1
  430.9 0.1 copy.93
  431.0 56.8 %all-to-all-done.1 = bf16[8,5,26,1536]{3,2,1,0:T(8,128)(2,1)} async-done(((bf16[8,5,26,1536]{3,2,1,0:T(8,128)(2,1)}), bf16[8,5,26,1536]{3,2,1,0:T(8,128)(2,1)}, u32[]{:S(2)}, u32[]{:S(2)}) %all-to-all-start.1) | async-done | bytes 3194912 | tf_op jit(solution)/shard_map/all_to_all | solution.py:218
  487.8 6.2 %reshape.319 = f32[1040,1536]{1,0:T(8,128)} reshape(bf16[8,5,26,1536]{3,2,1,0:T(8,128)(2,1)} %all-to-all-done.1) | data formatting | bytes 9584640 | tf_op jit(solution)/shard_map/reshape | solution.py:219
  494.0 10.6 %gather_fusion.2 = f32[1024,1536]{1,0:T(8,128)} fusion(f32[1040,1536]{1,0:T(8,128)} %reshape.319, s32[1024]{0:T(1024)S(1)} %broadcast_clamp_fusion), kind=kCustom, calls=%fused_computation.2 | custom fusion | bytes 12587008 | tf_op jit(solution)/shard_map/gather | solution.py:220
  504.6 5.2 fusion.1
  509.7 1.2 copy.94
  510.9 1.4 copy.95
  512.3 1.5 gather_fusion.3
  513.8 1.2 copy.114
  515.0 0.8 fusion.30
  (65 shorter events, 1.1 us)
Async XLA Ops:
  7.2 2.7 copy-start
  7.2 6.9 %copy-start.6 = (bf16[1,48,1024]{2,1,0:T(8,128)(2,1)S(1)}, bf16[1,48,1024]{2,1,0:T(8,128)(2,1)}, u32[]{:S(2)}) copy-start(bf16[1,48,1024]{2,1,0:T(8,128)(2,1)} %param.19) | copy-start | bytes 294916
  7.2 7.8 %copy-start.8 = (bf16[1536]{0:T(1024)(128)(2,1)S(1)}, bf16[1536]{0:T(1024)(128)(2,1)}, u32[]{:S(2)}) copy-start(bf16[1536]{0:T(1024)(128)(2,1)} %param.21) | copy-start | bytes 9220
  7.2 7.8 %copy-start.7 = (s32[128,8]{0,1:T(8,128)S(1)}, s32[128,8]{0,1:T(8,128)}, u32[]{:S(2)}) copy-start(s32[128,8]{0,1:T(8,128)} %param.22) | copy-start | bytes 12292
  7.2 70.4 %all-gather.2.cloned.1.call-start = ((), (), s32[]{:S(2)}) async-start(), calls=%async_computation.2 | async-start | bytes 11894784 | tf_op jit(solution)/shard_map/all_gather | solution.py:170
  9.9 10.7 %copy-start.2 = (bf16[128,1536]{1,0:T(8,128)(2,1)S(1)}, bf16[128,1536]{1,0:T(8,128)(2,1)}, u32[]{:S(2)}) copy-start(bf16[128,1536]{1,0:T(8,128)(2,1)} %param.13) | copy-start | bytes 1179652
  121.1 393.9 %copy-start.3 = (bf16[128,1536]{1,0:T(8,128)(2,1)}, bf16[128,1536]{1,0:T(8,128)(2,1)S(1)}, u32[]{:S(2)}) copy-start(bf16[128,1536]{1,0:T(8,128)(2,1)S(1)} %get-tuple-element.15) | copy-start | bytes 1179652
  132.7 5.1 copy-start.5
  132.7 69.6 %all-to-all-start = ((bf16[8,5,26,1536]{3,2,1,0:T(8,128)(2,1)}), bf16[8,5,26,1536]{3,2,1,0:T(8,128)(2,1)}, u32[]{:S(2)}, u32[]{:S(2)}) async-start(bf16[8,5,26,1536]{3,2,1,0:T(8,128)(2,1)} %reshape.329), calls=%async_computation | async-start | bytes 7864320 | tf_op jit(solution)/shard_map/all_to_all | solution.py:205
  137.8 96.3 %copy-start.4 = (bf16[1,5,384,256]{3,2,1,0:T(8,128)(2,1)S(1)}, bf16[1,5,384,256]{3,2,1,0:T(8,128)(2,1)}, u32[]{:S(2)}) copy-start(bf16[1,5,384,256]{3,2,1,0:T(8,128)(2,1)} %param.24) | copy-start | bytes 2949124
  137.9 74.7 %collective-permute-start.6 = (bf16[5,128,384]{2,1,0:T(8,128)(2,1)S(1)}, bf16[5,128,384]{2,1,0:T(8,128)(2,1)S(1)}, u32[]{:S(2)}, u32[]{:S(2)}) collective-permute-start(bf16[5,128,384]{2,1,0:T(8,128)(2,1)S(1)} %bitcast.114), channel_id=1, source_target_pairs={{0,98},{2,96},{32,2},{34,0},{64,34},{66,32},{96,66},{98,64},{1,99}... | collective-permute-start | bytes 1474568 | tf_op jit(solution)/shard_map/ppermute | solution.py:113
  206.2 189.7 %collective-permute-start.14 = (bf16[8,5,26,1536]{3,0,2,1:T(8,128)(2,1)S(1)}, bf16[8,5,26,1536]{3,0,2,1:T(8,128)(2,1)S(1)}, u32[]{:S(2)}, u32[]{:S(2)}) collective-permute-start(bf16[8,5,26,1536]{3,0,2,1:T(8,128)(2,1)S(1)} %copy.88), channel_id=1, source_target_pairs={{0,1},{1,0},{2,3},{3,2},{4,5},{5,4},{6,7},{7,6},{8,9},{9,8},{10,11... | collective-permute-start | bytes 9584648 | tf_op jit(solution)/shard_map/ppermute | solution.py:215
  206.3 17.6 %collective-permute-start.5 = (bf16[5,128,384]{2,1,0:T(8,128)(2,1)S(1)}, bf16[5,128,384]{2,1,0:T(8,128)(2,1)S(1)}, u32[]{:S(2)}, u32[]{:S(2)}) collective-permute-start(bf16[5,128,384]{2,1,0:T(8,128)(2,1)S(1)} %bitcast.115), channel_id=1, source_target_pairs={{0,66},{2,64},{32,98},{34,96},{64,2},{66,0},{96,34},{98,32},{1,67}... | collective-permute-start | bytes 1474568 | tf_op jit(solution)/shard_map/ppermute | solution.py:113
  211.3 22.9 %collective-permute-start.4 = (bf16[5,128,384]{2,1,0:T(8,128)(2,1)S(1)}, bf16[5,128,384]{2,1,0:T(8,128)(2,1)S(1)}, u32[]{:S(2)}, u32[]{:S(2)}) collective-permute-start(bf16[5,128,384]{2,1,0:T(8,128)(2,1)S(1)} %bitcast.116), channel_id=1, source_target_pairs={{0,34},{2,32},{32,66},{34,64},{64,98},{66,96},{96,2},{98,0},{1,35}... | collective-permute-start | bytes 1474568 | tf_op jit(solution)/shard_map/ppermute | solution.py:113
  211.3 32.9 %collective-permute-start.3 = (bf16[5,128,384]{2,1,0:T(8,128)(2,1)S(1)}, bf16[5,128,384]{2,1,0:T(8,128)(2,1)S(1)}, u32[]{:S(2)}, u32[]{:S(2)}) collective-permute-start(bf16[5,128,384]{2,1,0:T(8,128)(2,1)S(1)} %bitcast.117), channel_id=1, source_target_pairs={{0,2},{2,0},{32,34},{34,32},{64,66},{66,64},{96,98},{98,96},{1,3},... | collective-permute-start | bytes 1474568 | tf_op jit(solution)/shard_map/ppermute | solution.py:113
  212.5 34.4 %collective-permute-start.2 = (bf16[5,128,384]{2,1,0:T(8,128)(2,1)S(1)}, bf16[5,128,384]{2,1,0:T(8,128)(2,1)S(1)}, u32[]{:S(2)}, u32[]{:S(2)}) collective-permute-start(bf16[5,128,384]{2,1,0:T(8,128)(2,1)S(1)} %bitcast.118), channel_id=1, source_target_pairs={{0,96},{2,98},{32,0},{34,2},{64,32},{66,34},{96,64},{98,66},{1,97}... | collective-permute-start | bytes 1474568 | tf_op jit(solution)/shard_map/ppermute | solution.py:113
  223.9 23.0 %collective-permute-start.1 = (bf16[5,128,384]{2,1,0:T(8,128)(2,1)S(1)}, bf16[5,128,384]{2,1,0:T(8,128)(2,1)S(1)}, u32[]{:S(2)}, u32[]{:S(2)}) collective-permute-start(bf16[5,128,384]{2,1,0:T(8,128)(2,1)S(1)} %bitcast.119), channel_id=1, source_target_pairs={{0,64},{2,66},{32,96},{34,98},{64,0},{66,2},{96,32},{98,34},{1,65}... | collective-permute-start | bytes 1474568 | tf_op jit(solution)/shard_map/ppermute | solution.py:113
  234.2 67.2 %collective-permute-start.9 = (bf16[5,384,256]{2,1,0:T(8,128)(2,1)S(1)}, bf16[5,384,256]{2,1,0:T(8,128)(2,1)S(1)}, u32[]{:S(2)}, u32[]{:S(2)}) collective-permute-start(bf16[5,384,256]{2,1,0:T(8,128)(2,1)S(1)} %bitcast.105), channel_id=1, source_target_pairs={{0,96},{2,98},{32,0},{34,2},{64,32},{66,34},{96,64},{98,66},{1,97}... | collective-permute-start | bytes 2949128 | tf_op jit(solution)/shard_map/ppermute | solution.py:113
  244.1 59.4 %collective-permute-start.8 = (bf16[5,384,256]{2,1,0:T(8,128)(2,1)S(1)}, bf16[5,384,256]{2,1,0:T(8,128)(2,1)S(1)}, u32[]{:S(2)}, u32[]{:S(2)}) collective-permute-start(bf16[5,384,256]{2,1,0:T(8,128)(2,1)S(1)} %bitcast.106), channel_id=1, source_target_pairs={{0,64},{2,66},{32,96},{34,98},{64,0},{66,2},{96,32},{98,34},{1,65}... | collective-permute-start | bytes 2949128 | tf_op jit(solution)/shard_map/ppermute | solution.py:113
  246.9 57.5 %collective-permute-start.7 = (bf16[5,384,256]{2,1,0:T(8,128)(2,1)S(1)}, bf16[5,384,256]{2,1,0:T(8,128)(2,1)S(1)}, u32[]{:S(2)}, u32[]{:S(2)}) collective-permute-start(bf16[5,384,256]{2,1,0:T(8,128)(2,1)S(1)} %bitcast.107), channel_id=1, source_target_pairs={{0,32},{2,34},{32,64},{34,66},{64,96},{66,98},{96,0},{98,2},{1,33}... | collective-permute-start | bytes 2949128 | tf_op jit(solution)/shard_map/ppermute | solution.py:113
  246.9 53.3 %collective-permute-start = (bf16[5,128,384]{2,1,0:T(8,128)(2,1)S(1)}, bf16[5,128,384]{2,1,0:T(8,128)(2,1)S(1)}, u32[]{:S(2)}, u32[]{:S(2)}) collective-permute-start(bf16[5,128,384]{2,1,0:T(8,128)(2,1)S(1)} %bitcast.120), channel_id=1, source_target_pairs={{0,32},{2,34},{32,64},{34,66},{64,96},{66,98},{96,0},{98,2},{1,33}... | collective-permute-start | bytes 1474568 | tf_op jit(solution)/shard_map/ppermute | solution.py:113
  300.2 51.9 %collective-permute-start.13 = (bf16[5,384,256]{2,1,0:T(8,128)(2,1)S(1)}, bf16[5,384,256]{2,1,0:T(8,128)(2,1)S(1)}, u32[]{:S(2)}, u32[]{:S(2)}) collective-permute-start(bf16[5,384,256]{2,1,0:T(8,128)(2,1)S(1)} %bitcast.108), channel_id=1, source_target_pairs={{0,98},{2,96},{32,2},{34,0},{64,34},{66,32},{96,66},{98,64},{1,99}... | collective-permute-start | bytes 2949128 | tf_op jit(solution)/shard_map/ppermute | solution.py:113
  301.4 93.8 %collective-permute-start.12 = (bf16[5,384,256]{2,1,0:T(8,128)(2,1)S(1)}, bf16[5,384,256]{2,1,0:T(8,128)(2,1)S(1)}, u32[]{:S(2)}, u32[]{:S(2)}) collective-permute-start(bf16[5,384,256]{2,1,0:T(8,128)(2,1)S(1)} %bitcast.109), channel_id=1, source_target_pairs={{0,66},{2,64},{32,98},{34,96},{64,2},{66,0},{96,34},{98,32},{1,67}... | collective-permute-start | bytes 2949128 | tf_op jit(solution)/shard_map/ppermute | solution.py:113
  303.5 91.7 %collective-permute-start.11 = (bf16[5,384,256]{2,1,0:T(8,128)(2,1)S(1)}, bf16[5,384,256]{2,1,0:T(8,128)(2,1)S(1)}, u32[]{:S(2)}, u32[]{:S(2)}) collective-permute-start(bf16[5,384,256]{2,1,0:T(8,128)(2,1)S(1)} %bitcast.110), channel_id=1, source_target_pairs={{0,34},{2,32},{32,66},{34,64},{64,98},{66,96},{96,2},{98,0},{1,35}... | collective-permute-start | bytes 2949128 | tf_op jit(solution)/shard_map/ppermute | solution.py:113
  304.4 90.8 %collective-permute-start.10 = (bf16[5,384,256]{2,1,0:T(8,128)(2,1)S(1)}, bf16[5,384,256]{2,1,0:T(8,128)(2,1)S(1)}, u32[]{:S(2)}, u32[]{:S(2)}) collective-permute-start(bf16[5,384,256]{2,1,0:T(8,128)(2,1)S(1)} %bitcast.111), channel_id=1, source_target_pairs={{0,2},{2,0},{32,34},{34,32},{64,66},{66,64},{96,98},{98,96},{1,3},... | collective-permute-start | bytes 2949128 | tf_op jit(solution)/shard_map/ppermute | solution.py:113
  395.9 1.7 copy-start.10
  410.9 8.0 %collective-permute-start.15 = (bf16[8,5,26,1536]{3,0,2,1:T(8,128)(2,1)}, bf16[8,5,26,1536]{3,0,2,1:T(8,128)(2,1)}, u32[]{:S(2)}, u32[]{:S(2)}) collective-permute-start(bf16[8,5,26,1536]{3,0,2,1:T(8,128)(2,1)} %copy.91), channel_id=1, source_target_pairs={{0,1},{1,0},{2,3},{3,2},{4,5},{5,4},{6,7},{7,6},{8,9},{9,8},{10,11... | collective-permute-start | bytes 9584648 | tf_op jit(solution)/shard_map/ppermute | solution.py:216
  426.0 4.9 copy-start.9
  426.0 61.9 %all-to-all-start.1 = ((bf16[8,5,26,1536]{3,2,1,0:T(8,128)(2,1)}), bf16[8,5,26,1536]{3,2,1,0:T(8,128)(2,1)}, u32[]{:S(2)}, u32[]{:S(2)}) async-start(bf16[8,5,26,1536]{3,2,1,0:T(8,128)(2,1)} %copy.92), calls=%async_computation.1 | async-start | bytes 7864320 | tf_op jit(solution)/shard_map/all_to_all | solution.py:218
  504.6 11.3 %copy-start.1 = (bf16[1536,512]{1,0:T(8,128)(2,1)S(1)}, bf16[1536,512]{1,0:T(8,128)(2,1)}, u32[]{:S(2)}) copy-start(bf16[1536,512]{1,0:T(8,128)(2,1)} %param.17) | copy-start | bytes 4718596
Sparse Core Ops, SparseCore 0:
  15.0 62.5 all-gather.1

commit v10 on v9

--- a/solution.py
+++ b/solution.py
@@ -95,24 +95,22 @@
     )(bounds, limit, query, keys, keys)
 
 
-def spread_pieces(local, width_axis):
+def permute_piece(local, dr, dz):
     req_count = lax.axis_size("req")
     pair = lax.axis_size("zlo")
-    stacked = []
-    for dz in range(pair):
-        chunks = []
-        for dr in range(req_count):
-            if dr == 0 and dz == 0:
-                chunks.append(local)
-                continue
-            perm = [
-                (a * pair + z, ((a + dr) % req_count) * pair + (z + dz) % pair)
-                for a in range(req_count)
-                for z in range(pair)
-            ]
-            chunks.append(lax.ppermute(local, ("req", "zlo"), perm))
-        stacked.append(jnp.concatenate(chunks, axis=width_axis))
-    return jnp.stack(stacked, axis=0)
+    perm = [
+        (a * pair + z, ((a + dr) % req_count) * pair + (z + dz) % pair)
+        for a in range(req_count)
+        for z in range(pair)
+    ]
+    return lax.ppermute(local, ("req", "zlo"), perm)
+
+
+def spread_pieces(local, width_axis, near, far):
+    return jnp.stack(
+        [jnp.concatenate([local] + near, axis=width_axis), jnp.concatenate(far, axis=width_axis)],
+        axis=0,
+    )
 
 
 def in_chunk_order(rows, chunk_order):
@@ -152,6 +150,8 @@
     cache_count = cache_rows.shape[0]
     req_index = lax.axis_index("req")
     chunk_order = (req_index - jnp.arange(lax.axis_size("req"), dtype=jnp.int32)) % lax.axis_size("req")
+    gate_up_near = [permute_piece(w_gate_up[0], dr, 0) for dr in range(1, lax.axis_size("req"))]
+    down_near = [permute_piece(w_down[0], dr, 0) for dr in range(1, lax.axis_size("req"))]
     normed = rms_scale(hidden_in, attn_gain)
     query_pos = position_exp * rows_here + jnp.arange(rows_here, dtype=jnp.int32)
     positions = length + query_pos
@@ -169,8 +169,11 @@
     joined = jnp.concatenate([cache_rows, new_kv], axis=0)
     piece = lax.all_gather(joined, EXP_AXES, axis=0, tiled=True)
     gate_up_local, down_local, piece = lax.optimization_barrier((w_gate_up[0], w_down[0], piece))
-    gate_up_full = spread_pieces(gate_up_local, 1)
-    down_full = spread_pieces(down_local, 2)
+    req_count = lax.axis_size("req")
+    gate_up_far = [permute_piece(gate_up_local, dr, 1) for dr in range(req_count)]
+    down_far = [permute_piece(down_local, dr, 1) for dr in range(req_count)]
+    gate_up_full = spread_pieces(w_gate_up[0], 1, gate_up_near, gate_up_far)
+    down_full = spread_pieces(w_down[0], 2, down_near, down_far)
     shard_rows = cache_count + rows_here
     key_index = jnp.arange(piece.shape[0], dtype=jnp.int32)
     owner = key_index // shard_rows

time: 528 us -> 535 us (1.013)
  the two profiles are of different devices: /device:TPU:8 before, /device:TPU:0 now
where the time goes in v10:
time: 535 us; the launch traced here: 527 us
  waiting for transfers between devices  335 us (63%)
  local copies, waits for them, and re-layouts  51.7 us (10%)
  Pallas kernels  40.1 us (7%)
  starting transfers between devices  37.1 us (7%)
  matrix products  31.7 us (6%)
  other arithmetic  16.4 us (3%)
  between operations  15.4 us (3%)
    ppermute x14, waiting for transfers between devices, permute_piece(): return lax.ppermute(local, ('req', 'zlo'), perm)  174 us
    all_to_all x1, waiting for transfers between devices, shards(): lax.all_to_all(computed, ('x', 'zhi'), split_axis=0, concat_axis=0, tiled...  56.6 us
    all_to_all x1, waiting for transfers between devices, shards(): lax.all_to_all(outgoing, ('x', 'zhi'), split_axis=0, concat_axis=0, tiled...  53.2 us
    all_gather x1, waiting for transfers between devices, shards(): piece = lax.all_gather(joined, EXP_AXES, axis=0, tiled=True)  51 us
    pallas_call x1, Pallas kernels, attend(): pl.pallas_call(kernel, grid_spec=grid_spec, out_shape=jax.ShapeDtypeStruc...  40.1 us
    ppermute x14, starting transfers between devices, permute_piece(): return lax.ppermute(local, ('req', 'zlo'), perm)  26.2 us
    dot_general x2, matrix products, experts_on(): jnp.einsum('skmd,pkdf->spkmf', rows_in, gate_up_full, preferred_element_t...  11.5 us
  transfers between devices with their start and end apart: 19, of which 10 were waited for; matrix products, arithmetic and copies ran while one was open for 5% of the time, Pallas kernels for 0%

profile of v10, /device:TPU:0, one launch (start us, length us, event | category | flops | bytes accessed | tf_op | source)
XLA Modules:
  0.0 527.2 jit_solution(15656000591600629156)
XLA Ops:
  8.0 1.2 fusion.24
  9.2 0.7 convert_element_type.81
  9.9 1.5 convolution_convert_fusion
  11.4 2.3 fusion.49
  13.7 0.1 multiply_cosine_fusion
  13.9 0.1 copy.77
  14.1 0.8 maximum_maximum_fusion
  15.4 0.6 fusion.23
  16.0 4.3 scatter_custom_fusion
  20.5 0.1 reshape.330
  20.6 4.3 fusion.51
  25.1 0.9 copy.78.q_ref
  26.0 0.7 compare_select_fusion.2.lim_ref
  26.7 51.0 %all-gather.2.cloned.1.call-done.k_ref.v_ref = bf16[5632,1024]{1,0:T(8,128)(2,1)} async-done(((bf16[176,1024]{1,0:T(8,128)(2,1)}), bf16[5632,1024]{1,0:T(8,128)(2,1)}) %all-gather.2.cloned.1.call-update) | async-done | bytes 11534352 | tf_op jit(solution)/shard_map/all_gather | solution.py:170
  77.8 40.1 %shard_map.140 = bf16[128,1536]{1,0:T(8,128)(2,1)} custom-call(s32[1]{0:T(128)} %bitcast.bounds_ref, s32[1,5632]{1,0:T(1,128)} %compare_select_fusion.2.lim_ref, bf16[128,1536]{1,0:T(8,128)(2,1)} %copy.78.q_ref, bf16[5632,1024]{1,0:T(8,128)(2,1)} %all-gather.2.cloned.1.call-done.k_ref.v_ref, bf16[5632,1024]{1,0:T(8,128)(2,1)} %all-gather.2.cloned.1.call-done.k_ref.v_ref), custom_call_target="tpu_custom_call" | custom-call | tf_op jit(solution)/shard_map/pallas_call | solution.py:89
  117.9 3.3 fusion.27
  121.3 0.2 fusion.29
  121.5 0.6 gather_fusion
  122.2 5.2 gather_fusion.1
  127.4 5.5 %reshape.329 = bf16[8,5,26,1536]{3,2,1,0:T(8,128)(2,1)} reshape(bf16[1040,1536]{1,0:T(8,128)(2,1)} %gather_fusion.1) | data formatting | bytes 6389760 | tf_op jit(solution)/shard_map/gather | solution.py:207
  132.9 5.1 all-to-all-start
  138.1 3.3 collective-permute-start.2
  141.4 53.2 %all-to-all-done = bf16[8,5,26,1536]{3,2,1,0:T(8,128)(2,1)} async-done(((bf16[8,5,26,1536]{3,2,1,0:T(8,128)(2,1)}), bf16[8,5,26,1536]{3,2,1,0:T(8,128)(2,1)}, u32[]{:S(2)}, u32[]{:S(2)}) %all-to-all-start) | async-done | bytes 3194912 | tf_op jit(solution)/shard_map/all_to_all | solution.py:208
  194.5 3.9 copy.88
  198.5 3.1 collective-permute-start.1
  201.6 1.2 collective-permute-start.9
  202.8 1.5 collective-permute-start.8
  204.3 10.0 %collective-permute-done.1 = bf16[5,128,384]{2,1,0:T(8,128)(2,1)S(1)} collective-permute-done((bf16[5,128,384]{2,1,0:T(8,128)(2,1)S(1)}, bf16[5,128,384]{2,1,0:T(8,128)(2,1)S(1)}, u32[]{:S(2)}, u32[]{:S(2)}) %collective-permute-start.1) | collective-permute-done | bytes 491552 | tf_op jit(solution)/shard_map/ppermute | solution.py:106
  214.3 1.5 collective-permute-start
  215.8 50.6 %collective-permute-done = bf16[5,128,384]{2,1,0:T(8,128)(2,1)S(1)} collective-permute-done((bf16[5,128,384]{2,1,0:T(8,128)(2,1)S(1)}, bf16[5,128,384]{2,1,0:T(8,128)(2,1)S(1)}, u32[]{:S(2)}, u32[]{:S(2)}) %collective-permute-start) | collective-permute-done | bytes 491552 | tf_op jit(solution)/shard_map/ppermute | solution.py:106
  266.3 0.8 collective-permute-start.6
  267.2 3.7 collective-permute-start.5
  270.9 1.0 collective-permute-start.4
  271.9 1.3 collective-permute-start.3
  273.1 21.1 %collective-permute-done.6 = bf16[5,128,384]{2,1,0:T(8,128)(2,1)S(1)} collective-permute-done((bf16[5,128,384]{2,1,0:T(8,128)(2,1)S(1)}, bf16[5,128,384]{2,1,0:T(8,128)(2,1)S(1)}, u32[]{:S(2)}, u32[]{:S(2)}) %collective-permute-start.6) | collective-permute-done | bytes 491552 | tf_op jit(solution)/shard_map/ppermute | solution.py:106
  294.3 4.9 collective-permute-start.13
  299.1 3.0 collective-permute-start.12
  302.2 31.6 %collective-permute-done.4 = bf16[5,128,384]{2,1,0:T(8,128)(2,1)S(1)} collective-permute-done((bf16[5,128,384]{2,1,0:T(8,128)(2,1)S(1)}, bf16[5,128,384]{2,1,0:T(8,128)(2,1)S(1)}, u32[]{:S(2)}, u32[]{:S(2)}) %collective-permute-start.4) | collective-permute-done | bytes 491552 | tf_op jit(solution)/shard_map/ppermute | solution.py:106
  333.8 41.4 %collective-permute-done.3 = bf16[5,128,384]{2,1,0:T(8,128)(2,1)S(1)} collective-permute-done((bf16[5,128,384]{2,1,0:T(8,128)(2,1)S(1)}, bf16[5,128,384]{2,1,0:T(8,128)(2,1)S(1)}, u32[]{:S(2)}, u32[]{:S(2)}) %collective-permute-start.3) | collective-permute-done | bytes 491552 | tf_op jit(solution)/shard_map/ppermute | solution.py:106
  375.2 1.0 collective-permute-start.10
  376.1 1.5 maximum_bitcast_fusion.5
  377.6 0.7 maximum_bitcast_fusion.3
  378.3 1.5 maximum_bitcast_fusion.6
  379.8 6.0 %collective-permute-done.11 = bf16[5,384,256]{2,1,0:T(8,128)(2,1)S(1)} collective-permute-done((bf16[5,384,256]{2,1,0:T(8,128)(2,1)S(1)}, bf16[5,384,256]{2,1,0:T(8,128)(2,1)S(1)}, u32[]{:S(2)}, u32[]{:S(2)}) %collective-permute-start.11) | collective-permute-done | bytes 983072 | tf_op jit(solution)/shard_map/ppermute | solution.py:106
  385.8 13.2 %collective-permute-done.10 = bf16[5,384,256]{2,1,0:T(8,128)(2,1)S(1)} collective-permute-done((bf16[5,384,256]{2,1,0:T(8,128)(2,1)S(1)}, bf16[5,384,256]{2,1,0:T(8,128)(2,1)S(1)}, u32[]{:S(2)}, u32[]{:S(2)}) %collective-permute-start.10) | collective-permute-done | bytes 983072 | tf_op jit(solution)/shard_map/ppermute | solution.py:106
  399.0 0.7 maximum_bitcast_fusion.4
  399.7 1.7 copy-done.10
  401.4 5.6 %fusion.16 = f32[8,2,5,26,256]{4,3,0,1,2:T(8,128)} fusion(bf16[8,5,26,1536,1]{3,0,2,1,4:T(8,128)(2,1)} %bitcast.126, bf16[1,5,1536,256]{3,2,0,1:T(8,128)(2,1)S(1)} %maximum_bitcast_fusion.4, bf16[1,5,1536,256]{3,2,0,1:T(8,128)(2,1)S(1)} %maximum_bitcast_fusion.3), kind=kOutput, calls=%fused_computation.28 | convolution fusion | flops 1651507200 | bytes 13189120 | tf_op jit(solution)/shard_map/skmd,pkdf->spkmf/dot_general | solution.py:212
  407.0 4.1 fusion.9
  411.1 3.5 copy.91
  414.6 5.9 %fusion.13 = f32[8,2,5,26,256]{4,3,0,1,2:T(8,128)} fusion(bf16[1,5,1536,256]{3,2,0,1:T(8,128)(2,1)S(1)} %maximum_bitcast_fusion.4, bf16[1,5,1536,256]{3,2,0,1:T(8,128)(2,1)S(1)} %maximum_bitcast_fusion.3, bf16[8,5,26,1536]{3,2,1,0:T(8,128)(2,1)} %all-to-all-done), kind=kOutput, calls=%fused_computation.27 | convolution fusion | flops 1651507200 | bytes 13189120 | tf_op jit(solution)/shard_map/skmd,pkdf->spkmf/dot_general | solution.py:212
  420.5 2.1 fusion.20
  422.6 4.1 fusion
  426.7 3.0 copy.92
  429.7 5.7 %all-to-all-start.1 = ((bf16[8,5,26,1536]{3,2,1,0:T(8,128)(2,1)}), bf16[8,5,26,1536]{3,2,1,0:T(8,128)(2,1)}, u32[]{:S(2)}, u32[]{:S(2)}) async-start(bf16[8,5,26,1536]{3,2,1,0:T(8,128)(2,1)} %copy.92), calls=%async_computation.1 | async-start | bytes 7864320 | tf_op jit(solution)/shard_map/all_to_all | solution.py:221
  435.5 56.6 %all-to-all-done.1 = bf16[8,5,26,1536]{3,2,1,0:T(8,128)(2,1)} async-done(((bf16[8,5,26,1536]{3,2,1,0:T(8,128)(2,1)}), bf16[8,5,26,1536]{3,2,1,0:T(8,128)(2,1)}, u32[]{:S(2)}, u32[]{:S(2)}) %all-to-all-start.1) | async-done | bytes 3194912 | tf_op jit(solution)/shard_map/all_to_all | solution.py:221
  492.1 6.2 %reshape.319 = f32[1040,1536]{1,0:T(8,128)} reshape(bf16[8,5,26,1536]{3,2,1,0:T(8,128)(2,1)} %all-to-all-done.1) | data formatting | bytes 9584640 | tf_op jit(solution)/shard_map/reshape | solution.py:222
  498.3 10.6 %gather_fusion.2 = f32[1024,1536]{1,0:T(8,128)} fusion(f32[1040,1536]{1,0:T(8,128)} %reshape.319, s32[1024]{0:T(1024)S(1)} %broadcast_clamp_fusion), kind=kCustom, calls=%fused_computation.2 | custom fusion | bytes 12587008 | tf_op jit(solution)/shard_map/gather | solution.py:223
  508.9 5.2 fusion.1
  514.0 1.2 copy.94
  515.2 1.4 copy.95
  516.6 1.5 gather_fusion.3
  518.1 1.2 copy.114
  519.3 0.8 fusion.30
  (65 shorter events, 1.4 us)
Async XLA Ops:
  7.2 2.7 copy-start
  7.2 6.9 %copy-start.6 = (bf16[1,48,1024]{2,1,0:T(8,128)(2,1)S(1)}, bf16[1,48,1024]{2,1,0:T(8,128)(2,1)}, u32[]{:S(2)}) copy-start(bf16[1,48,1024]{2,1,0:T(8,128)(2,1)} %param.19) | copy-start | bytes 294916
  7.2 7.8 %copy-start.8 = (bf16[1536]{0:T(1024)(128)(2,1)S(1)}, bf16[1536]{0:T(1024)(128)(2,1)}, u32[]{:S(2)}) copy-start(bf16[1536]{0:T(1024)(128)(2,1)} %param.21) | copy-start | bytes 9220
  7.2 7.8 %copy-start.7 = (s32[128,8]{0,1:T(8,128)S(1)}, s32[128,8]{0,1:T(8,128)}, u32[]{:S(2)}) copy-start(s32[128,8]{0,1:T(8,128)} %param.22) | copy-start | bytes 12292
  7.2 70.6 %all-gather.2.cloned.1.call-start = ((), (), s32[]{:S(2)}) async-start(), calls=%async_computation.2 | async-start | bytes 11894784 | tf_op jit(solution)/shard_map/all_gather | solution.py:170
  9.9 10.7 %copy-start.2 = (bf16[128,1536]{1,0:T(8,128)(2,1)S(1)}, bf16[128,1536]{1,0:T(8,128)(2,1)}, u32[]{:S(2)}) copy-start(bf16[128,1536]{1,0:T(8,128)(2,1)} %param.13) | copy-start | bytes 1179652
  121.3 398.0 %copy-start.3 = (bf16[128,1536]{1,0:T(8,128)(2,1)}, bf16[128,1536]{1,0:T(8,128)(2,1)S(1)}, u32[]{:S(2)}) copy-start(bf16[128,1536]{1,0:T(8,128)(2,1)S(1)} %get-tuple-element.15) | copy-start | bytes 1179652
  132.9 5.1 copy-start.5
  132.9 61.6 %all-to-all-start = ((bf16[8,5,26,1536]{3,2,1,0:T(8,128)(2,1)}), bf16[8,5,26,1536]{3,2,1,0:T(8,128)(2,1)}, u32[]{:S(2)}, u32[]{:S(2)}) async-start(bf16[8,5,26,1536]{3,2,1,0:T(8,128)(2,1)} %reshape.329), calls=%async_computation | async-start | bytes 7864320 | tf_op jit(solution)/shard_map/all_to_all | solution.py:208
  138.0 63.6 %copy-start.4 = (bf16[1,5,384,256]{3,2,1,0:T(8,128)(2,1)S(1)}, bf16[1,5,384,256]{3,2,1,0:T(8,128)(2,1)}, u32[]{:S(2)}) copy-start(bf16[1,5,384,256]{3,2,1,0:T(8,128)(2,1)} %param.24) | copy-start | bytes 2949124
  138.1 66.2 %collective-permute-start.2 = (bf16[5,128,384]{2,1,0:T(8,128)(2,1)S(1)}, bf16[5,128,384]{2,1,0:T(8,128)(2,1)S(1)}, u32[]{:S(2)}, u32[]{:S(2)}) collective-permute-start(bf16[5,128,384]{2,1,0:T(8,128)(2,1)S(1)} %bitcast.114), channel_id=1, source_target_pairs={{0,96},{2,98},{32,0},{34,2},{64,32},{66,34},{96,64},{98,66},{1,97}... | collective-permute-start | bytes 1474568 | tf_op jit(solution)/shard_map/ppermute | solution.py:106
  198.4 201.3 %collective-permute-start.14 = (bf16[8,5,26,1536]{3,0,2,1:T(8,128)(2,1)S(1)}, bf16[8,5,26,1536]{3,0,2,1:T(8,128)(2,1)S(1)}, u32[]{:S(2)}, u32[]{:S(2)}) collective-permute-start(bf16[8,5,26,1536]{3,0,2,1:T(8,128)(2,1)S(1)} %copy.88), channel_id=1, source_target_pairs={{0,1},{1,0},{2,3},{3,2},{4,5},{5,4},{6,7},{7,6},{8,9},{9,8},{10,11... | collective-permute-start | bytes 9584648 | tf_op jit(solution)/shard_map/ppermute | solution.py:218
  198.5 15.8 %collective-permute-start.1 = (bf16[5,128,384]{2,1,0:T(8,128)(2,1)S(1)}, bf16[5,128,384]{2,1,0:T(8,128)(2,1)S(1)}, u32[]{:S(2)}, u32[]{:S(2)}) collective-permute-start(bf16[5,128,384]{2,1,0:T(8,128)(2,1)S(1)} %bitcast.115), channel_id=1, source_target_pairs={{0,64},{2,66},{32,96},{34,98},{64,0},{66,2},{96,32},{98,34},{1,65}... | collective-permute-start | bytes 1474568 | tf_op jit(solution)/shard_map/ppermute | solution.py:106
  201.6 65.6 %collective-permute-start.9 = (bf16[5,384,256]{2,1,0:T(8,128)(2,1)S(1)}, bf16[5,384,256]{2,1,0:T(8,128)(2,1)S(1)}, u32[]{:S(2)}, u32[]{:S(2)}) collective-permute-start(bf16[5,384,256]{2,1,0:T(8,128)(2,1)S(1)} %bitcast.105), channel_id=1, source_target_pairs={{0,96},{2,98},{32,0},{34,2},{64,32},{66,34},{96,64},{98,66},{1,97}... | collective-permute-start | bytes 2949128 | tf_op jit(solution)/shard_map/ppermute | solution.py:106
  202.8 68.0 %collective-permute-start.8 = (bf16[5,384,256]{2,1,0:T(8,128)(2,1)S(1)}, bf16[5,384,256]{2,1,0:T(8,128)(2,1)S(1)}, u32[]{:S(2)}, u32[]{:S(2)}) collective-permute-start(bf16[5,384,256]{2,1,0:T(8,128)(2,1)S(1)} %bitcast.106), channel_id=1, source_target_pairs={{0,64},{2,66},{32,96},{34,98},{64,0},{66,2},{96,32},{98,34},{1,65}... | collective-permute-start | bytes 2949128 | tf_op jit(solution)/shard_map/ppermute | solution.py:106
  204.3 67.6 %collective-permute-start.7 = (bf16[5,384,256]{2,1,0:T(8,128)(2,1)S(1)}, bf16[5,384,256]{2,1,0:T(8,128)(2,1)S(1)}, u32[]{:S(2)}, u32[]{:S(2)}) collective-permute-start(bf16[5,384,256]{2,1,0:T(8,128)(2,1)S(1)} %bitcast.107), channel_id=1, source_target_pairs={{0,32},{2,34},{32,64},{34,66},{64,96},{66,98},{96,0},{98,2},{1,33}... | collective-permute-start | bytes 2949128 | tf_op jit(solution)/shard_map/ppermute | solution.py:106
  214.3 52.0 %collective-permute-start = (bf16[5,128,384]{2,1,0:T(8,128)(2,1)S(1)}, bf16[5,128,384]{2,1,0:T(8,128)(2,1)S(1)}, u32[]{:S(2)}, u32[]{:S(2)}) collective-permute-start(bf16[5,128,384]{2,1,0:T(8,128)(2,1)S(1)} %bitcast.116), channel_id=1, source_target_pairs={{0,32},{2,34},{32,64},{34,66},{64,96},{66,98},{96,0},{98,2},{1,33}... | collective-permute-start | bytes 1474568 | tf_op jit(solution)/shard_map/ppermute | solution.py:106
  266.3 27.9 %collective-permute-start.6 = (bf16[5,128,384]{2,1,0:T(8,128)(2,1)S(1)}, bf16[5,128,384]{2,1,0:T(8,128)(2,1)S(1)}, u32[]{:S(2)}, u32[]{:S(2)}) collective-permute-start(bf16[5,128,384]{2,1,0:T(8,128)(2,1)S(1)} %bitcast.117), channel_id=1, source_target_pairs={{0,98},{2,96},{32,2},{34,0},{64,34},{66,32},{96,66},{98,64},{1,99}... | collective-permute-start | bytes 1474568 | tf_op jit(solution)/shard_map/ppermute | solution.py:106
  267.2 31.9 %collective-permute-start.5 = (bf16[5,128,384]{2,1,0:T(8,128)(2,1)S(1)}, bf16[5,128,384]{2,1,0:T(8,128)(2,1)S(1)}, u32[]{:S(2)}, u32[]{:S(2)}) collective-permute-start(bf16[5,128,384]{2,1,0:T(8,128)(2,1)S(1)} %bitcast.118), channel_id=1, source_target_pairs={{0,66},{2,64},{32,98},{34,96},{64,2},{66,0},{96,34},{98,32},{1,67}... | collective-permute-start | bytes 1474568 | tf_op jit(solution)/shard_map/ppermute | solution.py:106
  270.9 62.9 %collective-permute-start.4 = (bf16[5,128,384]{2,1,0:T(8,128)(2,1)S(1)}, bf16[5,128,384]{2,1,0:T(8,128)(2,1)S(1)}, u32[]{:S(2)}, u32[]{:S(2)}) collective-permute-start(bf16[5,128,384]{2,1,0:T(8,128)(2,1)S(1)} %bitcast.119), channel_id=1, source_target_pairs={{0,34},{2,32},{32,66},{34,64},{64,98},{66,96},{96,2},{98,0},{1,35}... | collective-permute-start | bytes 1474568 | tf_op jit(solution)/shard_map/ppermute | solution.py:106
  271.9 103.3 %collective-permute-start.3 = (bf16[5,128,384]{2,1,0:T(8,128)(2,1)S(1)}, bf16[5,128,384]{2,1,0:T(8,128)(2,1)S(1)}, u32[]{:S(2)}, u32[]{:S(2)}) collective-permute-start(bf16[5,128,384]{2,1,0:T(8,128)(2,1)S(1)} %bitcast.120), channel_id=1, source_target_pairs={{0,2},{2,0},{32,34},{34,32},{64,66},{66,64},{96,98},{98,96},{1,3},... | collective-permute-start | bytes 1474568 | tf_op jit(solution)/shard_map/ppermute | solution.py:106
  294.3 85.5 %collective-permute-start.13 = (bf16[5,384,256]{2,1,0:T(8,128)(2,1)S(1)}, bf16[5,384,256]{2,1,0:T(8,128)(2,1)S(1)}, u32[]{:S(2)}, u32[]{:S(2)}) collective-permute-start(bf16[5,384,256]{2,1,0:T(8,128)(2,1)S(1)} %bitcast.108), channel_id=1, source_target_pairs={{0,98},{2,96},{32,2},{34,0},{64,34},{66,32},{96,66},{98,64},{1,99}... | collective-permute-start | bytes 2949128 | tf_op jit(solution)/shard_map/ppermute | solution.py:106
  299.1 80.7 %collective-permute-start.12 = (bf16[5,384,256]{2,1,0:T(8,128)(2,1)S(1)}, bf16[5,384,256]{2,1,0:T(8,128)(2,1)S(1)}, u32[]{:S(2)}, u32[]{:S(2)}) collective-permute-start(bf16[5,384,256]{2,1,0:T(8,128)(2,1)S(1)} %bitcast.109), channel_id=1, source_target_pairs={{0,66},{2,64},{32,98},{34,96},{64,2},{66,0},{96,34},{98,32},{1,67}... | collective-permute-start | bytes 2949128 | tf_op jit(solution)/shard_map/ppermute | solution.py:106
  333.8 52.0 %collective-permute-start.11 = (bf16[5,384,256]{2,1,0:T(8,128)(2,1)S(1)}, bf16[5,384,256]{2,1,0:T(8,128)(2,1)S(1)}, u32[]{:S(2)}, u32[]{:S(2)}) collective-permute-start(bf16[5,384,256]{2,1,0:T(8,128)(2,1)S(1)} %bitcast.110), channel_id=1, source_target_pairs={{0,34},{2,32},{32,66},{34,64},{64,98},{66,96},{96,2},{98,0},{1,35}... | collective-permute-start | bytes 2949128 | tf_op jit(solution)/shard_map/ppermute | solution.py:106
  375.2 23.8 %collective-permute-start.10 = (bf16[5,384,256]{2,1,0:T(8,128)(2,1)S(1)}, bf16[5,384,256]{2,1,0:T(8,128)(2,1)S(1)}, u32[]{:S(2)}, u32[]{:S(2)}) collective-permute-start(bf16[5,384,256]{2,1,0:T(8,128)(2,1)S(1)} %bitcast.111), channel_id=1, source_target_pairs={{0,2},{2,0},{32,34},{34,32},{64,66},{66,64},{96,98},{98,96},{1,3},... | collective-permute-start | bytes 2949128 | tf_op jit(solution)/shard_map/ppermute | solution.py:106
  399.7 1.7 copy-start.10
  414.6 8.0 %collective-permute-start.15 = (bf16[8,5,26,1536]{3,0,2,1:T(8,128)(2,1)}, bf16[8,5,26,1536]{3,0,2,1:T(8,128)(2,1)}, u32[]{:S(2)}, u32[]{:S(2)}) collective-permute-start(bf16[8,5,26,1536]{3,0,2,1:T(8,128)(2,1)} %copy.91), channel_id=1, source_target_pairs={{0,1},{1,0},{2,3},{3,2},{4,5},{5,4},{6,7},{7,6},{8,9},{9,8},{10,11... | collective-permute-start | bytes 9584648 | tf_op jit(solution)/shard_map/ppermute | solution.py:219
  429.7 5.7 %copy-start.9 = (bf16[128,8]{0,1:T(8,128)(2,1)S(1)}, bf16[128,8]{0,1:T(8,128)(2,1)}, u32[]{:S(2)}) copy-start(bf16[128,8]{0,1:T(8,128)(2,1)} %param.23) | copy-start | bytes 6148
  429.7 62.4 %all-to-all-start.1 = ((bf16[8,5,26,1536]{3,2,1,0:T(8,128)(2,1)}), bf16[8,5,26,1536]{3,2,1,0:T(8,128)(2,1)}, u32[]{:S(2)}, u32[]{:S(2)}) async-start(bf16[8,5,26,1536]{3,2,1,0:T(8,128)(2,1)} %copy.92), calls=%async_computation.1 | async-start | bytes 7864320 | tf_op jit(solution)/shard_map/all_to_all | solution.py:221
  508.9 11.3 %copy-start.1 = (bf16[1536,512]{1,0:T(8,128)(2,1)S(1)}, bf16[1536,512]{1,0:T(8,128)(2,1)}, u32[]{:S(2)}) copy-start(bf16[1536,512]{1,0:T(8,128)(2,1)} %param.17) | copy-start | bytes 4718596
Sparse Core Ops, SparseCore 0:
  15.0 62.7 all-gather.1

commit v11 on v10

--- a/solution.py
+++ b/solution.py
@@ -204,7 +204,9 @@
     token_of = jnp.arange(flat_ids.shape[0], dtype=jnp.int32) // TOPK
     slot_token = jnp.zeros((EXPERTS * MOST,), jnp.int32).at[slot_index].set(token_of)
     blocks = EXPERTS // block_experts
-    outgoing = moe_in[slot_token.reshape(blocks, block_experts, MOST)]
+    pick = (slot_token[:, None] == jnp.arange(rows_here, dtype=jnp.int32)[None, :]).astype(jnp.bfloat16)
+    outgoing = jnp.dot(pick, moe_in, preferred_element_type=jnp.float32).astype(jnp.bfloat16)
+    outgoing = outgoing.reshape(blocks, block_experts, MOST, width)
     arrived = lax.all_to_all(outgoing, ("x", "zhi"), split_axis=0, concat_axis=0, tiled=True)
     swap = [(0, 1), (1, 0)]
 
@@ -219,9 +221,15 @@
     theirs = lax.ppermute(theirs, "core", swap)
     computed = (experts_on(arrived) + theirs.astype(jnp.float32)).astype(jnp.bfloat16)
     returned = lax.all_to_all(computed, ("x", "zhi"), split_axis=0, concat_axis=0, tiled=True)
-    summed = returned.astype(jnp.float32).reshape(EXPERTS * MOST, width)
-    picked = summed[slot_index] * expert_weights.reshape(-1).astype(jnp.float32)[:, None]
-    mixture = in_chunk_order(jnp.sum(picked.reshape(rows_here, TOPK, width), axis=1), chunk_order)
+    mixing = (
+        jnp.zeros((rows_here, EXPERTS * MOST), jnp.bfloat16)
+        .at[token_of, slot_index]
+        .set(expert_weights.reshape(-1))
+    )
+    mixture = jnp.dot(
+        mixing, returned.reshape(EXPERTS * MOST, width), preferred_element_type=jnp.float32
+    )
+    mixture = in_chunk_order(mixture, chunk_order)
     layer_out = (attended.astype(jnp.float32) + residual_scale * mixture).astype(jnp.bfloat16)
     return (attended, layer_out)
 

time: 535 us -> 517 us (0.966)
  waiting for transfers between devices: 335 us -> 315 us
  starting transfers between devices: 37.1 us -> 48.4 us
  local copies, waits for them, and re-layouts: 51.7 us -> 40.9 us
    gather x3 -> x0, local copies, waits for them, and re-layouts: 21.2 us -> none  [the longest x2 10.6 us: shards(): outgoing = moe_in[slot_token.reshape(blocks, block_experts, MOST)]]
    all_to_all x1, waiting for transfers between devices: 53.2 us -> 41.4 us  [shards(): lax.all_to_all(outgoing, ('x', 'zhi'), split_axis=0, concat_axis=0, tiled...]
    ppermute x14, starting transfers between devices: 26.2 us -> 37.7 us  [permute_piece(): return lax.ppermute(local, ('req', 'zlo'), perm)]
    all_to_all x1, waiting for transfers between devices: 56.6 us -> 48.7 us  [shards(): lax.all_to_all(computed, ('x', 'zhi'), split_axis=0, concat_axis=0, tiled...]
    unnamed x23 -> x29, local copies, waits for them, and re-layouts: 1.83 us -> 9.64 us
    dot_general x0 -> x2, matrix products: none -> 5.4 us  [the longest x1 2.72 us: shards(): jnp.dot(mixing, returned.reshape(EXPERTS * MOST, width), preferred_elemen...]
    reshape x2 -> x3, local copies, waits for them, and re-layouts: 6.3 us -> 11.3 us  [the longest x1 5.71 us: shards(): returned.reshape(EXPERTS * MOST, width)]
  transfers between devices with their start and end apart: 19 -> 19, of which waited for: 10 -> 10; matrix products, arithmetic and copies ran while one was open for 5% -> 7% of each run, Pallas kernels for 0% -> 0%
where the time goes in v11:
time: 517 us; the launch traced here: 508 us
  waiting for transfers between devices  315 us (61%)
  starting transfers between devices  48.4 us (9%)
  local copies, waits for them, and re-layouts  40.9 us (8%)
  Pallas kernels  39.8 us (8%)
  matrix products  37 us (7%)
  between operations  15.4 us (3%)
  other arithmetic  11.4 us (2%)
    ppermute x14, waiting for transfers between devices, permute_piece(): return lax.ppermute(local, ('req', 'zlo'), perm)  174 us
    all_gather x1, waiting for transfers between devices, shards(): piece = lax.all_gather(joined, EXP_AXES, axis=0, tiled=True)  50.9 us
    all_to_all x1, waiting for transfers between devices, shards(): lax.all_to_all(computed, ('x', 'zhi'), split_axis=0, concat_axis=0, tiled...  48.7 us
    all_to_all x1, waiting for transfers between devices, shards(): lax.all_to_all(outgoing, ('x', 'zhi'), split_axis=0, concat_axis=0, tiled...  41.4 us
    pallas_call x1, Pallas kernels, attend(): pl.pallas_call(kernel, grid_spec=grid_spec, out_shape=jax.ShapeDtypeStruc...  39.8 us
    ppermute x14, starting transfers between devices, permute_piece(): return lax.ppermute(local, ('req', 'zlo'), perm)  37.7 us
    dot_general x2, matrix products, experts_on(): jnp.einsum('skmd,pkdf->spkmf', rows_in, gate_up_full, preferred_element_t...  11.5 us
  transfers between devices with their start and end apart: 19, of which 10 were waited for; matrix products, arithmetic and copies ran while one was open for 7% of the time, Pallas kernels for 0%

profile of v11, /device:TPU:0, one launch (start us, length us, event | category | flops | bytes accessed | tf_op | source)
XLA Modules:
  0.0 507.9 jit_solution(12262416631287445237)
XLA Ops:
  8.1 1.2 fusion.26
  9.2 0.7 convert_element_type.77
  9.9 1.4 convolution_convert_fusion.1
  11.4 2.3 fusion.59
  13.7 0.1 multiply_cosine_fusion
  13.9 0.1 copy.61
  14.0 0.8 maximum_maximum_fusion
  15.4 4.3 fusion.61
  19.7 0.1 subtract_convert_fusion
  19.9 0.9 copy.62.q_ref
  20.8 0.6 fusion.25
  21.4 4.7 scatter_custom_fusion
  26.1 0.7 compare_select_fusion.1.lim_ref
  26.8 50.9 %all-gather.2.cloned.1.call-done.k_ref.v_ref = bf16[5632,1024]{1,0:T(8,128)(2,1)} async-done(((bf16[176,1024]{1,0:T(8,128)(2,1)}), bf16[5632,1024]{1,0:T(8,128)(2,1)}) %all-gather.2.cloned.1.call-update) | async-done | bytes 11534352 | tf_op jit(solution)/shard_map/all_gather | solution.py:170
  77.7 39.8 %shard_map.140 = bf16[128,1536]{1,0:T(8,128)(2,1)} custom-call(s32[1]{0:T(128)} %bitcast.bounds_ref, s32[1,5632]{1,0:T(1,128)} %compare_select_fusion.1.lim_ref, bf16[128,1536]{1,0:T(8,128)(2,1)} %copy.62.q_ref, bf16[5632,1024]{1,0:T(8,128)(2,1)} %all-gather.2.cloned.1.call-done.k_ref.v_ref, bf16[5632,1024]{1,0:T(8,128)(2,1)} %all-gather.2.cloned.1.call-done.k_ref.v_ref), custom_call_target="tpu_custom_call" | custom-call | tf_op jit(solution)/shard_map/pallas_call | solution.py:89
  117.5 3.3 fusion.29
  120.9 0.2 fusion.31
  121.1 0.6 gather_fusion
  121.8 2.7 convolution_convert_fusion
  124.5 5.5 %reshape.318 = bf16[8,5,26,1536]{3,2,1,0:T(8,128)(2,1)} reshape(bf16[1040,1536]{1,0:T(8,128)(2,1)} %convolution_convert_fusion) | data formatting | bytes 6389760 | tf_op jit(solution)/shard_map/reshape | solution.py:209
  130.0 5.2 %all-to-all-start = ((bf16[8,5,26,1536]{3,2,1,0:T(8,128)(2,1)}), bf16[8,5,26,1536]{3,2,1,0:T(8,128)(2,1)}, u32[]{:S(2)}, u32[]{:S(2)}) async-start(bf16[8,5,26,1536]{3,2,1,0:T(8,128)(2,1)} %reshape.318), calls=%async_computation | async-start | bytes 7864320 | tf_op jit(solution)/shard_map/all_to_all | solution.py:210
  135.2 15.0 %collective-permute-start.2 = (bf16[5,128,384]{2,1,0:T(8,128)(2,1)S(1)}, bf16[5,128,384]{2,1,0:T(8,128)(2,1)S(1)}, u32[]{:S(2)}, u32[]{:S(2)}) collective-permute-start(bf16[5,128,384]{2,1,0:T(8,128)(2,1)S(1)} %bitcast.118), channel_id=1, source_target_pairs={{0,96},{2,98},{32,0},{34,2},{64,32},{66,34},{96,64},{98,66},{1,97}... | collective-permute-start | bytes 1474568 | tf_op jit(solution)/shard_map/ppermute | solution.py:106
  150.2 41.4 %all-to-all-done = bf16[8,5,26,1536]{3,2,1,0:T(8,128)(2,1)} async-done(((bf16[8,5,26,1536]{3,2,1,0:T(8,128)(2,1)}), bf16[8,5,26,1536]{3,2,1,0:T(8,128)(2,1)}, u32[]{:S(2)}, u32[]{:S(2)}) %all-to-all-start) | async-done | bytes 3194912 | tf_op jit(solution)/shard_map/all_to_all | solution.py:210
  191.6 3.9 copy.73
  195.6 3.1 collective-permute-start.1
  198.8 1.1 collective-permute-start.9
  199.9 1.5 collective-permute-start.8
  201.4 10.0 %collective-permute-done.1 = bf16[5,128,384]{2,1,0:T(8,128)(2,1)S(1)} collective-permute-done((bf16[5,128,384]{2,1,0:T(8,128)(2,1)S(1)}, bf16[5,128,384]{2,1,0:T(8,128)(2,1)S(1)}, u32[]{:S(2)}, u32[]{:S(2)}) %collective-permute-start.1) | collective-permute-done | bytes 491552 | tf_op jit(solution)/shard_map/ppermute | solution.py:106
  211.4 1.5 collective-permute-start
  212.9 50.6 %collective-permute-done = bf16[5,128,384]{2,1,0:T(8,128)(2,1)S(1)} collective-permute-done((bf16[5,128,384]{2,1,0:T(8,128)(2,1)S(1)}, bf16[5,128,384]{2,1,0:T(8,128)(2,1)S(1)}, u32[]{:S(2)}, u32[]{:S(2)}) %collective-permute-start) | collective-permute-done | bytes 491552 | tf_op jit(solution)/shard_map/ppermute | solution.py:106
  263.4 0.8 collective-permute-start.6
  264.3 3.7 collective-permute-start.5
  268.0 1.0 collective-permute-start.4
  269.0 1.3 collective-permute-start.3
  270.3 21.1 %collective-permute-done.6 = bf16[5,128,384]{2,1,0:T(8,128)(2,1)S(1)} collective-permute-done((bf16[5,128,384]{2,1,0:T(8,128)(2,1)S(1)}, bf16[5,128,384]{2,1,0:T(8,128)(2,1)S(1)}, u32[]{:S(2)}, u32[]{:S(2)}) %collective-permute-start.6) | collective-permute-done | bytes 491552 | tf_op jit(solution)/shard_map/ppermute | solution.py:106
  291.4 4.9 collective-permute-start.13
  296.3 3.0 collective-permute-start.12
  299.3 31.6 %collective-permute-done.4 = bf16[5,128,384]{2,1,0:T(8,128)(2,1)S(1)} collective-permute-done((bf16[5,128,384]{2,1,0:T(8,128)(2,1)S(1)}, bf16[5,128,384]{2,1,0:T(8,128)(2,1)S(1)}, u32[]{:S(2)}, u32[]{:S(2)}) %collective-permute-start.4) | collective-permute-done | bytes 491552 | tf_op jit(solution)/shard_map/ppermute | solution.py:106
  330.9 41.4 %collective-permute-done.3 = bf16[5,128,384]{2,1,0:T(8,128)(2,1)S(1)} collective-permute-done((bf16[5,128,384]{2,1,0:T(8,128)(2,1)S(1)}, bf16[5,128,384]{2,1,0:T(8,128)(2,1)S(1)}, u32[]{:S(2)}, u32[]{:S(2)}) %collective-permute-start.3) | collective-permute-done | bytes 491552 | tf_op jit(solution)/shard_map/ppermute | solution.py:106
  372.3 0.8 collective-permute-start.10
  373.1 1.5 maximum_bitcast_fusion.5
  374.5 0.7 maximum_bitcast_fusion.3
  375.3 1.5 maximum_bitcast_fusion.6
  376.7 6.4 %collective-permute-done.11 = bf16[5,384,256]{2,1,0:T(8,128)(2,1)S(1)} collective-permute-done((bf16[5,384,256]{2,1,0:T(8,128)(2,1)S(1)}, bf16[5,384,256]{2,1,0:T(8,128)(2,1)S(1)}, u32[]{:S(2)}, u32[]{:S(2)}) %collective-permute-start.11) | collective-permute-done | bytes 983072 | tf_op jit(solution)/shard_map/ppermute | solution.py:106
  383.2 12.8 %collective-permute-done.10 = bf16[5,384,256]{2,1,0:T(8,128)(2,1)S(1)} collective-permute-done((bf16[5,384,256]{2,1,0:T(8,128)(2,1)S(1)}, bf16[5,384,256]{2,1,0:T(8,128)(2,1)S(1)}, u32[]{:S(2)}, u32[]{:S(2)}) %collective-permute-start.10) | collective-permute-done | bytes 983072 | tf_op jit(solution)/shard_map/ppermute | solution.py:106
  395.9 0.7 maximum_bitcast_fusion.4
  396.7 1.7 copy-done.12
  398.3 5.6 %fusion.18 = f32[8,2,5,26,256]{4,3,0,1,2:T(8,128)} fusion(bf16[8,5,26,1536,1]{3,0,2,1,4:T(8,128)(2,1)} %bitcast.129, bf16[1,5,1536,256]{3,2,0,1:T(8,128)(2,1)S(1)} %maximum_bitcast_fusion.4, bf16[1,5,1536,256]{3,2,0,1:T(8,128)(2,1)S(1)} %maximum_bitcast_fusion.3), kind=kOutput, calls=%fused_computation.29 | convolution fusion | flops 1651507200 | bytes 13189120 | tf_op jit(solution)/shard_map/skmd,pkdf->spkmf/dot_general | solution.py:214
  404.0 4.1 fusion.8
  408.1 3.5 copy.76
  411.6 5.9 %fusion.15 = f32[8,2,5,26,256]{4,3,0,1,2:T(8,128)} fusion(bf16[1,5,1536,256]{3,2,0,1:T(8,128)(2,1)S(1)} %maximum_bitcast_fusion.4, bf16[1,5,1536,256]{3,2,0,1:T(8,128)(2,1)S(1)} %maximum_bitcast_fusion.3, bf16[8,5,26,1536]{3,2,1,0:T(8,128)(2,1)} %all-to-all-done), kind=kOutput, calls=%fused_computation.28 | convolution fusion | flops 1651507200 | bytes 13189120 | tf_op jit(solution)/shard_map/skmd,pkdf->spkmf/dot_general | solution.py:214
  417.5 2.1 fusion.22
  419.5 4.1 fusion
  423.7 3.0 copy.77
  426.7 5.4 %all-to-all-start.1 = ((bf16[8,5,26,1536]{3,2,1,0:T(8,128)(2,1)}), bf16[8,5,26,1536]{3,2,1,0:T(8,128)(2,1)}, u32[]{:S(2)}, u32[]{:S(2)}) async-start(bf16[8,5,26,1536]{3,2,1,0:T(8,128)(2,1)} %copy.77), calls=%async_computation.1 | async-start | bytes 7864320 | tf_op jit(solution)/shard_map/all_to_all | solution.py:223
  432.1 0.1 copy.65
  432.2 0.1 reshape.350
  432.5 7.7 %scatter_custom_fusion.1 = bf16[133120]{0:T(1024)(128)(2,1)S(1)} fusion(s32[1024]{0:T(1024)S(1)} %broadcast_select_fusion, bf16[1024]{0:T(1024)(128)(2,1)S(1)} %reshape.350, bf16[]{:T(256)} %constant.123.clone.1), kind=kCustom, calls=%fused_computation.65 | custom fusion | bytes 266242
  440.2 48.7 %all-to-all-done.1 = bf16[8,5,26,1536]{3,2,1,0:T(8,128)(2,1)} async-done(((bf16[8,5,26,1536]{3,2,1,0:T(8,128)(2,1)}), bf16[8,5,26,1536]{3,2,1,0:T(8,128)(2,1)}, u32[]{:S(2)}, u32[]{:S(2)}) %all-to-all-start.1) | async-done | bytes 3194912 | tf_op jit(solution)/shard_map/all_to_all | solution.py:223
  488.9 5.7 %reshape.319 = bf16[1040,1536]{1,0:T(8,128)(2,1)} reshape(bf16[8,5,26,1536]{3,2,1,0:T(8,128)(2,1)} %all-to-all-done.1) | data formatting | bytes 6389760 | tf_op jit(solution)/shard_map/reshape | solution.py:230
  494.6 2.7 fusion.11
  497.3 1.5 gather_fusion.1
  498.8 1.2 copy.98
  500.0 0.8 fusion.32
  (65 shorter events, 1.2 us)
Async XLA Ops:
  7.2 2.8 copy-start
  7.2 8.2 %copy-start.2 = (bf16[128,1536]{1,0:T(8,128)(2,1)S(1)}, bf16[128,1536]{1,0:T(8,128)(2,1)}, u32[]{:S(2)}) copy-start(bf16[128,1536]{1,0:T(8,128)(2,1)} %param.13) | copy-start | bytes 1179652
  7.2 6.8 %copy-start.6 = (bf16[1,48,1024]{2,1,0:T(8,128)(2,1)S(1)}, bf16[1,48,1024]{2,1,0:T(8,128)(2,1)}, u32[]{:S(2)}) copy-start(bf16[1,48,1024]{2,1,0:T(8,128)(2,1)} %param.19) | copy-start | bytes 294916
  7.2 7.7 %copy-start.8 = (bf16[1536]{0:T(1024)(128)(2,1)S(1)}, bf16[1536]{0:T(1024)(128)(2,1)}, u32[]{:S(2)}) copy-start(bf16[1536]{0:T(1024)(128)(2,1)} %param.21) | copy-start | bytes 9220
  7.2 7.7 %copy-start.7 = (s32[128,8]{0,1:T(8,128)S(1)}, s32[128,8]{0,1:T(8,128)}, u32[]{:S(2)}) copy-start(s32[128,8]{0,1:T(8,128)} %param.22) | copy-start | bytes 12292
  7.2 70.5 %all-gather.2.cloned.1.call-start = ((), (), s32[]{:S(2)}) async-start(), calls=%async_computation.2 | async-start | bytes 11894784 | tf_op jit(solution)/shard_map/all_gather | solution.py:170
  120.9 379.1 %copy-start.3 = (bf16[128,1536]{1,0:T(8,128)(2,1)}, bf16[128,1536]{1,0:T(8,128)(2,1)S(1)}, u32[]{:S(2)}) copy-start(bf16[128,1536]{1,0:T(8,128)(2,1)S(1)} %get-tuple-element.15) | copy-start | bytes 1179652
  130.0 5.2 %copy-start.5 = (bf16[1,5,128,384]{3,2,1,0:T(8,128)(2,1)S(1)}, bf16[1,5,128,384]{3,2,1,0:T(8,128)(2,1)}, u32[]{:S(2)}) copy-start(bf16[1,5,128,384]{3,2,1,0:T(8,128)(2,1)} %param.25) | copy-start | bytes 1474564
  130.0 61.7 %all-to-all-start = ((bf16[8,5,26,1536]{3,2,1,0:T(8,128)(2,1)}), bf16[8,5,26,1536]{3,2,1,0:T(8,128)(2,1)}, u32[]{:S(2)}, u32[]{:S(2)}) async-start(bf16[8,5,26,1536]{3,2,1,0:T(8,128)(2,1)} %reshape.318), calls=%async_computation | async-start | bytes 7864320 | tf_op jit(solution)/shard_map/all_to_all | solution.py:210
  135.2 63.6 %copy-start.4 = (bf16[1,5,384,256]{3,2,1,0:T(8,128)(2,1)S(1)}, bf16[1,5,384,256]{3,2,1,0:T(8,128)(2,1)}, u32[]{:S(2)}) copy-start(bf16[1,5,384,256]{3,2,1,0:T(8,128)(2,1)} %param.24) | copy-start | bytes 2949124
  135.2 66.2 %collective-permute-start.2 = (bf16[5,128,384]{2,1,0:T(8,128)(2,1)S(1)}, bf16[5,128,384]{2,1,0:T(8,128)(2,1)S(1)}, u32[]{:S(2)}, u32[]{:S(2)}) collective-permute-start(bf16[5,128,384]{2,1,0:T(8,128)(2,1)S(1)} %bitcast.118), channel_id=1, source_target_pairs={{0,96},{2,98},{32,0},{34,2},{64,32},{66,34},{96,64},{98,66},{1,97}... | collective-permute-start | bytes 1474568 | tf_op jit(solution)/shard_map/ppermute | solution.py:106
  195.5 201.1 %collective-permute-start.14 = (bf16[8,5,26,1536]{3,0,2,1:T(8,128)(2,1)S(1)}, bf16[8,5,26,1536]{3,0,2,1:T(8,128)(2,1)S(1)}, u32[]{:S(2)}, u32[]{:S(2)}) collective-permute-start(bf16[8,5,26,1536]{3,0,2,1:T(8,128)(2,1)S(1)} %copy.73), channel_id=1, source_target_pairs={{0,1},{1,0},{2,3},{3,2},{4,5},{5,4},{6,7},{7,6},{8,9},{9,8},{10,11... | collective-permute-start | bytes 9584648 | tf_op jit(solution)/shard_map/ppermute | solution.py:220
  195.6 15.8 %collective-permute-start.1 = (bf16[5,128,384]{2,1,0:T(8,128)(2,1)S(1)}, bf16[5,128,384]{2,1,0:T(8,128)(2,1)S(1)}, u32[]{:S(2)}, u32[]{:S(2)}) collective-permute-start(bf16[5,128,384]{2,1,0:T(8,128)(2,1)S(1)} %bitcast.119), channel_id=1, source_target_pairs={{0,64},{2,66},{32,96},{34,98},{64,0},{66,2},{96,32},{98,34},{1,65}... | collective-permute-start | bytes 1474568 | tf_op jit(solution)/shard_map/ppermute | solution.py:106
  198.8 65.5 %collective-permute-start.9 = (bf16[5,384,256]{2,1,0:T(8,128)(2,1)S(1)}, bf16[5,384,256]{2,1,0:T(8,128)(2,1)S(1)}, u32[]{:S(2)}, u32[]{:S(2)}) collective-permute-start(bf16[5,384,256]{2,1,0:T(8,128)(2,1)S(1)} %bitcast.109), channel_id=1, source_target_pairs={{0,96},{2,98},{32,0},{34,2},{64,32},{66,34},{96,64},{98,66},{1,97}... | collective-permute-start | bytes 2949128 | tf_op jit(solution)/shard_map/ppermute | solution.py:106
  199.9 68.1 %collective-permute-start.8 = (bf16[5,384,256]{2,1,0:T(8,128)(2,1)S(1)}, bf16[5,384,256]{2,1,0:T(8,128)(2,1)S(1)}, u32[]{:S(2)}, u32[]{:S(2)}) collective-permute-start(bf16[5,384,256]{2,1,0:T(8,128)(2,1)S(1)} %bitcast.110), channel_id=1, source_target_pairs={{0,64},{2,66},{32,96},{34,98},{64,0},{66,2},{96,32},{98,34},{1,65}... | collective-permute-start | bytes 2949128 | tf_op jit(solution)/shard_map/ppermute | solution.py:106
  201.4 67.6 %collective-permute-start.7 = (bf16[5,384,256]{2,1,0:T(8,128)(2,1)S(1)}, bf16[5,384,256]{2,1,0:T(8,128)(2,1)S(1)}, u32[]{:S(2)}, u32[]{:S(2)}) collective-permute-start(bf16[5,384,256]{2,1,0:T(8,128)(2,1)S(1)} %bitcast.111), channel_id=1, source_target_pairs={{0,32},{2,34},{32,64},{34,66},{64,96},{66,98},{96,0},{98,2},{1,33}... | collective-permute-start | bytes 2949128 | tf_op jit(solution)/shard_map/ppermute | solution.py:106
  211.4 52.0 %collective-permute-start = (bf16[5,128,384]{2,1,0:T(8,128)(2,1)S(1)}, bf16[5,128,384]{2,1,0:T(8,128)(2,1)S(1)}, u32[]{:S(2)}, u32[]{:S(2)}) collective-permute-start(bf16[5,128,384]{2,1,0:T(8,128)(2,1)S(1)} %bitcast.120), channel_id=1, source_target_pairs={{0,32},{2,34},{32,64},{34,66},{64,96},{66,98},{96,0},{98,2},{1,33}... | collective-permute-start | bytes 1474568 | tf_op jit(solution)/shard_map/ppermute | solution.py:106
  263.4 28.0 %collective-permute-start.6 = (bf16[5,128,384]{2,1,0:T(8,128)(2,1)S(1)}, bf16[5,128,384]{2,1,0:T(8,128)(2,1)S(1)}, u32[]{:S(2)}, u32[]{:S(2)}) collective-permute-start(bf16[5,128,384]{2,1,0:T(8,128)(2,1)S(1)} %bitcast.121), channel_id=1, source_target_pairs={{0,98},{2,96},{32,2},{34,0},{64,34},{66,32},{96,66},{98,64},{1,99}... | collective-permute-start | bytes 1474568 | tf_op jit(solution)/shard_map/ppermute | solution.py:106
  264.3 32.0 %collective-permute-start.5 = (bf16[5,128,384]{2,1,0:T(8,128)(2,1)S(1)}, bf16[5,128,384]{2,1,0:T(8,128)(2,1)S(1)}, u32[]{:S(2)}, u32[]{:S(2)}) collective-permute-start(bf16[5,128,384]{2,1,0:T(8,128)(2,1)S(1)} %bitcast.122), channel_id=1, source_target_pairs={{0,66},{2,64},{32,98},{34,96},{64,2},{66,0},{96,34},{98,32},{1,67}... | collective-permute-start | bytes 1474568 | tf_op jit(solution)/shard_map/ppermute | solution.py:106
  268.0 62.9 %collective-permute-start.4 = (bf16[5,128,384]{2,1,0:T(8,128)(2,1)S(1)}, bf16[5,128,384]{2,1,0:T(8,128)(2,1)S(1)}, u32[]{:S(2)}, u32[]{:S(2)}) collective-permute-start(bf16[5,128,384]{2,1,0:T(8,128)(2,1)S(1)} %bitcast.123), channel_id=1, source_target_pairs={{0,34},{2,32},{32,66},{34,64},{64,98},{66,96},{96,2},{98,0},{1,35}... | collective-permute-start | bytes 1474568 | tf_op jit(solution)/shard_map/ppermute | solution.py:106
  269.0 103.3 %collective-permute-start.3 = (bf16[5,128,384]{2,1,0:T(8,128)(2,1)S(1)}, bf16[5,128,384]{2,1,0:T(8,128)(2,1)S(1)}, u32[]{:S(2)}, u32[]{:S(2)}) collective-permute-start(bf16[5,128,384]{2,1,0:T(8,128)(2,1)S(1)} %bitcast.124), channel_id=1, source_target_pairs={{0,2},{2,0},{32,34},{34,32},{64,66},{66,64},{96,98},{98,96},{1,3},... | collective-permute-start | bytes 1474568 | tf_op jit(solution)/shard_map/ppermute | solution.py:106
  291.4 85.3 %collective-permute-start.13 = (bf16[5,384,256]{2,1,0:T(8,128)(2,1)S(1)}, bf16[5,384,256]{2,1,0:T(8,128)(2,1)S(1)}, u32[]{:S(2)}, u32[]{:S(2)}) collective-permute-start(bf16[5,384,256]{2,1,0:T(8,128)(2,1)S(1)} %bitcast.112), channel_id=1, source_target_pairs={{0,98},{2,96},{32,2},{34,0},{64,34},{66,32},{96,66},{98,64},{1,99}... | collective-permute-start | bytes 2949128 | tf_op jit(solution)/shard_map/ppermute | solution.py:106
  296.3 80.4 %collective-permute-start.12 = (bf16[5,384,256]{2,1,0:T(8,128)(2,1)S(1)}, bf16[5,384,256]{2,1,0:T(8,128)(2,1)S(1)}, u32[]{:S(2)}, u32[]{:S(2)}) collective-permute-start(bf16[5,384,256]{2,1,0:T(8,128)(2,1)S(1)} %bitcast.113), channel_id=1, source_target_pairs={{0,66},{2,64},{32,98},{34,96},{64,2},{66,0},{96,34},{98,32},{1,67}... | collective-permute-start | bytes 2949128 | tf_op jit(solution)/shard_map/ppermute | solution.py:106
  330.9 52.3 %collective-permute-start.11 = (bf16[5,384,256]{2,1,0:T(8,128)(2,1)S(1)}, bf16[5,384,256]{2,1,0:T(8,128)(2,1)S(1)}, u32[]{:S(2)}, u32[]{:S(2)}) collective-permute-start(bf16[5,384,256]{2,1,0:T(8,128)(2,1)S(1)} %bitcast.114), channel_id=1, source_target_pairs={{0,34},{2,32},{32,66},{34,64},{64,98},{66,96},{96,2},{98,0},{1,35}... | collective-permute-start | bytes 2949128 | tf_op jit(solution)/shard_map/ppermute | solution.py:106
  372.3 23.7 %collective-permute-start.10 = (bf16[5,384,256]{2,1,0:T(8,128)(2,1)S(1)}, bf16[5,384,256]{2,1,0:T(8,128)(2,1)S(1)}, u32[]{:S(2)}, u32[]{:S(2)}) collective-permute-start(bf16[5,384,256]{2,1,0:T(8,128)(2,1)S(1)} %bitcast.115), channel_id=1, source_target_pairs={{0,2},{2,0},{32,34},{34,32},{64,66},{66,64},{96,98},{98,96},{1,3},... | collective-permute-start | bytes 2949128 | tf_op jit(solution)/shard_map/ppermute | solution.py:106
  396.7 1.7 copy-start.12
  411.6 7.9 %collective-permute-start.15 = (bf16[8,5,26,1536]{3,0,2,1:T(8,128)(2,1)}, bf16[8,5,26,1536]{3,0,2,1:T(8,128)(2,1)}, u32[]{:S(2)}, u32[]{:S(2)}) collective-permute-start(bf16[8,5,26,1536]{3,0,2,1:T(8,128)(2,1)} %copy.76), channel_id=1, source_target_pairs={{0,1},{1,0},{2,3},{3,2},{4,5},{5,4},{6,7},{7,6},{8,9},{9,8},{10,11... | collective-permute-start | bytes 9584648 | tf_op jit(solution)/shard_map/ppermute | solution.py:221
  426.7 5.4 %copy-start.9 = (bf16[128,8]{0,1:T(8,128)(2,1)S(1)}, bf16[128,8]{0,1:T(8,128)(2,1)}, u32[]{:S(2)}) copy-start(bf16[128,8]{0,1:T(8,128)(2,1)} %param.23) | copy-start | bytes 6148
  426.7 5.6 %copy-start.11 = (s32[2]{0:T(128)S(1)}, s32[2]{0:T(128)}, u32[]{:S(2)}) copy-start(s32[2]{0:T(128)} %constant.134) | copy-start | bytes 28
  426.7 5.7 %copy-start.10 = (s32[2]{0:T(128)S(1)}, s32[2]{0:T(128)}, u32[]{:S(2)}) copy-start(s32[2]{0:T(128)} %constant.137) | copy-start | bytes 28
  426.7 62.2 %all-to-all-start.1 = ((bf16[8,5,26,1536]{3,2,1,0:T(8,128)(2,1)}), bf16[8,5,26,1536]{3,2,1,0:T(8,128)(2,1)}, u32[]{:S(2)}, u32[]{:S(2)}) async-start(bf16[8,5,26,1536]{3,2,1,0:T(8,128)(2,1)} %copy.77), calls=%async_computation.1 | async-start | bytes 7864320 | tf_op jit(solution)/shard_map/all_to_all | solution.py:223
  494.6 6.3 %copy-start.1 = (bf16[1536,512]{1,0:T(8,128)(2,1)S(1)}, bf16[1536,512]{1,0:T(8,128)(2,1)}, u32[]{:S(2)}) copy-start(bf16[1536,512]{1,0:T(8,128)(2,1)} %param.17) | copy-start | bytes 4718596
Sparse Core Ops, SparseCore 0:
  15.0 62.7 all-gather.1
